TPU v7x, 512 devices: a whole 4x8x8 slice. The times are simulated.
512 devices in a mesh: gx: 8 (over x, core), yz: 64 (over y, z).
Axes of the slice: x: 4, y: 8, z: 8, core: 2. Of those that a mesh axis runs over, the one named last changes fastest.
Arguments:
- old_coeff: bfloat16 [131072, 512], P(('gx', 'yz')), may hold values from -6 to 6
- basis_old: bfloat16 [8, 64, 64], replicated, may hold values from -0.75 to 0.75
- basis_new: bfloat16 [8, 64, 64], replicated, may hold values from -0.75 to 0.75
- quad_weight: float32 [8, 64], replicated, may hold values from 0.3 to 3
- tet_zone: int32 [1048576], P(('gx', 'yz')), may hold values from 0 to 255
- tet_table: int32 [1048576], P(('gx', 'yz')), may hold values from 0 to 7
- tet_volume: float32 [1048576], P(('gx', 'yz')), may hold values from 0.1 to 1
- tet_dest: int32 [1048576], P(('gx', 'yz')), may hold values from 0 to 415, as said below
- recv_list: int32 [512, 160], P(('gx', 'yz')), may hold values from 0 to 255
- inv_mass: bfloat16 [131072, 4096], P(('gx', 'yz')), may hold values from -0.75 to 0.75
Outputs:
- new_coeff: float32 [131072, 512], P(('gx', 'yz'))
Inputs may be any that keep to these rules, and one draw needn't show every extreme that they name: `tet_dest`: A value below 256 names an own new zone; 256 + k * 16 + s names slot s of partner k.
All inputs are finite; a program needn't handle non-finite values.
Results may differ from a plain program's by a relative error of at most 0.0042.
Values may be sent and summed in bfloat16 or wider, within the bound.
No kernel may reach another device: no remote copies, remote signals or barrier semaphores. Data moves between devices by JAX's collectives and lax.ppermute only.
A program may use at most 64 MiB of HBM per device.

v0:
```python
import jax
import jax.numpy as jnp
from jax import lax
from jax.sharding import PartitionSpec as P


def extended_2(block, sides, width):
    for axis, dim in sides:
        count = lax.axis_size(axis)
        forward = [(i, i + 1) for i in range(count - 1)]
        forward.append((count - 1, 0))
        backward = [(target, source) for source, target in forward]
        low = lax.ppermute(
            lax.slice_in_dim(block, block.shape[dim] - width, None, axis=dim), axis, forward
        )
        high = lax.ppermute(lax.slice_in_dim(block, 0, width, axis=dim), axis, backward)
        block = jnp.concatenate([low, block, high], axis=dim)
    return block


def passed_along(block, axis, distance):
    devices = range(lax.axis_size(axis))
    route = [((i - distance) % len(devices), i) for i in devices]
    return lax.ppermute(block, axis, route)


def on_device(
    old_coeff,
    basis_old,
    basis_new,
    quad_weight,
    tet_zone,
    tet_table,
    tet_volume,
    tet_dest,
    recv_list,
    inv_mass,
):
    zone_count = old_coeff.shape[0]
    row_width = old_coeff.shape[1]
    tables = basis_old.shape[0]
    basis_size = basis_old.shape[2]
    field_count = row_width // basis_size
    tet_count = tet_zone.shape[0]
    slot_total = recv_list.shape[1]
    partner_count = 10
    slot_cap = slot_total // partner_count
    row_count = zone_count + slot_total
    block_rows = min(512, tet_count)
    block_count = tet_count // block_rows

    def quad_block(partial_value, pieces):
        zone_blk, table_blk, volume_blk, dest_blk = pieces
        picked = jnp.take(old_coeff, zone_blk, axis=0).reshape(block_rows, basis_size, field_count)
        values = jnp.einsum("tqi,bif->btqf", basis_old, picked, preferred_element_type=jnp.float32)
        selector = (table_blk[:, None] == jnp.arange(tables, dtype=jnp.int32)[None, :]).astype(
            jnp.float32
        )
        scaling = selector[:, :, None] * quad_weight[None, :, :] * volume_blk[:, None, None]
        weighted = jnp.sum(scaling[:, :, :, None] * values, axis=1).astype(jnp.bfloat16)
        spread = selector.astype(jnp.bfloat16)[:, :, None, None] * weighted[:, None, :, :]
        moment = jnp.einsum("btqf,tqj->bjf", spread, basis_new, preferred_element_type=jnp.float32)
        partial_value = partial_value + jax.ops.segment_sum(
            moment.reshape(block_rows, row_width), dest_blk, num_segments=row_count
        )
        return (partial_value, None)

    pieces = (
        tet_zone.reshape(block_count, block_rows),
        tet_table.reshape(block_count, block_rows),
        tet_volume.reshape(block_count, block_rows),
        tet_dest.reshape(block_count, block_rows),
    )
    partial_value, _ = lax.scan(quad_block, jnp.zeros((row_count, row_width), jnp.float32), pieces)
    own_part = partial_value[:zone_count]
    outgoing = (
        partial_value[zone_count:].astype(jnp.bfloat16).reshape(partner_count, slot_cap, row_width)
    )
    lane_count = lax.axis_size("yz")
    face_side = 1 << (lane_count.bit_length() - 1) // 2
    going_down = jnp.stack([outgoing[1], outgoing[5], outgoing[6]], axis=0)
    going_up = jnp.stack([outgoing[0], outgoing[4], outgoing[7]], axis=0)
    stepped = extended_2(jnp.stack([going_down, going_up], axis=0), (("yz", 0),), 1)
    from_left = stepped[0]
    from_right = stepped[3]
    upward = jnp.stack([outgoing[2], from_left[1], from_right[2]], axis=0)
    downward = jnp.stack([outgoing[3], from_left[2], from_right[1]], axis=0)
    came_up = passed_along(upward, "yz", face_side)
    came_down = passed_along(downward, "yz", lane_count - face_side)
    face_rows = jnp.stack(
        [
            from_left[0],
            from_right[0],
            came_up[0],
            came_down[0],
            came_up[1],
            came_down[2],
            came_up[2],
            came_down[1],
        ],
        axis=0,
    )
    sweep_rows = jnp.stack([outgoing[9], outgoing[8]], axis=0)
    extended = extended_2(sweep_rows, (("gx", 0),), 1)
    received = jnp.concatenate([face_rows, extended[0:1], extended[3:4]], axis=0).reshape(
        slot_total, row_width
    )
    gathered = own_part + jax.ops.segment_sum(
        received.astype(jnp.float32), recv_list[0], num_segments=zone_count
    )
    rounded = gathered.astype(jnp.bfloat16).reshape(zone_count, basis_size, field_count)
    inverse = inv_mass.reshape(zone_count, basis_size, basis_size)
    result = jnp.einsum("zjk,zkf->zjf", inverse, rounded, preferred_element_type=jnp.float32)
    return result.reshape(zone_count, row_width)


def solution(mesh):
    placed = (
        P(("gx", "yz"), None),
        P(),
        P(),
        P(),
        P(("gx", "yz")),
        P(("gx", "yz")),
        P(("gx", "yz")),
        P(("gx", "yz")),
        P(("gx", "yz"), None),
        P(("gx", "yz"), None),
    )
    return jax.shard_map(
        on_device, mesh=mesh, in_specs=placed, out_specs=P(("gx", "yz"), None), check_vma=False
    )
```

profile of v0, /device:TPU:56, one launch (start us, length us, event | category | flops | bytes accessed | tf_op | source)
XLA Modules:
  0.0 96.2 jit_solution(17290052055296826778)
XLA Ops:
  2.8 1.0 %copy.29 = bf16[8,64,64]{1,2,0:T(8,128)(2,1)S(1)} copy(bf16[8,64,64]{2,1,0:T(8,128)(2,1)} %param.14) | data formatting | bytes 131072 | tf_op jit(solution)/shard_map/while | solution.py:74
  4.0 42.6 %while.10 = (s32[]{:T(128)}, f32[416,512]{1,0:T(8,128)S(1)}, s32[4,512]{1,0:T(4,128)S(1)}, s32[4,512]{1,0:T(4,128)S(1)}, f32[8,64]{1,0:T(8,128)}, /*index=5*/f32...) while((s32[]{:T(128)}, f32[416,512]{1,0:T(8,128)S(1)}, ...), condition=%wide.region_3.4_spmd, body=%wide.region_0.3_spmd.sunk | while | flops 550258176 | bytes 15692985 | solution.py:74
  4.1 3.0 %gather_fusion = bf16[512,512]{1,0:T(8,128)(2,1)S(1)} fusion(bf16[256,512]{1,0:T(8,128)(2,1)} %get-tuple-element.230, s32[1024]{0:T(1024)S(1)} %pad_clamp_fusion.2), kind=kCustom, calls=%fused_computation.clone.1 | custom fusion | bytes 1050624 | tf_op jit(solution)/shard_map/while/body/eval_jaxpr/jit(_take)/gather | solution.py:54
  7.5 1.3 %multiply_reduce_fusion.2 = bf16[512,8,64]{0,2,1:T(8,128)(2,1)S(1)} fusion(f32[512,8,64]{0,2,1:T(8,128)S(1)} %multiply_multiply_fusion.2, bf16[512,64,8,1]{0,2,1,3:T(8,128)(2,1)S(1)} %fusion.29, bf16[8,64,64]{2,1,0:T(8,128)(2,1)S(1)} %copy-done.1), kind=kOutput, calls=%fused_computation.3.clone.1 | convolution fusion | flops 272367616 | bytes 2162688 | tf_op jit(solution)/shard_map/while/body/eval_jaxpr/tqi,bif->btqf/dot_general | solution.py:55
  8.8 0.9 fusion.30
  10.7 3.9 %scatter_fusion = f32[416,512]{1,0:T(8,128)S(1)} fusion(f32[416,512]{1,0:T(8,128)S(1)} %get-tuple-element.213, s32[512]{0:T(512)S(1)} %bitcast.110, f32[512,512]{1,0:T(8,128)S(1)} %copy.51), kind=kCustom, calls=%fused_computation.1.clone.1 | custom fusion | flops 262144 | bytes 3147776 | tf_op jit(solution)/shard_map/while/body/eval_jaxpr/scatter-add | solution.py:63
  14.7 3.0 %gather_fusion = bf16[512,512]{1,0:T(8,128)(2,1)S(1)} fusion(bf16[256,512]{1,0:T(8,128)(2,1)} %get-tuple-element.230, s32[1024]{0:T(1024)S(1)} %pad_clamp_fusion.2), kind=kCustom, calls=%fused_computation.clone.1 | custom fusion | bytes 1050624 | tf_op jit(solution)/shard_map/while/body/eval_jaxpr/jit(_take)/gather | solution.py:54
  18.2 1.3 %multiply_reduce_fusion.2 = bf16[512,8,64]{0,2,1:T(8,128)(2,1)S(1)} fusion(f32[512,8,64]{0,2,1:T(8,128)S(1)} %multiply_multiply_fusion.2, bf16[512,64,8,1]{0,2,1,3:T(8,128)(2,1)S(1)} %fusion.29, bf16[8,64,64]{2,1,0:T(8,128)(2,1)S(1)} %copy-done.1), kind=kOutput, calls=%fused_computation.3.clone.1 | convolution fusion | flops 272367616 | bytes 2162688 | tf_op jit(solution)/shard_map/while/body/eval_jaxpr/tqi,bif->btqf/dot_general | solution.py:55
  19.5 0.9 fusion.30
  21.3 3.9 %scatter_fusion = f32[416,512]{1,0:T(8,128)S(1)} fusion(f32[416,512]{1,0:T(8,128)S(1)} %get-tuple-element.213, s32[512]{0:T(512)S(1)} %bitcast.110, f32[512,512]{1,0:T(8,128)S(1)} %copy.51), kind=kCustom, calls=%fused_computation.1.clone.1 | custom fusion | flops 262144 | bytes 3147776 | tf_op jit(solution)/shard_map/while/body/eval_jaxpr/scatter-add | solution.py:63
  25.4 3.0 %gather_fusion = bf16[512,512]{1,0:T(8,128)(2,1)S(1)} fusion(bf16[256,512]{1,0:T(8,128)(2,1)} %get-tuple-element.230, s32[1024]{0:T(1024)S(1)} %pad_clamp_fusion.2), kind=kCustom, calls=%fused_computation.clone.1 | custom fusion | bytes 1050624 | tf_op jit(solution)/shard_map/while/body/eval_jaxpr/jit(_take)/gather | solution.py:54
  28.8 1.3 %multiply_reduce_fusion.2 = bf16[512,8,64]{0,2,1:T(8,128)(2,1)S(1)} fusion(f32[512,8,64]{0,2,1:T(8,128)S(1)} %multiply_multiply_fusion.2, bf16[512,64,8,1]{0,2,1,3:T(8,128)(2,1)S(1)} %fusion.29, bf16[8,64,64]{2,1,0:T(8,128)(2,1)S(1)} %copy-done.1), kind=kOutput, calls=%fused_computation.3.clone.1 | convolution fusion | flops 272367616 | bytes 2162688 | tf_op jit(solution)/shard_map/while/body/eval_jaxpr/tqi,bif->btqf/dot_general | solution.py:55
  30.1 0.9 fusion.30
  32.0 3.9 %scatter_fusion = f32[416,512]{1,0:T(8,128)S(1)} fusion(f32[416,512]{1,0:T(8,128)S(1)} %get-tuple-element.213, s32[512]{0:T(512)S(1)} %bitcast.110, f32[512,512]{1,0:T(8,128)S(1)} %copy.51), kind=kCustom, calls=%fused_computation.1.clone.1 | custom fusion | flops 262144 | bytes 3147776 | tf_op jit(solution)/shard_map/while/body/eval_jaxpr/scatter-add | solution.py:63
  36.0 3.0 %gather_fusion = bf16[512,512]{1,0:T(8,128)(2,1)S(1)} fusion(bf16[256,512]{1,0:T(8,128)(2,1)} %get-tuple-element.230, s32[1024]{0:T(1024)S(1)} %pad_clamp_fusion.2), kind=kCustom, calls=%fused_computation.clone.1 | custom fusion | bytes 1050624 | tf_op jit(solution)/shard_map/while/body/eval_jaxpr/jit(_take)/gather | solution.py:54
  39.5 1.3 %multiply_reduce_fusion.2 = bf16[512,8,64]{0,2,1:T(8,128)(2,1)S(1)} fusion(f32[512,8,64]{0,2,1:T(8,128)S(1)} %multiply_multiply_fusion.2, bf16[512,64,8,1]{0,2,1,3:T(8,128)(2,1)S(1)} %fusion.29, bf16[8,64,64]{2,1,0:T(8,128)(2,1)S(1)} %copy-done.1), kind=kOutput, calls=%fused_computation.3.clone.1 | convolution fusion | flops 272367616 | bytes 2162688 | tf_op jit(solution)/shard_map/while/body/eval_jaxpr/tqi,bif->btqf/dot_general | solution.py:55
  40.8 0.9 fusion.30
  42.6 3.9 %scatter_fusion = f32[416,512]{1,0:T(8,128)S(1)} fusion(f32[416,512]{1,0:T(8,128)S(1)} %get-tuple-element.213, s32[512]{0:T(512)S(1)} %bitcast.110, f32[512,512]{1,0:T(8,128)S(1)} %copy.51), kind=kCustom, calls=%fused_computation.1.clone.1 | custom fusion | flops 262144 | bytes 3147776 | tf_op jit(solution)/shard_map/while/body/eval_jaxpr/scatter-add | solution.py:63
  47.3 2.2 %collective-permute-start.5 = (bf16[1,16,512]{2,1,0:T(8,128)(2,1)}, bf16[1,16,512]{2,1,0:T(8,128)(2,1)}, u32[]{:S(2)}, u32[]{:S(2)}) collective-permute-start(bf16[1,16,512]{2,1,0:T(8,128)(2,1)} %get-tuple-element.114), channel_id=1, source_target_pairs={{64,0},{128,64},{192,128},{256,192},{320,256},{384,320},{448,384},... | collective-permute-start | bytes 49160 | tf_op jit(solution)/shard_map/ppermute | solution.py:16
  49.5 4.3 %collective-permute-start = (bf16[1,3,16,512]{3,2,1,0:T(8,128)(2,1)S(1)}, bf16[1,3,16,512]{3,2,1,0:T(8,128)(2,1)}, u32[]{:S(2)}, u32[]{:S(2)}) collective-permute-start(bf16[1,3,16,512]{3,2,1,0:T(8,128)(2,1)S(1)} %maximum_bitcast_fusion), channel_id=1, source_target_pairs={{0,1},{1,2},{2,3},{3,4},{4,5},{5,6},{6,7},{7,8},{8,9},{9,10},{10,1... | collective-permute-start | bytes 147464 | tf_op jit(solution)/shard_map/ppermute | solution.py:13
  54.4 9.4 %collective-permute-start.1 = (bf16[1,3,16,512]{3,2,1,0:T(8,128)(2,1)}, bf16[1,3,16,512]{3,2,1,0:T(8,128)(2,1)}, u32[]{:S(2)}, u32[]{:S(2)}) collective-permute-start(bf16[1,3,16,512]{3,2,1,0:T(8,128)(2,1)} %maximum_bitcast_fusion.1), channel_id=1, source_target_pairs={{1,0},{2,1},{3,2},{4,3},{5,4},{6,5},{7,6},{8,7},{9,8},{10,9},{11,1... | collective-permute-start | bytes 147464 | tf_op jit(solution)/shard_map/ppermute | solution.py:16
  63.8 3.3 %copy.31 = bf16[256,4096]{0,1:T(8,128)(2,1)S(1)} copy(bf16[256,4096]{1,0:T(8,128)(2,1)} %param.21) | data formatting | bytes 4194304 | tf_op args[9]
  67.1 6.7 %copy.33 = bf16[256,64,64]{2,1,0:T(8,128)(2,1)} copy(bf16[256,64,64]{0,2,1:T(8,128)(2,1)S(1)} %bitcast.107) | data formatting | bytes 4194304 | tf_op jit(solution)/shard_map/reshape | solution.py:112
  73.8 0.7 slice_bitcast_fusion.3
  74.5 0.7 slice_bitcast_fusion.2
  75.3 3.8 %collective-permute-start.2 = (bf16[3,16,512]{2,1,0:T(8,128)(2,1)S(1)}, bf16[3,16,512]{2,1,0:T(8,128)(2,1)S(1)}, u32[]{:S(2)}, u32[]{:S(2)}) collective-permute-start(bf16[3,16,512]{2,1,0:T(8,128)(2,1)S(1)} %pad_maximum_fusion), channel_id=1, source_target_pairs={{56,0},{57,1},{58,2},{59,3},{60,4},{61,5},{62,6},{63,7},{0,8},{1,9... | collective-permute-start | bytes 147464 | tf_op jit(solution)/shard_map/ppermute | solution.py:24
  79.1 2.0 %collective-permute-start.3 = (bf16[3,16,512]{2,1,0:T(8,128)(2,1)S(1)}, bf16[3,16,512]{2,1,0:T(8,128)(2,1)S(1)}, u32[]{:S(2)}, u32[]{:S(2)}) collective-permute-start(bf16[3,16,512]{2,1,0:T(8,128)(2,1)S(1)} %pad_maximum_fusion.1), channel_id=1, source_target_pairs={{8,0},{9,1},{10,2},{11,3},{12,4},{13,5},{14,6},{15,7},{16,8},{17,9... | collective-permute-start | bytes 147464 | tf_op jit(solution)/shard_map/ppermute | solution.py:24
  82.6 3.7 %collective-permute-done.3 = bf16[3,16,512]{2,1,0:T(8,128)(2,1)S(1)} collective-permute-done((bf16[3,16,512]{2,1,0:T(8,128)(2,1)S(1)}, bf16[3,16,512]{2,1,0:T(8,128)(2,1)S(1)}, u32[]{:S(2)}, u32[]{:S(2)}) %collective-permute-start.3) | collective-permute-done | bytes 49184 | tf_op jit(solution)/shard_map/ppermute | solution.py:24
  86.3 0.7 constant_dynamic-update-slice_fusion.1
  87.8 1.9 %scatter_custom_fusion.1 = f32[256,512]{1,0:T(8,128)S(1)} fusion(f32[256,512]{1,0:T(8,128)S(1)} %slice.129, s32[160]{0:T(256)} %bitcast.116, bf16[160,512]{1,0:T(8,128)(2,1)S(1)} %bitcast.115), kind=kCustom, calls=%fused_computation.29 | custom fusion | flops 163840 | bytes 688128 | tf_op jit(solution)/shard_map/scatter-add | solution.py:108
  90.3 4.4 %convolution_bitcast_fusion = f32[256,64,8]{1,2,0:T(8,128)S(1)} fusion(bf16[256,64,8]{1,2,0:T(8,128)(2,1)S(1)} %copy.32, bf16[256,64,64]{2,1,0:T(8,128)(2,1)} %copy.33), kind=kOutput, calls=%fused_computation.28 | convolution fusion | flops 16777216 | bytes 2883584 | tf_op jit(solution)/shard_map/zjk,zkf->zjf/dot_general | solution.py:113
  95.2 1.0 %copy.35 = f32[256,512]{1,0:T(8,128)} copy(f32[256,512]{0,1:T(8,128)S(1)} %bitcast.108) | data formatting | bytes 1048576 | tf_op jit(solution)/shard_map/reshape | solution.py:114
  (91 shorter events, 13.2 us)
Async XLA Ops:
  4.0 3.4 %copy-start = (f32[8,64]{1,0:T(8,128)S(1)}, f32[8,64]{1,0:T(8,128)}, u32[]{:S(2)}) copy-start(f32[8,64]{1,0:T(8,128)} %get-tuple-element.227) | copy-start | bytes 6148 | tf_op jit(solution)/shard_map/while
  4.0 3.5 %copy-start.1 = (bf16[8,64,64]{2,1,0:T(8,128)(2,1)S(1)}, bf16[8,64,64]{2,1,0:T(8,128)(2,1)}, u32[]{:S(2)}) copy-start(bf16[8,64,64]{2,1,0:T(8,128)(2,1)} %get-tuple-element.231) | copy-start | bytes 196612 | tf_op jit(solution)/shard_map/while
  14.6 3.4 %copy-start = (f32[8,64]{1,0:T(8,128)S(1)}, f32[8,64]{1,0:T(8,128)}, u32[]{:S(2)}) copy-start(f32[8,64]{1,0:T(8,128)} %get-tuple-element.227) | copy-start | bytes 6148 | tf_op jit(solution)/shard_map/while
  14.6 3.5 %copy-start.1 = (bf16[8,64,64]{2,1,0:T(8,128)(2,1)S(1)}, bf16[8,64,64]{2,1,0:T(8,128)(2,1)}, u32[]{:S(2)}) copy-start(bf16[8,64,64]{2,1,0:T(8,128)(2,1)} %get-tuple-element.231) | copy-start | bytes 196612 | tf_op jit(solution)/shard_map/while
  25.3 3.4 %copy-start = (f32[8,64]{1,0:T(8,128)S(1)}, f32[8,64]{1,0:T(8,128)}, u32[]{:S(2)}) copy-start(f32[8,64]{1,0:T(8,128)} %get-tuple-element.227) | copy-start | bytes 6148 | tf_op jit(solution)/shard_map/while
  25.3 3.5 %copy-start.1 = (bf16[8,64,64]{2,1,0:T(8,128)(2,1)S(1)}, bf16[8,64,64]{2,1,0:T(8,128)(2,1)}, u32[]{:S(2)}) copy-start(bf16[8,64,64]{2,1,0:T(8,128)(2,1)} %get-tuple-element.231) | copy-start | bytes 196612 | tf_op jit(solution)/shard_map/while
  35.9 3.4 %copy-start = (f32[8,64]{1,0:T(8,128)S(1)}, f32[8,64]{1,0:T(8,128)}, u32[]{:S(2)}) copy-start(f32[8,64]{1,0:T(8,128)} %get-tuple-element.227) | copy-start | bytes 6148 | tf_op jit(solution)/shard_map/while
  35.9 3.5 %copy-start.1 = (bf16[8,64,64]{2,1,0:T(8,128)(2,1)S(1)}, bf16[8,64,64]{2,1,0:T(8,128)(2,1)}, u32[]{:S(2)}) copy-start(bf16[8,64,64]{2,1,0:T(8,128)(2,1)} %get-tuple-element.231) | copy-start | bytes 196612 | tf_op jit(solution)/shard_map/while
  47.3 39.8 %collective-permute-start.5 = (bf16[1,16,512]{2,1,0:T(8,128)(2,1)}, bf16[1,16,512]{2,1,0:T(8,128)(2,1)}, u32[]{:S(2)}, u32[]{:S(2)}) collective-permute-start(bf16[1,16,512]{2,1,0:T(8,128)(2,1)} %get-tuple-element.114), channel_id=1, source_target_pairs={{64,0},{128,64},{192,128},{256,192},{320,256},{384,320},{448,384},... | collective-permute-start | bytes 49160 | tf_op jit(solution)/shard_map/ppermute | solution.py:16
  49.5 36.9 %collective-permute-start.4 = (bf16[1,16,512]{2,1,0:T(8,128)(2,1)}, bf16[1,16,512]{2,1,0:T(8,128)(2,1)}, u32[]{:S(2)}, u32[]{:S(2)}) collective-permute-start(bf16[1,16,512]{2,1,0:T(8,128)(2,1)} %get-tuple-element.115), channel_id=1, source_target_pairs={{0,64},{64,128},{128,192},{192,256},{256,320},{320,384},{384,448},... | collective-permute-start | bytes 49160 | tf_op jit(solution)/shard_map/ppermute | solution.py:13
  49.5 24.3 %collective-permute-start = (bf16[1,3,16,512]{3,2,1,0:T(8,128)(2,1)S(1)}, bf16[1,3,16,512]{3,2,1,0:T(8,128)(2,1)}, u32[]{:S(2)}, u32[]{:S(2)}) collective-permute-start(bf16[1,3,16,512]{3,2,1,0:T(8,128)(2,1)S(1)} %maximum_bitcast_fusion), channel_id=1, source_target_pairs={{0,1},{1,2},{2,3},{3,4},{4,5},{5,6},{6,7},{7,8},{8,9},{9,10},{10,1... | collective-permute-start | bytes 147464 | tf_op jit(solution)/shard_map/ppermute | solution.py:13
  54.4 20.1 %collective-permute-start.1 = (bf16[1,3,16,512]{3,2,1,0:T(8,128)(2,1)}, bf16[1,3,16,512]{3,2,1,0:T(8,128)(2,1)}, u32[]{:S(2)}, u32[]{:S(2)}) collective-permute-start(bf16[1,3,16,512]{3,2,1,0:T(8,128)(2,1)} %maximum_bitcast_fusion.1), channel_id=1, source_target_pairs={{1,0},{2,1},{3,2},{4,3},{5,4},{6,5},{7,6},{8,7},{9,8},{10,9},{11,1... | collective-permute-start | bytes 147464 | tf_op jit(solution)/shard_map/ppermute | solution.py:16
  75.3 7.3 %collective-permute-start.2 = (bf16[3,16,512]{2,1,0:T(8,128)(2,1)S(1)}, bf16[3,16,512]{2,1,0:T(8,128)(2,1)S(1)}, u32[]{:S(2)}, u32[]{:S(2)}) collective-permute-start(bf16[3,16,512]{2,1,0:T(8,128)(2,1)S(1)} %pad_maximum_fusion), channel_id=1, source_target_pairs={{56,0},{57,1},{58,2},{59,3},{60,4},{61,5},{62,6},{63,7},{0,8},{1,9... | collective-permute-start | bytes 147464 | tf_op jit(solution)/shard_map/ppermute | solution.py:24
  79.1 7.2 %collective-permute-start.3 = (bf16[3,16,512]{2,1,0:T(8,128)(2,1)S(1)}, bf16[3,16,512]{2,1,0:T(8,128)(2,1)S(1)}, u32[]{:S(2)}, u32[]{:S(2)}) collective-permute-start(bf16[3,16,512]{2,1,0:T(8,128)(2,1)S(1)} %pad_maximum_fusion.1), channel_id=1, source_target_pairs={{8,0},{9,1},{10,2},{11,3},{12,4},{13,5},{14,6},{15,7},{16,8},{17,9... | collective-permute-start | bytes 147464 | tf_op jit(solution)/shard_map/ppermute | solution.py:24
where the time goes:
time: 97.4 us; the launch traced here: 96.2 us
  local copies, waits for them, and re-layouts  37.6 us (39%)
  starting transfers between devices  21.7 us (22%)
  other arithmetic  19.3 us (20%)
  matrix products  13.2 us (14%)
  waiting for transfers between devices  3.71 us (4%)
    scatter-add x4, other arithmetic, quad_block(): jax.ops.segment_sum(moment.reshape(block_rows, row_width), dest_blk, num_...  15.7 us
    gather x8, local copies, waits for them, and re-layouts, quad_block(): jnp.take(old_coeff, zone_blk, axis=0)  12.7 us
    ppermute x2, starting transfers between devices, extended_2(): lax.ppermute(lax.slice_in_dim(block, 0, width, axis=dim), axis, backward)  11.6 us
    reshape x1, local copies, waits for them, and re-layouts, on_device(): inverse = inv_mass.reshape(zone_count, basis_size, basis_size)  6.69 us
    ppermute x2, starting transfers between devices, passed_along(): return lax.ppermute(block, axis, route)  5.84 us
    unnamed x10, local copies, waits for them, and re-layouts  5.45 us
    dot_general x4, matrix products, quad_block(): jnp.einsum('tqi,bif->btqf', basis_old, picked, preferred_element_type=jnp...  5.11 us
    dot_general x1, matrix products, on_device(): jnp.einsum('zjk,zkf->zjf', inverse, rounded, preferred_element_type=jnp.f...  4.43 us
  transfers between devices with their start and end apart: 6, of which 1 were waited for; matrix products, arithmetic and copies ran while one was open for 15% of the time, Pallas kernels for 0%

commit v1 on v0

v1 whole, which is shorter than its diff:
```python
import functools

import jax
import jax.numpy as jnp
from jax import lax
from jax.experimental import pallas as pl
from jax.experimental.pallas import tpu as pltpu
from jax.sharding import PartitionSpec as P

F32 = jnp.float32
BF16 = jnp.bfloat16


def tet_kernel(
    zone_ref, table_ref, vol_ref, dest_ref, ct_ref, bold_ref, bnewt_ref, qwt_ref, out_ref, mom_ref,
    *, tables, basis, fields, zones, rows_pad
):
    step = pl.program_id(0)

    @pl.when(step == 0)
    def _():
        out_ref[...] = jnp.zeros_like(out_ref)

    block = zone_ref.shape[1]
    zone = zone_ref[...]
    zone_hot = (lax.broadcasted_iota(jnp.int32, (zones, block), 0) == zone).astype(BF16)
    picked = jnp.dot(ct_ref[...], zone_hot, preferred_element_type=F32).astype(BF16)
    table = table_ref[...]
    masks = [table == t for t in range(tables)]
    qwt = qwt_ref[...]
    scale = jnp.broadcast_to(qwt[:, 0:1], (basis, block))
    for t in range(1, tables):
        scale = jnp.where(masks[t], qwt[:, t : t + 1], scale)
    scale = scale * vol_ref[...]
    bold = bold_ref[...]
    bnewt = bnewt_ref[...]
    for f in range(fields):
        every = jnp.dot(bold, picked[f * basis : (f + 1) * basis, :], preferred_element_type=F32)
        values = every[0:basis]
        for t in range(1, tables):
            values = jnp.where(masks[t], every[t * basis : (t + 1) * basis], values)
        weighted = (scale * values).astype(BF16)
        every = jnp.dot(bnewt, weighted, preferred_element_type=F32)
        moment = every[0:basis]
        for t in range(1, tables):
            moment = jnp.where(masks[t], every[t * basis : (t + 1) * basis], moment)
        mom_ref[f * basis : (f + 1) * basis, :] = moment
    moments = mom_ref[...]
    high = moments.astype(BF16)
    low = (moments - high.astype(F32)).astype(BF16)
    dest_hot = (lax.broadcasted_iota(jnp.int32, (block, rows_pad), 1) == dest_ref[...]).astype(BF16)
    out_ref[...] += jnp.dot(high, dest_hot, preferred_element_type=F32) + jnp.dot(
        low, dest_hot, preferred_element_type=F32
    )


def tet_partials(coeff_t, bold, bnewt, qwt, zone, table, vol, dest, rows_pad, block):
    tet_count = zone.shape[0]
    width, zones = coeff_t.shape
    tables = qwt.shape[1]
    basis = bold.shape[1]
    fields = width // basis
    kernel = functools.partial(
        tet_kernel, tables=tables, basis=basis, fields=fields, zones=zones, rows_pad=rows_pad
    )
    row_spec = pl.BlockSpec((1, block), lambda i: (0, i))
    whole = lambda shape: pl.BlockSpec(shape, lambda i: (0, 0))
    return pl.pallas_call(
        kernel,
        grid=(tet_count // block,),
        in_specs=[
            row_spec,
            row_spec,
            row_spec,
            pl.BlockSpec((block, 1), lambda i: (i, 0)),
            whole(coeff_t.shape),
            whole(bold.shape),
            whole(bnewt.shape),
            whole(qwt.shape),
        ],
        out_specs=whole((width, rows_pad)),
        out_shape=jax.ShapeDtypeStruct((width, rows_pad), F32),
        scratch_shapes=[pltpu.VMEM((width, block), F32)],
        compiler_params=pltpu.CompilerParams(dimension_semantics=("arbitrary",)),
    )(
        zone.reshape(1, tet_count),
        table.reshape(1, tet_count),
        vol.reshape(1, tet_count),
        dest.reshape(tet_count, 1),
        coeff_t,
        bold,
        bnewt,
        qwt,
    )


def shifted(block, axis, distance):
    count = lax.axis_size(axis)
    route = [(i, (i + distance) % count) for i in range(count)]
    return lax.ppermute(block, axis, route)


def on_device(
    old_coeff,
    basis_old,
    basis_new,
    quad_weight,
    tet_zone,
    tet_table,
    tet_volume,
    tet_dest,
    recv_list,
    inv_mass,
):
    zone_count, row_width = old_coeff.shape
    tables, quad, basis = basis_old.shape
    fields = row_width // basis
    slot_total = recv_list.shape[1]
    partner_count = 10
    slot_cap = slot_total // partner_count
    row_count = zone_count + slot_total
    rows_pad = -(-row_count // 128) * 128
    block = min(512, tet_zone.shape[0])

    coeff_t = old_coeff.reshape(zone_count, basis, fields).transpose(2, 1, 0).reshape(row_width, zone_count)
    bold = basis_old.reshape(tables * quad, basis)
    bnewt = basis_new.transpose(0, 2, 1).reshape(tables * basis, quad)
    qwt = quad_weight.T
    partial_t = tet_partials(
        coeff_t, bold, bnewt, qwt, tet_zone, tet_table, tet_volume, tet_dest, rows_pad, block
    )
    own_t = partial_t[:, :zone_count]
    outgoing = partial_t[:, zone_count:row_count].astype(BF16)

    lane_count = lax.axis_size("yz")
    face_side = 1 << (lane_count.bit_length() - 1) // 2
    offsets = [1, -1, face_side, -face_side, face_side + 1, -face_side - 1, face_side - 1, 1 - face_side]
    arrived = []
    for k in range(partner_count):
        piece = outgoing[:, k * slot_cap : (k + 1) * slot_cap]
        if k < 8:
            arrived.append(shifted(piece, "yz", offsets[k]))
        else:
            arrived.append(shifted(piece, "gx", 1 if k == 8 else -1))
    received_t = jnp.concatenate(arrived, axis=1)
    slot_hot = (recv_list[0][:, None] == jnp.arange(zone_count, dtype=jnp.int32)[None, :]).astype(BF16)
    gathered_t = own_t + jnp.dot(received_t, slot_hot, preferred_element_type=F32)
    rounded_t = gathered_t.astype(BF16).reshape(fields, basis, zone_count)
    rounded = rounded_t.transpose(2, 1, 0)
    inverse = inv_mass.reshape(zone_count, basis, basis)
    result = jnp.einsum("zjk,zkf->zjf", inverse, rounded, preferred_element_type=F32)
    return result.reshape(zone_count, row_width)


def solution(mesh):
    placed = (
        P(("gx", "yz"), None),
        P(),
        P(),
        P(),
        P(("gx", "yz")),
        P(("gx", "yz")),
        P(("gx", "yz")),
        P(("gx", "yz")),
        P(("gx", "yz"), None),
        P(("gx", "yz"), None),
    )
    return jax.shard_map(
        on_device, mesh=mesh, in_specs=placed, out_specs=P(("gx", "yz"), None), check_vma=False
    )
```

time: 97.4 us -> 89.6 us (0.920)
  the two profiles are of different devices: /device:TPU:56 before, /device:TPU:7 now
where the time goes in v1:
time: 89.6 us; the launch traced here: 89 us
  starting transfers between devices  41.8 us (47%)
  local copies, waits for them, and re-layouts  22 us (25%)
  Pallas kernels  18.9 us (21%)
  matrix products  4.72 us (5%)
  other arithmetic  1.29 us (1%)
    ppermute x10, starting transfers between devices, shifted(): return lax.ppermute(block, axis, route)  41.8 us
    pallas_call x1, Pallas kernels, tet_partials(): pl.pallas_call(kernel, grid=(tet_count // block,), in_specs=[row_spec, ro...  18.9 us
    reshape x1, local copies, waits for them, and re-layouts, on_device(): inverse = inv_mass.reshape(zone_count, basis, basis)  6.67 us
    unnamed x15, local copies, waits for them, and re-layouts  6.38 us
    dot_general x1, matrix products, on_device(): jnp.einsum('zjk,zkf->zjf', inverse, rounded, preferred_element_type=F32)  4.43 us
    reshape x1, local copies, waits for them, and re-layouts, tet_partials(): dest.reshape(tet_count, 1)  2.04 us
  transfers between devices with their start and end apart: 10, of which 0 were waited for; matrix products, arithmetic and copies ran while one was open for 11% of the time, Pallas kernels for 0%

profile of v1, /device:TPU:7, one launch (start us, length us, event | category | flops | bytes accessed | tf_op | source)
XLA Modules:
  0.0 89.0 jit_solution(16114730263099444009)
XLA Ops:
  0.0 1.4 %copy.18 = f32[8,64]{0,1:T(8,128)} copy(f32[8,64]{1,0:T(8,128)} %param.13) | data formatting | bytes 4096 | tf_op args[3]
  1.4 1.7 %copy.17 = bf16[8,64,64]{2,1,0:T(8,128)(2,1)} copy(bf16[8,64,64]{1,2,0:T(8,128)(2,1)} %bitcast.29) | data formatting | bytes 131072 | tf_op jit(solution)/shard_map/transpose | solution.py:127
  3.0 1.1 %copy.15 = bf16[256,512]{0,1:T(8,128)(2,1)S(1)} copy(bf16[256,512]{1,0:T(8,128)(2,1)} %param.10) | data formatting | bytes 524288 | tf_op args[0]
  4.1 0.8 copy.16
  4.9 2.0 %copy.19.dest_ref = s32[2048,1]{1,0:T(8,128)} copy(s32[2048,1]{0,1:T(1,128)} %bitcast.32) | data formatting | bytes 16384 | tf_op jit(solution)/shard_map/reshape | solution.py:89
  6.9 18.9 %shard_map.100 = f32[512,512]{1,0:T(8,128)} custom-call(s32[1,2048]{1,0:T(1,128)} %bitcast.33, s32[1,2048]{1,0:T(1,128)} %bitcast.34, f32[1,2048]{1,0:T(1,128)} %bitcast.35, s32[2048,1]{1,0:T(8,128)} %copy.19.dest_ref, bf16[512,256]{1,0:T(8,128)(2,1)} %bitcast.27, bf16[512,64]{1,0:T(8,128)(2,1)} %bitcast.30, bf16[512,64]{1,0:T(8,128)(2,1)} %bitcast.28, ...), custom_call_target="tpu_custom_call" | custom-call | tf_op jit(solution)/shard_map/pallas_call | solution.py:68
  25.8 1.3 %convert.3 = bf16[512,512]{1,0:T(8,128)(2,1)S(1)} convert(f32[512,512]{1,0:T(8,128)} %shard_map.100) | non-fusion elementwise | flops 262144 | bytes 1572864 | tf_op jit(solution)/shard_map/convert
  27.1 1.1 %fusion.3 = (bf16[512,16]{1,0:T(8,128)(2,1)S(1)}, bf16[512,16]{1,0:T(8,128)(2,1)S(1)}, bf16[512,16]{1,0:T(8,128)(2,1)S(1)}, bf16[512,16]{1,0:T(8,128)(2,1)S(1)},...) fusion(bf16[512,512]{1,0:T(8,128)(2,1)S(1)} %convert.3), kind=kLoop, calls=%fused_computation.6 | loop fusion | bytes 327680 | tf_op jit(solution)/shard_map/slice | solution.py:140
  28.2 0.7 collective-permute-start.9
  28.8 5.4 %collective-permute-start.8 = (bf16[512,16]{1,0:T(8,128)(2,1)S(1)}, bf16[512,16]{1,0:T(8,128)(2,1)S(1)}, u32[]{:S(2)}, u32[]{:S(2)}) collective-permute-start(bf16[512,16]{1,0:T(8,128)(2,1)S(1)} %get-tuple-element.6), channel_id=1, source_target_pairs={{0,64},{64,128},{128,192},{192,256},{256,320},{320,384},{384,448},... | collective-permute-start | bytes 49160 | tf_op jit(solution)/shard_map/ppermute | solution.py:100
  34.3 3.7 %collective-permute-start.7 = (bf16[512,16]{1,0:T(8,128)(2,1)S(1)}, bf16[512,16]{1,0:T(8,128)(2,1)S(1)}, u32[]{:S(2)}, u32[]{:S(2)}) collective-permute-start(bf16[512,16]{1,0:T(8,128)(2,1)S(1)} %get-tuple-element.7), channel_id=1, source_target_pairs={{0,57},{1,58},{2,59},{3,60},{4,61},{5,62},{6,63},{7,0},{8,1},{9,2}... | collective-permute-start | bytes 49160 | tf_op jit(solution)/shard_map/ppermute | solution.py:100
  38.0 5.7 %collective-permute-start.6 = (bf16[512,16]{1,0:T(8,128)(2,1)S(1)}, bf16[512,16]{1,0:T(8,128)(2,1)S(1)}, u32[]{:S(2)}, u32[]{:S(2)}) collective-permute-start(bf16[512,16]{1,0:T(8,128)(2,1)S(1)} %get-tuple-element.8), channel_id=1, source_target_pairs={{0,7},{1,8},{2,9},{3,10},{4,11},{5,12},{6,13},{7,14},{8,15},{9,16}... | collective-permute-start | bytes 49160 | tf_op jit(solution)/shard_map/ppermute | solution.py:100
  43.7 8.0 %collective-permute-start.5 = (bf16[512,16]{1,0:T(8,128)(2,1)S(1)}, bf16[512,16]{1,0:T(8,128)(2,1)S(1)}, u32[]{:S(2)}, u32[]{:S(2)}) collective-permute-start(bf16[512,16]{1,0:T(8,128)(2,1)S(1)} %get-tuple-element.9), channel_id=1, source_target_pairs={{0,55},{1,56},{2,57},{3,58},{4,59},{5,60},{6,61},{7,62},{8,63},{9,... | collective-permute-start | bytes 49160 | tf_op jit(solution)/shard_map/ppermute | solution.py:100
  51.6 1.9 %collective-permute-start.4 = (bf16[512,16]{1,0:T(8,128)(2,1)}, bf16[512,16]{1,0:T(8,128)(2,1)}, u32[]{:S(2)}, u32[]{:S(2)}) collective-permute-start(bf16[512,16]{1,0:T(8,128)(2,1)} %get-tuple-element.10), channel_id=1, source_target_pairs={{0,9},{1,10},{2,11},{3,12},{4,13},{5,14},{6,15},{7,16},{8,17},{9,1... | collective-permute-start | bytes 49160 | tf_op jit(solution)/shard_map/ppermute | solution.py:100
  53.6 3.0 %collective-permute-start.3 = (bf16[512,16]{1,0:T(8,128)(2,1)}, bf16[512,16]{1,0:T(8,128)(2,1)}, u32[]{:S(2)}, u32[]{:S(2)}) collective-permute-start(bf16[512,16]{1,0:T(8,128)(2,1)} %get-tuple-element.11), channel_id=1, source_target_pairs={{0,56},{1,57},{2,58},{3,59},{4,60},{5,61},{6,62},{7,63},{8,0},{9,1... | collective-permute-start | bytes 49160 | tf_op jit(solution)/shard_map/ppermute | solution.py:100
  56.6 2.5 %collective-permute-start.2 = (bf16[512,16]{1,0:T(8,128)(2,1)}, bf16[512,16]{1,0:T(8,128)(2,1)}, u32[]{:S(2)}, u32[]{:S(2)}) collective-permute-start(bf16[512,16]{1,0:T(8,128)(2,1)} %get-tuple-element.12), channel_id=1, source_target_pairs={{0,8},{1,9},{2,10},{3,11},{4,12},{5,13},{6,14},{7,15},{8,16},{9,17... | collective-permute-start | bytes 49160 | tf_op jit(solution)/shard_map/ppermute | solution.py:100
  59.1 9.1 %collective-permute-start.1 = (bf16[512,16]{1,0:T(8,128)(2,1)S(1)}, bf16[512,16]{1,0:T(8,128)(2,1)}, u32[]{:S(2)}, u32[]{:S(2)}) collective-permute-start(bf16[512,16]{1,0:T(8,128)(2,1)S(1)} %get-tuple-element.13), channel_id=1, source_target_pairs={{0,63},{1,0},{2,1},{3,2},{4,3},{5,4},{6,5},{7,6},{8,7},{9,8},{10,9... | collective-permute-start | bytes 49160 | tf_op jit(solution)/shard_map/ppermute | solution.py:100
  68.2 0.0 collective-permute-done.5
  68.2 0.6 copy-done.4
  68.9 1.9 %collective-permute-start = (bf16[512,16]{1,0:T(8,128)(2,1)S(1)}, bf16[512,16]{1,0:T(8,128)(2,1)}, u32[]{:S(2)}, u32[]{:S(2)}) collective-permute-start(bf16[512,16]{1,0:T(8,128)(2,1)S(1)} %get-tuple-element.14), channel_id=1, source_target_pairs={{0,1},{1,2},{2,3},{3,4},{4,5},{5,6},{6,7},{7,8},{8,9},{9,10},{10,1... | collective-permute-start | bytes 49160 | tf_op jit(solution)/shard_map/ppermute | solution.py:100
  70.8 3.3 %copy.21 = bf16[256,4096]{0,1:T(8,128)(2,1)S(1)} copy(bf16[256,4096]{1,0:T(8,128)(2,1)} %param.19) | data formatting | bytes 4194304 | tf_op args[9]
  74.1 0.0 copy-start.5
  74.1 6.7 %copy.22 = bf16[256,64,64]{2,1,0:T(8,128)(2,1)} copy(bf16[256,64,64]{0,2,1:T(8,128)(2,1)S(1)} %bitcast.23) | data formatting | bytes 4194304 | tf_op jit(solution)/shard_map/reshape | solution.py:150
  80.8 0.0 collective-permute-done.4
  80.8 0.0 collective-permute-done.3
  80.8 0.0 collective-permute-done.2
  80.8 1.6 %concatenate.3 = bf16[512,160]{1,0:T(8,128)(2,1)S(1)} concatenate(bf16[512,16]{1,0:T(8,128)(2,1)} %collective-permute-done, bf16[512,16]{1,0:T(8,128)(2,1)} %collective-permute-done.1, bf16[512,16]{1,0:T(8,128)(2,1)} %collective-permute-done.2, bf16[512,16]{1,0:T(8,128)(2,1)} %collective-permute-done.3, bf16[512,16]{1,0:T(8,128)(2,1)} %collective-permute-done.4, ...), dimensions={1} | concatenate | bytes 327680 | tf_op jit(solution)/shard_map/concatenate | solution.py:145
  82.4 0.3 fusion
  82.7 0.3 copy.20
  83.0 4.4 %convolution_bitcast_fusion = f32[256,64,8]{1,2,0:T(8,128)S(1)} fusion(bf16[256,64,64]{2,1,0:T(8,128)(2,1)} %copy.22, bf16[8,64,256]{1,0,2:T(8,128)(2,1)S(1)} %copy.20), kind=kOutput, calls=%fused_computation | convolution fusion | flops 16777216 | bytes 2883584 | tf_op jit(solution)/shard_map/zjk,zkf->zjf/dot_general | solution.py:151
  87.5 0.5 copy.23
  88.0 1.0 %copy.24 = f32[256,512]{1,0:T(8,128)} copy(f32[256,512]{0,1:T(8,128)S(1)} %bitcast.24) | data formatting | bytes 1048576 | tf_op jit(solution)/shard_map/reshape | solution.py:152
  (16 shorter events, 0.0 us)
Async XLA Ops:
  28.2 23.5 %collective-permute-start.9 = (bf16[512,16]{1,0:T(8,128)(2,1)S(1)}, bf16[512,16]{1,0:T(8,128)(2,1)S(1)}, u32[]{:S(2)}, u32[]{:S(2)}) collective-permute-start(bf16[512,16]{1,0:T(8,128)(2,1)S(1)} %get-tuple-element.5), channel_id=1, source_target_pairs={{0,448},{64,0},{128,64},{192,128},{256,192},{320,256},{384,320},{4... | collective-permute-start | bytes 49160 | tf_op jit(solution)/shard_map/ppermute | solution.py:100
  28.8 24.7 %collective-permute-start.8 = (bf16[512,16]{1,0:T(8,128)(2,1)S(1)}, bf16[512,16]{1,0:T(8,128)(2,1)S(1)}, u32[]{:S(2)}, u32[]{:S(2)}) collective-permute-start(bf16[512,16]{1,0:T(8,128)(2,1)S(1)} %get-tuple-element.6), channel_id=1, source_target_pairs={{0,64},{64,128},{128,192},{192,256},{256,320},{320,384},{384,448},... | collective-permute-start | bytes 49160 | tf_op jit(solution)/shard_map/ppermute | solution.py:100
  34.3 22.4 %collective-permute-start.7 = (bf16[512,16]{1,0:T(8,128)(2,1)S(1)}, bf16[512,16]{1,0:T(8,128)(2,1)S(1)}, u32[]{:S(2)}, u32[]{:S(2)}) collective-permute-start(bf16[512,16]{1,0:T(8,128)(2,1)S(1)} %get-tuple-element.7), channel_id=1, source_target_pairs={{0,57},{1,58},{2,59},{3,60},{4,61},{5,62},{6,63},{7,0},{8,1},{9,2}... | collective-permute-start | bytes 49160 | tf_op jit(solution)/shard_map/ppermute | solution.py:100
  38.0 21.1 %collective-permute-start.6 = (bf16[512,16]{1,0:T(8,128)(2,1)S(1)}, bf16[512,16]{1,0:T(8,128)(2,1)S(1)}, u32[]{:S(2)}, u32[]{:S(2)}) collective-permute-start(bf16[512,16]{1,0:T(8,128)(2,1)S(1)} %get-tuple-element.8), channel_id=1, source_target_pairs={{0,7},{1,8},{2,9},{3,10},{4,11},{5,12},{6,13},{7,14},{8,15},{9,16}... | collective-permute-start | bytes 49160 | tf_op jit(solution)/shard_map/ppermute | solution.py:100
  43.7 24.5 %collective-permute-start.5 = (bf16[512,16]{1,0:T(8,128)(2,1)S(1)}, bf16[512,16]{1,0:T(8,128)(2,1)S(1)}, u32[]{:S(2)}, u32[]{:S(2)}) collective-permute-start(bf16[512,16]{1,0:T(8,128)(2,1)S(1)} %get-tuple-element.9), channel_id=1, source_target_pairs={{0,55},{1,56},{2,57},{3,58},{4,59},{5,60},{6,61},{7,62},{8,63},{9,... | collective-permute-start | bytes 49160 | tf_op jit(solution)/shard_map/ppermute | solution.py:100
  51.6 29.1 %collective-permute-start.4 = (bf16[512,16]{1,0:T(8,128)(2,1)}, bf16[512,16]{1,0:T(8,128)(2,1)}, u32[]{:S(2)}, u32[]{:S(2)}) collective-permute-start(bf16[512,16]{1,0:T(8,128)(2,1)} %get-tuple-element.10), channel_id=1, source_target_pairs={{0,9},{1,10},{2,11},{3,12},{4,13},{5,14},{6,15},{7,16},{8,17},{9,1... | collective-permute-start | bytes 49160 | tf_op jit(solution)/shard_map/ppermute | solution.py:100
  53.6 14.6 %copy-start.1 = (bf16[512,16]{1,0:T(8,128)(2,1)}, bf16[512,16]{1,0:T(8,128)(2,1)S(1)}, u32[]{:S(2)}) copy-start(bf16[512,16]{1,0:T(8,128)(2,1)S(1)} %collective-permute-done.8) | copy-start | bytes 49156
  53.6 27.2 %collective-permute-start.3 = (bf16[512,16]{1,0:T(8,128)(2,1)}, bf16[512,16]{1,0:T(8,128)(2,1)}, u32[]{:S(2)}, u32[]{:S(2)}) collective-permute-start(bf16[512,16]{1,0:T(8,128)(2,1)} %get-tuple-element.11), channel_id=1, source_target_pairs={{0,56},{1,57},{2,58},{3,59},{4,60},{5,61},{6,62},{7,63},{8,0},{9,1... | collective-permute-start | bytes 49160 | tf_op jit(solution)/shard_map/ppermute | solution.py:100
  56.6 11.6 %copy-start.2 = (bf16[512,16]{1,0:T(8,128)(2,1)}, bf16[512,16]{1,0:T(8,128)(2,1)S(1)}, u32[]{:S(2)}) copy-start(bf16[512,16]{1,0:T(8,128)(2,1)S(1)} %collective-permute-done.7) | copy-start | bytes 49156
  56.6 24.1 %collective-permute-start.2 = (bf16[512,16]{1,0:T(8,128)(2,1)}, bf16[512,16]{1,0:T(8,128)(2,1)}, u32[]{:S(2)}, u32[]{:S(2)}) collective-permute-start(bf16[512,16]{1,0:T(8,128)(2,1)} %get-tuple-element.12), channel_id=1, source_target_pairs={{0,8},{1,9},{2,10},{3,11},{4,12},{5,13},{6,14},{7,15},{8,16},{9,17... | collective-permute-start | bytes 49160 | tf_op jit(solution)/shard_map/ppermute | solution.py:100
  59.1 9.1 %copy-start.3 = (bf16[512,16]{1,0:T(8,128)(2,1)}, bf16[512,16]{1,0:T(8,128)(2,1)S(1)}, u32[]{:S(2)}) copy-start(bf16[512,16]{1,0:T(8,128)(2,1)S(1)} %collective-permute-done.6) | copy-start | bytes 49156
  59.1 21.7 %collective-permute-start.1 = (bf16[512,16]{1,0:T(8,128)(2,1)S(1)}, bf16[512,16]{1,0:T(8,128)(2,1)}, u32[]{:S(2)}, u32[]{:S(2)}) collective-permute-start(bf16[512,16]{1,0:T(8,128)(2,1)S(1)} %get-tuple-element.13), channel_id=1, source_target_pairs={{0,63},{1,0},{2,1},{3,2},{4,3},{5,4},{6,5},{7,6},{8,7},{9,8},{10,9... | collective-permute-start | bytes 49160 | tf_op jit(solution)/shard_map/ppermute | solution.py:100
  68.2 0.7 copy-start.4
  68.9 11.9 %collective-permute-start = (bf16[512,16]{1,0:T(8,128)(2,1)S(1)}, bf16[512,16]{1,0:T(8,128)(2,1)}, u32[]{:S(2)}, u32[]{:S(2)}) collective-permute-start(bf16[512,16]{1,0:T(8,128)(2,1)S(1)} %get-tuple-element.14), channel_id=1, source_target_pairs={{0,1},{1,2},{2,3},{3,4},{4,5},{5,6},{6,7},{7,8},{8,9},{9,10},{10,1... | collective-permute-start | bytes 49160 | tf_op jit(solution)/shard_map/ppermute | solution.py:100
  74.1 8.3 %copy-start = (f32[512,512]{1,0:T(8,128)S(1)}, f32[512,512]{1,0:T(8,128)}, u32[]{:S(2)}) copy-start(f32[512,512]{1,0:T(8,128)} %shard_map.100) | copy-start | bytes 3145732
  74.1 8.3 %copy-start.5 = (s32[1,160]{1,0:T(1,128)S(1)}, s32[1,160]{1,0:T(1,128)}, u32[]{:S(2)}) copy-start(s32[1,160]{1,0:T(1,128)} %param.18) | copy-start | bytes 1924

commit v2 on v1

v2 whole, which is shorter than its diff:
```python
import functools

import jax
import jax.numpy as jnp
from jax import lax
from jax.experimental import pallas as pl
from jax.experimental.pallas import tpu as pltpu
from jax.sharding import PartitionSpec as P

F32 = jnp.float32
BF16 = jnp.bfloat16


def tet_kernel(
    zone_ref, table_ref, vol_ref, dest_ref, ct_ref, bold_ref, bnewt_ref, qwt_ref, own_ref, slot_ref, mom_ref,
    *, tables, basis, fields, zones, slots_pad
):
    step = pl.program_id(0)

    @pl.when(step == 0)
    def _():
        own_ref[...] = jnp.zeros_like(own_ref)
        slot_ref[...] = jnp.zeros_like(slot_ref)

    block = zone_ref.shape[1]
    zone = zone_ref[...]
    zone_hot = (lax.broadcasted_iota(jnp.int32, (zones, block), 0) == zone).astype(BF16)
    picked = jnp.dot(ct_ref[...], zone_hot, preferred_element_type=F32).astype(BF16)
    table = table_ref[...]
    masks = [table == t for t in range(tables)]
    qwt = qwt_ref[...]
    scale = jnp.broadcast_to(qwt[:, 0:1], (basis, block))
    for t in range(1, tables):
        scale = jnp.where(masks[t], qwt[:, t : t + 1], scale)
    scale = scale * vol_ref[...]
    bold = bold_ref[...]
    bnewt = bnewt_ref[...]
    for f in range(fields):
        every = jnp.dot(bold, picked[f * basis : (f + 1) * basis, :], preferred_element_type=F32)
        values = every[0:basis]
        for t in range(1, tables):
            values = jnp.where(masks[t], every[t * basis : (t + 1) * basis], values)
        weighted = (scale * values).astype(BF16)
        every = jnp.dot(bnewt, weighted, preferred_element_type=F32)
        moment = every[0:basis]
        for t in range(1, tables):
            moment = jnp.where(masks[t], every[t * basis : (t + 1) * basis], moment)
        mom_ref[f * basis : (f + 1) * basis, :] = moment
    moments = mom_ref[...]
    high = moments.astype(BF16)
    low = (moments - high.astype(F32)).astype(BF16)
    dest = dest_ref[...]
    nt = (((1,), (1,)), ((), ()))
    own_hot = (lax.broadcasted_iota(jnp.int32, (zones, block), 0) == dest).astype(BF16)
    own_ref[...] += lax.dot_general(high, own_hot, nt, preferred_element_type=F32) + lax.dot_general(
        low, own_hot, nt, preferred_element_type=F32
    )
    slot_hot = (lax.broadcasted_iota(jnp.int32, (slots_pad, block), 0) + zones == dest).astype(BF16)
    slot_ref[...] += lax.dot_general(slot_hot, high, nt, preferred_element_type=F32) + lax.dot_general(
        slot_hot, low, nt, preferred_element_type=F32
    )


def tet_partials(coeff_t, bold, bnewt, qwt, zone, table, vol, dest, slots_pad, block):
    tet_count = zone.shape[0]
    width, zones = coeff_t.shape
    tables = qwt.shape[1]
    basis = bold.shape[1]
    fields = width // basis
    kernel = functools.partial(
        tet_kernel, tables=tables, basis=basis, fields=fields, zones=zones, slots_pad=slots_pad
    )
    row_spec = pl.BlockSpec((1, block), lambda i: (0, i))
    whole = lambda shape: pl.BlockSpec(shape, lambda i: (0, 0))
    return pl.pallas_call(
        kernel,
        grid=(tet_count // block,),
        in_specs=[
            row_spec,
            row_spec,
            row_spec,
            row_spec,
            whole(coeff_t.shape),
            whole(bold.shape),
            whole(bnewt.shape),
            whole(qwt.shape),
        ],
        out_specs=[whole((width, zones)), whole((slots_pad, width))],
        out_shape=[
            jax.ShapeDtypeStruct((width, zones), F32),
            jax.ShapeDtypeStruct((slots_pad, width), F32),
        ],
        scratch_shapes=[pltpu.VMEM((width, block), F32)],
        compiler_params=pltpu.CompilerParams(dimension_semantics=("arbitrary",)),
    )(
        zone.reshape(1, tet_count),
        table.reshape(1, tet_count),
        vol.reshape(1, tet_count),
        dest.reshape(1, tet_count),
        coeff_t,
        bold,
        bnewt,
        qwt,
    )


def finish_kernel(own_ref, recv_ref, list_ref, inv_ref, out_ref, g_ref, h_ref, invt_ref, acc_ref, *, basis, fields):
    width, zones = own_ref.shape
    slots = recv_ref.shape[0]
    slot_hot = (lax.broadcasted_iota(jnp.int32, (zones, slots), 0) == list_ref[...]).astype(F32)
    arrived = jnp.dot(slot_hot, recv_ref[...].astype(F32), preferred_element_type=F32)
    rounded = (own_ref[...] + arrived.T).astype(BF16).astype(F32)
    lanes = 128
    halves = zones // lanes
    for half in range(halves):
        g_ref[half * width : (half + 1) * width, :] = rounded[:, half * lanes : (half + 1) * lanes]
    for k in range(basis):
        for half in range(halves):
            h_ref[k * fields : (k + 1) * fields, half * lanes : (half + 1) * lanes] = g_ref[
                pl.ds(half * width + k, fields, stride=basis), :
            ]
    chunk = 128
    for c in range(basis * basis // chunk):
        invt_ref[c * chunk : (c + 1) * chunk, :] = inv_ref[:, c * chunk : (c + 1) * chunk].astype(F32).T

    def body(j, carry):
        acc = jnp.zeros((fields, zones), F32)
        for k in range(basis):
            acc = acc + invt_ref[pl.ds(j * basis + k, 1), :] * h_ref[k * fields : (k + 1) * fields, :]
        acc_ref[pl.ds(pl.multiple_of(j * fields, fields), fields), :] = acc
        return carry

    lax.fori_loop(0, basis, body, 0)
    out_ref[...] = acc_ref[...].T


def finish(own_t, received, recv_row, inv_mass, basis, fields):
    width, zones = own_t.shape
    kernel = functools.partial(finish_kernel, basis=basis, fields=fields)
    return pl.pallas_call(
        kernel,
        out_shape=jax.ShapeDtypeStruct((zones, width), F32),
        scratch_shapes=[
            pltpu.VMEM((zones // 128 * width, 128), F32),
            pltpu.VMEM((width, zones), F32),
            pltpu.VMEM((basis * basis, zones), F32),
            pltpu.VMEM((width, zones), F32),
        ],
    )(own_t, received, recv_row, inv_mass)


def shifted(block, axis, distance):
    count = lax.axis_size(axis)
    route = [(i, (i + distance) % count) for i in range(count)]
    return lax.ppermute(block, axis, route)


def on_device(
    old_coeff,
    basis_old,
    basis_new,
    quad_weight,
    tet_zone,
    tet_table,
    tet_volume,
    tet_dest,
    recv_list,
    inv_mass,
):
    zone_count, row_width = old_coeff.shape
    tables, quad, basis = basis_old.shape
    fields = row_width // basis
    slot_total = recv_list.shape[1]
    partner_count = 10
    slot_cap = slot_total // partner_count
    slots_pad = -(-slot_total // 128) * 128
    block = min(512, tet_zone.shape[0])

    coeff_t = old_coeff.reshape(zone_count, basis, fields).transpose(2, 1, 0).reshape(row_width, zone_count)
    bold = basis_old.reshape(tables * quad, basis)
    bnewt = basis_new.transpose(0, 2, 1).reshape(tables * basis, quad)
    qwt = quad_weight.T
    own_t, slot_rows = tet_partials(
        coeff_t, bold, bnewt, qwt, tet_zone, tet_table, tet_volume, tet_dest, slots_pad, block
    )
    outgoing = slot_rows[:slot_total].astype(BF16).reshape(partner_count, slot_cap, row_width)

    lane_count = lax.axis_size("yz")
    face_side = 1 << (lane_count.bit_length() - 1) // 2
    going_up = jnp.concatenate([outgoing[0], outgoing[4], outgoing[7]], axis=0)
    going_down = jnp.concatenate([outgoing[1], outgoing[5], outgoing[6]], axis=0)
    from_left = shifted(going_up, "yz", 1).reshape(3, slot_cap, row_width)
    from_right = shifted(going_down, "yz", -1).reshape(3, slot_cap, row_width)
    from_back = shifted(outgoing[8], "gx", 1)
    from_front = shifted(outgoing[9], "gx", -1)
    upward = jnp.concatenate([outgoing[2], from_left[1], from_right[2]], axis=0)
    downward = jnp.concatenate([outgoing[3], from_left[2], from_right[1]], axis=0)
    came_up = shifted(upward, "yz", face_side).reshape(3, slot_cap, row_width)
    came_down = shifted(downward, "yz", -face_side).reshape(3, slot_cap, row_width)
    received = jnp.concatenate(
        [
            from_left[0],
            from_right[0],
            came_up[0],
            came_down[0],
            came_up[1],
            came_down[2],
            came_up[2],
            came_down[1],
            from_back,
            from_front,
        ],
        axis=0,
    )
    return finish(own_t, received, recv_list, inv_mass, basis, fields)


def solution(mesh):
    placed = (
        P(("gx", "yz"), None),
        P(),
        P(),
        P(),
        P(("gx", "yz")),
        P(("gx", "yz")),
        P(("gx", "yz")),
        P(("gx", "yz")),
        P(("gx", "yz"), None),
        P(("gx", "yz"), None),
    )
    return jax.shard_map(
        on_device, mesh=mesh, in_specs=placed, out_specs=P(("gx", "yz"), None), check_vma=False
    )
```

time: 89.6 us -> 65.1 us (0.73)
  the two profiles are of different devices: /device:TPU:7 before, /device:TPU:56 now
where the time goes in v2:
time: 65.1 us; the launch traced here: 64.7 us
  Pallas kernels  29.3 us (45%)
  starting transfers between devices  21.7 us (33%)
  waiting for transfers between devices  6.86 us (11%)
  local copies, waits for them, and re-layouts  5.58 us (9%)
  other arithmetic  1.09 us (2%)
    ppermute x6, starting transfers between devices, shifted(): return lax.ppermute(block, axis, route)  21.7 us
    pallas_call x1, Pallas kernels, tet_partials(): pl.pallas_call(kernel, grid=(tet_count // block,), in_specs=[row_spec, ro...  18.7 us
    pallas_call x1, Pallas kernels, finish(): pl.pallas_call(kernel, out_shape=jax.ShapeDtypeStruct((zones, width), F32...  10.6 us
    ppermute x6, waiting for transfers between devices, shifted(): return lax.ppermute(block, axis, route)  6.86 us
    unnamed x11, local copies, waits for them, and re-layouts  3.14 us
    transpose x1, local copies, waits for them, and re-layouts, on_device(): bnewt = basis_new.transpose(0, 2, 1).reshape(tables * basis, quad)  1.67 us
  transfers between devices with their start and end apart: 6, of which 4 were waited for; matrix products, arithmetic and copies ran while one was open for 0% of the time, Pallas kernels for 0%

profile of v2, /device:TPU:56, one launch (start us, length us, event | category | flops | bytes accessed | tf_op | source)
XLA Modules:
  0.0 64.7 jit_solution(8588654716129354650)
XLA Ops:
  0.0 1.4 %copy.17 = f32[8,64]{0,1:T(8,128)} copy(f32[8,64]{1,0:T(8,128)} %param.13) | data formatting | bytes 4096 | tf_op args[3]
  1.4 1.7 %copy.16 = bf16[8,64,64]{2,1,0:T(8,128)(2,1)} copy(bf16[8,64,64]{1,2,0:T(8,128)(2,1)} %bitcast.16) | data formatting | bytes 131072 | tf_op jit(solution)/shard_map/transpose | solution.py:181
  3.1 1.1 %copy.14 = bf16[256,512]{0,1:T(8,128)(2,1)S(1)} copy(bf16[256,512]{1,0:T(8,128)(2,1)} %param.10) | data formatting | bytes 524288 | tf_op args[0]
  4.1 0.7 %copy.15 = bf16[8,64,256]{2,1,0:T(8,128)(2,1)} copy(bf16[8,64,256]{2,0,1:T(8,128)(2,1)S(1)} %bitcast.13) | data formatting | bytes 524288 | tf_op jit(solution)/shard_map/transpose | solution.py:179
  4.9 18.7 %shard_map.100 = (f32[512,256]{1,0:T(8,128)}, f32[256,512]{1,0:T(8,128)}) custom-call(s32[1,2048]{1,0:T(1,128)} %bitcast.18, s32[1,2048]{1,0:T(1,128)} %bitcast.19, f32[1,2048]{1,0:T(1,128)} %bitcast.20, s32[1,2048]{1,0:T(1,128)} %bitcast.21, bf16[512,256]{1,0:T(8,128)(2,1)} %bitcast.12, bf16[512,64]{1,0:T(8,128)(2,1)} %bitcast.17, ...), custom_call_target="tpu_custom_call" | custom-call | tf_op jit(solution)/shard_map/pallas_call | solution.py:75
  23.6 1.1 %convert.3 = bf16[256,512]{1,0:T(8,128)(2,1)S(1)} convert(f32[256,512]{1,0:T(8,128)} %get-tuple-element.8) | non-fusion elementwise | flops 131072 | bytes 786432 | tf_op jit(solution)/shard_map/convert
  24.7 2.2 %collective-permute-start.5 = (bf16[16,512]{1,0:T(8,128)(2,1)S(1)}, bf16[16,512]{1,0:T(8,128)(2,1)S(1)}, u32[]{:S(2)}, u32[]{:S(2)}) collective-permute-start(bf16[16,512]{1,0:T(8,128)(2,1)S(1)} %get-tuple-element.9), channel_id=1, source_target_pairs={{0,448},{64,0},{128,64},{192,128},{256,192},{320,256},{384,320},{4... | collective-permute-start | bytes 49160 | tf_op jit(solution)/shard_map/ppermute | solution.py:155
  26.9 0.0 collective-permute-start.4
  26.9 4.3 %collective-permute-start = (bf16[48,512]{1,0:T(8,128)(2,1)S(1)}, bf16[48,512]{1,0:T(8,128)(2,1)S(1)}, u32[]{:S(2)}, u32[]{:S(2)}) collective-permute-start(bf16[48,512]{1,0:T(8,128)(2,1)S(1)} %pad_maximum_fusion), channel_id=1, source_target_pairs={{0,1},{1,2},{2,3},{3,4},{4,5},{5,6},{6,7},{7,8},{8,9},{9,10},{10,1... | collective-permute-start | bytes 147464 | tf_op jit(solution)/shard_map/ppermute | solution.py:155
  31.3 9.4 %collective-permute-start.1 = (bf16[48,512]{1,0:T(8,128)(2,1)S(1)}, bf16[48,512]{1,0:T(8,128)(2,1)S(1)}, u32[]{:S(2)}, u32[]{:S(2)}) collective-permute-start(bf16[48,512]{1,0:T(8,128)(2,1)S(1)} %pad_maximum_fusion.1), channel_id=1, source_target_pairs={{0,63},{1,0},{2,1},{3,2},{4,3},{5,4},{6,5},{7,6},{8,7},{9,8},{10,9... | collective-permute-start | bytes 147464 | tf_op jit(solution)/shard_map/ppermute | solution.py:155
  40.6 0.1 collective-permute-done
  40.8 1.6 %collective-permute-done.1 = bf16[48,512]{1,0:T(8,128)(2,1)S(1)} collective-permute-done((bf16[48,512]{1,0:T(8,128)(2,1)S(1)}, bf16[48,512]{1,0:T(8,128)(2,1)S(1)}, u32[]{:S(2)}, u32[]{:S(2)}) %collective-permute-start.1) | collective-permute-done | bytes 49184 | tf_op jit(solution)/shard_map/ppermute | solution.py:155
  42.4 3.8 %collective-permute-start.2 = (bf16[48,512]{1,0:T(8,128)(2,1)S(1)}, bf16[48,512]{1,0:T(8,128)(2,1)S(1)}, u32[]{:S(2)}, u32[]{:S(2)}) collective-permute-start(bf16[48,512]{1,0:T(8,128)(2,1)S(1)} %pad_maximum_fusion.2), channel_id=1, source_target_pairs={{0,8},{1,9},{2,10},{3,11},{4,12},{5,13},{6,14},{7,15},{8,16},{9,17... | collective-permute-start | bytes 147464 | tf_op jit(solution)/shard_map/ppermute | solution.py:155
  46.2 2.1 %collective-permute-start.3 = (bf16[48,512]{1,0:T(8,128)(2,1)S(1)}, bf16[48,512]{1,0:T(8,128)(2,1)S(1)}, u32[]{:S(2)}, u32[]{:S(2)}) collective-permute-start(bf16[48,512]{1,0:T(8,128)(2,1)S(1)} %pad_maximum_fusion.3), channel_id=1, source_target_pairs={{0,56},{1,57},{2,58},{3,59},{4,60},{5,61},{6,62},{7,63},{8,0},{9,1... | collective-permute-start | bytes 147464 | tf_op jit(solution)/shard_map/ppermute | solution.py:155
  48.3 0.1 collective-permute-done.2
  48.4 5.0 %collective-permute-done.3 = bf16[48,512]{1,0:T(8,128)(2,1)S(1)} collective-permute-done((bf16[48,512]{1,0:T(8,128)(2,1)S(1)}, bf16[48,512]{1,0:T(8,128)(2,1)S(1)}, u32[]{:S(2)}, u32[]{:S(2)}) %collective-permute-start.3) | collective-permute-done | bytes 49184 | tf_op jit(solution)/shard_map/ppermute | solution.py:155
  53.4 0.0 collective-permute-done.4
  53.5 0.0 collective-permute-done.5
  53.5 0.0 copy-start
  53.5 0.6 %copy-done = bf16[160,512]{1,0:T(8,128)(2,1)} copy-done((bf16[160,512]{1,0:T(8,128)(2,1)}, bf16[160,512]{1,0:T(8,128)(2,1)S(1)}, u32[]{:S(2)}) %copy-start) | copy-done | bytes 163864
  54.1 10.6 %shard_map.101 = f32[256,512]{1,0:T(8,128)} custom-call(f32[512,256]{1,0:T(8,128)} %get-tuple-element.7.own_ref, bf16[160,512]{1,0:T(8,128)(2,1)} %copy-done, s32[1,160]{1,0:T(1,128)} %list_ref.1, bf16[256,4096]{1,0:T(8,128)(2,1)} %inv_ref.1), custom_call_target="tpu_custom_call" | custom-call | tf_op jit(solution)/shard_map/pallas_call | solution.py:140
  (16 shorter events, 0.1 us)
Async XLA Ops:
  24.7 28.7 %collective-permute-start.5 = (bf16[16,512]{1,0:T(8,128)(2,1)S(1)}, bf16[16,512]{1,0:T(8,128)(2,1)S(1)}, u32[]{:S(2)}, u32[]{:S(2)}) collective-permute-start(bf16[16,512]{1,0:T(8,128)(2,1)S(1)} %get-tuple-element.9), channel_id=1, source_target_pairs={{0,448},{64,0},{128,64},{192,128},{256,192},{320,256},{384,320},{4... | collective-permute-start | bytes 49160 | tf_op jit(solution)/shard_map/ppermute | solution.py:155
  26.9 26.5 %collective-permute-start.4 = (bf16[16,512]{1,0:T(8,128)(2,1)S(1)}, bf16[16,512]{1,0:T(8,128)(2,1)S(1)}, u32[]{:S(2)}, u32[]{:S(2)}) collective-permute-start(bf16[16,512]{1,0:T(8,128)(2,1)S(1)} %get-tuple-element.10), channel_id=1, source_target_pairs={{0,64},{64,128},{128,192},{192,256},{256,320},{320,384},{384,448},... | collective-permute-start | bytes 49160 | tf_op jit(solution)/shard_map/ppermute | solution.py:155
  26.9 13.8 %collective-permute-start = (bf16[48,512]{1,0:T(8,128)(2,1)S(1)}, bf16[48,512]{1,0:T(8,128)(2,1)S(1)}, u32[]{:S(2)}, u32[]{:S(2)}) collective-permute-start(bf16[48,512]{1,0:T(8,128)(2,1)S(1)} %pad_maximum_fusion), channel_id=1, source_target_pairs={{0,1},{1,2},{2,3},{3,4},{4,5},{5,6},{6,7},{7,8},{8,9},{9,10},{10,1... | collective-permute-start | bytes 147464 | tf_op jit(solution)/shard_map/ppermute | solution.py:155
  31.3 11.1 %collective-permute-start.1 = (bf16[48,512]{1,0:T(8,128)(2,1)S(1)}, bf16[48,512]{1,0:T(8,128)(2,1)S(1)}, u32[]{:S(2)}, u32[]{:S(2)}) collective-permute-start(bf16[48,512]{1,0:T(8,128)(2,1)S(1)} %pad_maximum_fusion.1), channel_id=1, source_target_pairs={{0,63},{1,0},{2,1},{3,2},{4,3},{5,4},{6,5},{7,6},{8,7},{9,8},{10,9... | collective-permute-start | bytes 147464 | tf_op jit(solution)/shard_map/ppermute | solution.py:155
  42.4 6.0 %collective-permute-start.2 = (bf16[48,512]{1,0:T(8,128)(2,1)S(1)}, bf16[48,512]{1,0:T(8,128)(2,1)S(1)}, u32[]{:S(2)}, u32[]{:S(2)}) collective-permute-start(bf16[48,512]{1,0:T(8,128)(2,1)S(1)} %pad_maximum_fusion.2), channel_id=1, source_target_pairs={{0,8},{1,9},{2,10},{3,11},{4,12},{5,13},{6,14},{7,15},{8,16},{9,17... | collective-permute-start | bytes 147464 | tf_op jit(solution)/shard_map/ppermute | solution.py:155
  46.2 7.2 %collective-permute-start.3 = (bf16[48,512]{1,0:T(8,128)(2,1)S(1)}, bf16[48,512]{1,0:T(8,128)(2,1)S(1)}, u32[]{:S(2)}, u32[]{:S(2)}) collective-permute-start(bf16[48,512]{1,0:T(8,128)(2,1)S(1)} %pad_maximum_fusion.3), channel_id=1, source_target_pairs={{0,56},{1,57},{2,58},{3,59},{4,60},{5,61},{6,62},{7,63},{8,0},{9,1... | collective-permute-start | bytes 147464 | tf_op jit(solution)/shard_map/ppermute | solution.py:155
  53.5 0.7 %copy-start = (bf16[160,512]{1,0:T(8,128)(2,1)}, bf16[160,512]{1,0:T(8,128)(2,1)S(1)}, u32[]{:S(2)}) copy-start(bf16[160,512]{1,0:T(8,128)(2,1)S(1)} %constant_dynamic-update-slice_fusion.recv_ref) | copy-start | bytes 491524

commit v3 on v2

--- a/solution.py
+++ b/solution.py
@@ -12,15 +12,39 @@
 
 
 def tet_kernel(
-    zone_ref, table_ref, vol_ref, dest_ref, ct_ref, bold_ref, bnewt_ref, qwt_ref, own_ref, slot_ref, mom_ref,
+    zone_ref, table_ref, vol_ref, dest_ref, coeff_ref, bold_ref, bnew_ref, qw_ref,
+    own_ref, slot_out_ref, ct_ref, bnewt_ref, qwt_ref, slot_ref, mom_ref,
     *, tables, basis, fields, zones, slots_pad
 ):
     step = pl.program_id(0)
+    nt = (((1,), (1,)), ((), ()))
+    width = basis * fields
 
     @pl.when(step == 0)
     def _():
         own_ref[...] = jnp.zeros_like(own_ref)
         slot_ref[...] = jnp.zeros_like(slot_ref)
+        row = lax.broadcasted_iota(jnp.int32, (width, width), 0)
+        col = lax.broadcasted_iota(jnp.int32, (width, width), 1)
+        shuffle = (col == (row % basis) * fields + row // basis).astype(BF16)
+        ct_ref[...] = lax.dot_general(shuffle, coeff_ref[...], nt, preferred_element_type=F32).astype(BF16)
+        eye = (
+            lax.broadcasted_iota(jnp.int32, (basis, basis), 0) == lax.broadcasted_iota(jnp.int32, (basis, basis), 1)
+        ).astype(BF16)
+        for t in range(tables):
+            piece = bnew_ref[t * basis : (t + 1) * basis, :]
+            bnewt_ref[t * basis : (t + 1) * basis, :] = lax.dot_general(
+                eye, piece, nt, preferred_element_type=F32
+            ).astype(BF16)
+        weights = qw_ref[...]
+        high = weights.astype(BF16)
+        rest = weights - high.astype(F32)
+        mid = rest.astype(BF16)
+        low = (rest - mid.astype(F32)).astype(BF16)
+        qwt_ref[...] = (
+            lax.dot_general(eye, high, nt, preferred_element_type=F32)
+            + lax.dot_general(eye, mid, nt, preferred_element_type=F32)
+        ) + lax.dot_general(eye, low, nt, preferred_element_type=F32)
 
     block = zone_ref.shape[1]
     zone = zone_ref[...]
@@ -50,7 +74,6 @@
     high = moments.astype(BF16)
     low = (moments - high.astype(F32)).astype(BF16)
     dest = dest_ref[...]
-    nt = (((1,), (1,)), ((), ()))
     own_hot = (lax.broadcasted_iota(jnp.int32, (zones, block), 0) == dest).astype(BF16)
     own_ref[...] += lax.dot_general(high, own_hot, nt, preferred_element_type=F32) + lax.dot_general(
         low, own_hot, nt, preferred_element_type=F32
@@ -60,11 +83,15 @@
         slot_hot, low, nt, preferred_element_type=F32
     )
 
-
-def tet_partials(coeff_t, bold, bnewt, qwt, zone, table, vol, dest, slots_pad, block):
+    @pl.when(step == pl.num_programs(0) - 1)
+    def _():
+        slot_out_ref[...] = slot_ref[...].astype(BF16)
+
+
+def tet_partials(old_coeff, bold, bnew, quad_weight, zone, table, vol, dest, slots_pad, block):
     tet_count = zone.shape[0]
-    width, zones = coeff_t.shape
-    tables = qwt.shape[1]
+    zones, width = old_coeff.shape
+    tables = quad_weight.shape[0]
     basis = bold.shape[1]
     fields = width // basis
     kernel = functools.partial(
@@ -80,27 +107,33 @@
             row_spec,
             row_spec,
             row_spec,
-            whole(coeff_t.shape),
+            whole(old_coeff.shape),
             whole(bold.shape),
-            whole(bnewt.shape),
-            whole(qwt.shape),
+            whole(bnew.shape),
+            whole(quad_weight.shape),
         ],
         out_specs=[whole((width, zones)), whole((slots_pad, width))],
         out_shape=[
             jax.ShapeDtypeStruct((width, zones), F32),
-            jax.ShapeDtypeStruct((slots_pad, width), F32),
-        ],
-        scratch_shapes=[pltpu.VMEM((width, block), F32)],
+            jax.ShapeDtypeStruct((slots_pad, width), BF16),
+        ],
+        scratch_shapes=[
+            pltpu.VMEM((width, zones), BF16),
+            pltpu.VMEM(bnew.shape, BF16),
+            pltpu.VMEM((basis, tables), F32),
+            pltpu.VMEM((slots_pad, width), F32),
+            pltpu.VMEM((width, block), F32),
+        ],
         compiler_params=pltpu.CompilerParams(dimension_semantics=("arbitrary",)),
     )(
         zone.reshape(1, tet_count),
         table.reshape(1, tet_count),
         vol.reshape(1, tet_count),
         dest.reshape(1, tet_count),
-        coeff_t,
+        old_coeff,
         bold,
-        bnewt,
-        qwt,
+        bnew,
+        quad_weight,
     )
 
 
@@ -176,14 +209,12 @@
     slots_pad = -(-slot_total // 128) * 128
     block = min(512, tet_zone.shape[0])
 
-    coeff_t = old_coeff.reshape(zone_count, basis, fields).transpose(2, 1, 0).reshape(row_width, zone_count)
     bold = basis_old.reshape(tables * quad, basis)
-    bnewt = basis_new.transpose(0, 2, 1).reshape(tables * basis, quad)
-    qwt = quad_weight.T
+    bnew = basis_new.reshape(tables * quad, basis)
     own_t, slot_rows = tet_partials(
-        coeff_t, bold, bnewt, qwt, tet_zone, tet_table, tet_volume, tet_dest, slots_pad, block
-    )
-    outgoing = slot_rows[:slot_total].astype(BF16).reshape(partner_count, slot_cap, row_width)
+        old_coeff, bold, bnew, quad_weight, tet_zone, tet_table, tet_volume, tet_dest, slots_pad, block
+    )
+    outgoing = slot_rows[:slot_total].reshape(partner_count, slot_cap, row_width)
 
     lane_count = lax.axis_size("yz")
     face_side = 1 << (lane_count.bit_length() - 1) // 2

time: 65.1 us -> 60.9 us (0.935)
  local copies, waits for them, and re-layouts: 5.58 us -> 2.3 us
  other arithmetic: 1.09 us -> 0.02 us
    unnamed x11 -> x9, local copies, waits for them, and re-layouts: 3.14 us -> 0.67 us
    transpose x2 -> x0, local copies, waits for them, and re-layouts: 2.41 us -> none  [the longest x1 1.67 us: on_device(): bnewt = basis_new.transpose(0, 2, 1).reshape(tables * basis, quad)]
    another operation x1 -> x0, other arithmetic: 1.07 us -> none
    slice x1, local copies, waits for them, and re-layouts: 0.01 us -> 0.85 us  [on_device(): from_front = shifted(outgoing[9], 'gx', -1)]
    slice x1, local copies, waits for them, and re-layouts: 0.01 us -> 0.76 us  [on_device(): outgoing[5]]
  transfers between devices with their start and end apart: 6 -> 6, of which waited for: 4 -> 3; matrix products, arithmetic and copies ran while one was open for 0% -> 1% of each run, Pallas kernels for 0% -> 0%
where the time goes in v3:
time: 60.9 us; the launch traced here: 60.5 us
  Pallas kernels  29.6 us (49%)
  starting transfers between devices  21.7 us (36%)
  waiting for transfers between devices  6.85 us (11%)
  local copies, waits for them, and re-layouts  2.3 us (4%)
    ppermute x6, starting transfers between devices, shifted(): return lax.ppermute(block, axis, route)  21.7 us
    pallas_call x1, Pallas kernels, tet_partials(): pl.pallas_call(kernel, grid=(tet_count // block,), in_specs=[row_spec, ro...  19 us
    pallas_call x1, Pallas kernels, finish(): pl.pallas_call(kernel, out_shape=jax.ShapeDtypeStruct((zones, width), F32...  10.6 us
    ppermute x6, waiting for transfers between devices, shifted(): return lax.ppermute(block, axis, route)  6.85 us
  transfers between devices with their start and end apart: 6, of which 3 were waited for; matrix products, arithmetic and copies ran while one was open for 1% of the time, Pallas kernels for 0%

profile of v3, /device:TPU:56, one launch (start us, length us, event | category | flops | bytes accessed | tf_op | source)
XLA Modules:
  0.0 60.5 jit_solution(7774987541170059097)
XLA Ops:
  0.0 19.0 %shard_map.100 = (f32[512,256]{1,0:T(8,128)}, bf16[256,512]{1,0:T(8,128)(2,1)}) custom-call(s32[1,2048]{1,0:T(1,128)} %bitcast.8, s32[1,2048]{1,0:T(1,128)} %bitcast.9, f32[1,2048]{1,0:T(1,128)} %bitcast.10, s32[1,2048]{1,0:T(1,128)} %bitcast.11, bf16[256,512]{1,0:T(8,128)(2,1)} %coeff_ref.1, bf16[512,64]{1,0:T(8,128)(2,1)} %bitcast.6, ...), custom_call_target="tpu_custom_call" | custom-call | tf_op jit(solution)/shard_map/pallas_call | solution.py:102
  19.0 0.8 %fusion = (bf16[16,512]{1,0:T(8,128)(2,1)S(1)}, bf16[16,512]{1,0:T(8,128)(2,1)S(1)}, bf16[16,512]{1,0:T(8,128)(2,1)S(1)}, bf16[16,512]{1,0:T(8,128)(2,1)S(1)}, b...) fusion(bf16[256,512]{1,0:T(8,128)(2,1)} %get-tuple-element.8), kind=kLoop, calls=%fused_computation.14 | loop fusion | bytes 262144 | tf_op jit(solution)/shard_map/slice | solution.py:226
  19.8 2.2 %collective-permute-start.5 = (bf16[16,512]{1,0:T(8,128)(2,1)S(1)}, bf16[16,512]{1,0:T(8,128)(2,1)S(1)}, u32[]{:S(2)}, u32[]{:S(2)}) collective-permute-start(bf16[16,512]{1,0:T(8,128)(2,1)S(1)} %get-tuple-element.9), channel_id=1, source_target_pairs={{0,448},{64,0},{128,64},{192,128},{256,192},{320,256},{384,320},{4... | collective-permute-start | bytes 49160 | tf_op jit(solution)/shard_map/ppermute | solution.py:188
  22.0 0.0 collective-permute-start.4
  22.0 4.3 %collective-permute-start = (bf16[48,512]{1,0:T(8,128)(2,1)S(1)}, bf16[48,512]{1,0:T(8,128)(2,1)S(1)}, u32[]{:S(2)}, u32[]{:S(2)}) collective-permute-start(bf16[48,512]{1,0:T(8,128)(2,1)S(1)} %pad_maximum_fusion), channel_id=1, source_target_pairs={{0,1},{1,2},{2,3},{3,4},{4,5},{5,6},{6,7},{7,8},{8,9},{9,10},{10,1... | collective-permute-start | bytes 147464 | tf_op jit(solution)/shard_map/ppermute | solution.py:188
  26.3 0.8 %slice.103 = bf16[32,512]{1,0:T(8,128)(2,1)S(1)} slice(bf16[256,512]{1,0:T(8,128)(2,1)} %get-tuple-element.8), slice={[80:112], [0:512]} | slice | bytes 65536 | tf_op jit(solution)/shard_map/slice | solution.py:222
  27.1 9.4 %collective-permute-start.1 = (bf16[48,512]{1,0:T(8,128)(2,1)S(1)}, bf16[48,512]{1,0:T(8,128)(2,1)S(1)}, u32[]{:S(2)}, u32[]{:S(2)}) collective-permute-start(bf16[48,512]{1,0:T(8,128)(2,1)S(1)} %pad_maximum_fusion.1), channel_id=1, source_target_pairs={{0,63},{1,0},{2,1},{3,2},{4,3},{5,4},{6,5},{7,6},{8,7},{9,8},{10,9... | collective-permute-start | bytes 147464 | tf_op jit(solution)/shard_map/ppermute | solution.py:188
  36.5 0.0 collective-permute-done
  36.5 1.7 %collective-permute-done.1 = bf16[48,512]{1,0:T(8,128)(2,1)S(1)} collective-permute-done((bf16[48,512]{1,0:T(8,128)(2,1)S(1)}, bf16[48,512]{1,0:T(8,128)(2,1)S(1)}, u32[]{:S(2)}, u32[]{:S(2)}) %collective-permute-start.1) | collective-permute-done | bytes 49184 | tf_op jit(solution)/shard_map/ppermute | solution.py:188
  38.2 3.8 %collective-permute-start.2 = (bf16[48,512]{1,0:T(8,128)(2,1)S(1)}, bf16[48,512]{1,0:T(8,128)(2,1)S(1)}, u32[]{:S(2)}, u32[]{:S(2)}) collective-permute-start(bf16[48,512]{1,0:T(8,128)(2,1)S(1)} %pad_maximum_fusion.2), channel_id=1, source_target_pairs={{0,8},{1,9},{2,10},{3,11},{4,12},{5,13},{6,14},{7,15},{8,16},{9,17... | collective-permute-start | bytes 147464 | tf_op jit(solution)/shard_map/ppermute | solution.py:188
  42.0 2.0 %collective-permute-start.3 = (bf16[48,512]{1,0:T(8,128)(2,1)S(1)}, bf16[48,512]{1,0:T(8,128)(2,1)S(1)}, u32[]{:S(2)}, u32[]{:S(2)}) collective-permute-start(bf16[48,512]{1,0:T(8,128)(2,1)S(1)} %pad_maximum_fusion.3), channel_id=1, source_target_pairs={{0,56},{1,57},{2,58},{3,59},{4,60},{5,61},{6,62},{7,63},{8,0},{9,1... | collective-permute-start | bytes 147464 | tf_op jit(solution)/shard_map/ppermute | solution.py:188
  44.1 0.1 collective-permute-done.2
  44.2 5.0 %collective-permute-done.3 = bf16[48,512]{1,0:T(8,128)(2,1)S(1)} collective-permute-done((bf16[48,512]{1,0:T(8,128)(2,1)S(1)}, bf16[48,512]{1,0:T(8,128)(2,1)S(1)}, u32[]{:S(2)}, u32[]{:S(2)}) %collective-permute-start.3) | collective-permute-done | bytes 49184 | tf_op jit(solution)/shard_map/ppermute | solution.py:188
  49.3 0.0 collective-permute-done.4
  49.3 0.0 collective-permute-done.5
  49.3 0.0 copy-start
  49.3 0.6 %copy-done = bf16[160,512]{1,0:T(8,128)(2,1)} copy-done((bf16[160,512]{1,0:T(8,128)(2,1)}, bf16[160,512]{1,0:T(8,128)(2,1)S(1)}, u32[]{:S(2)}) %copy-start) | copy-done | bytes 163864
  50.0 10.6 %shard_map.101 = f32[256,512]{1,0:T(8,128)} custom-call(f32[512,256]{1,0:T(8,128)} %get-tuple-element.7.own_ref, bf16[160,512]{1,0:T(8,128)(2,1)} %copy-done, s32[1,160]{1,0:T(1,128)} %list_ref.1, bf16[256,4096]{1,0:T(8,128)(2,1)} %inv_ref.1), custom_call_target="tpu_custom_call" | custom-call | tf_op jit(solution)/shard_map/pallas_call | solution.py:173
  (14 shorter events, 0.1 us)
Async XLA Ops:
  19.8 29.5 %collective-permute-start.5 = (bf16[16,512]{1,0:T(8,128)(2,1)S(1)}, bf16[16,512]{1,0:T(8,128)(2,1)S(1)}, u32[]{:S(2)}, u32[]{:S(2)}) collective-permute-start(bf16[16,512]{1,0:T(8,128)(2,1)S(1)} %get-tuple-element.9), channel_id=1, source_target_pairs={{0,448},{64,0},{128,64},{192,128},{256,192},{320,256},{384,320},{4... | collective-permute-start | bytes 49160 | tf_op jit(solution)/shard_map/ppermute | solution.py:188
  22.0 27.2 %collective-permute-start.4 = (bf16[16,512]{1,0:T(8,128)(2,1)S(1)}, bf16[16,512]{1,0:T(8,128)(2,1)S(1)}, u32[]{:S(2)}, u32[]{:S(2)}) collective-permute-start(bf16[16,512]{1,0:T(8,128)(2,1)S(1)} %get-tuple-element.10), channel_id=1, source_target_pairs={{0,64},{64,128},{128,192},{192,256},{256,320},{320,384},{384,448},... | collective-permute-start | bytes 49160 | tf_op jit(solution)/shard_map/ppermute | solution.py:188
  22.0 14.4 %collective-permute-start = (bf16[48,512]{1,0:T(8,128)(2,1)S(1)}, bf16[48,512]{1,0:T(8,128)(2,1)S(1)}, u32[]{:S(2)}, u32[]{:S(2)}) collective-permute-start(bf16[48,512]{1,0:T(8,128)(2,1)S(1)} %pad_maximum_fusion), channel_id=1, source_target_pairs={{0,1},{1,2},{2,3},{3,4},{4,5},{5,6},{6,7},{7,8},{8,9},{9,10},{10,1... | collective-permute-start | bytes 147464 | tf_op jit(solution)/shard_map/ppermute | solution.py:188
  27.1 11.1 %collective-permute-start.1 = (bf16[48,512]{1,0:T(8,128)(2,1)S(1)}, bf16[48,512]{1,0:T(8,128)(2,1)S(1)}, u32[]{:S(2)}, u32[]{:S(2)}) collective-permute-start(bf16[48,512]{1,0:T(8,128)(2,1)S(1)} %pad_maximum_fusion.1), channel_id=1, source_target_pairs={{0,63},{1,0},{2,1},{3,2},{4,3},{5,4},{6,5},{7,6},{8,7},{9,8},{10,9... | collective-permute-start | bytes 147464 | tf_op jit(solution)/shard_map/ppermute | solution.py:188
  38.2 6.0 %collective-permute-start.2 = (bf16[48,512]{1,0:T(8,128)(2,1)S(1)}, bf16[48,512]{1,0:T(8,128)(2,1)S(1)}, u32[]{:S(2)}, u32[]{:S(2)}) collective-permute-start(bf16[48,512]{1,0:T(8,128)(2,1)S(1)} %pad_maximum_fusion.2), channel_id=1, source_target_pairs={{0,8},{1,9},{2,10},{3,11},{4,12},{5,13},{6,14},{7,15},{8,16},{9,17... | collective-permute-start | bytes 147464 | tf_op jit(solution)/shard_map/ppermute | solution.py:188
  42.0 7.2 %collective-permute-start.3 = (bf16[48,512]{1,0:T(8,128)(2,1)S(1)}, bf16[48,512]{1,0:T(8,128)(2,1)S(1)}, u32[]{:S(2)}, u32[]{:S(2)}) collective-permute-start(bf16[48,512]{1,0:T(8,128)(2,1)S(1)} %pad_maximum_fusion.3), channel_id=1, source_target_pairs={{0,56},{1,57},{2,58},{3,59},{4,60},{5,61},{6,62},{7,63},{8,0},{9,1... | collective-permute-start | bytes 147464 | tf_op jit(solution)/shard_map/ppermute | solution.py:188
  49.3 0.7 %copy-start = (bf16[160,512]{1,0:T(8,128)(2,1)}, bf16[160,512]{1,0:T(8,128)(2,1)S(1)}, u32[]{:S(2)}) copy-start(bf16[160,512]{1,0:T(8,128)(2,1)S(1)} %constant_dynamic-update-slice_fusion.recv_ref) | copy-start | bytes 491524

commit v4 on v3

--- a/solution.py
+++ b/solution.py
@@ -13,7 +13,7 @@
 
 def tet_kernel(
     zone_ref, table_ref, vol_ref, dest_ref, coeff_ref, bold_ref, bnew_ref, qw_ref,
-    own_ref, slot_out_ref, ct_ref, bnewt_ref, qwt_ref, slot_ref, mom_ref,
+    own_ref, slot_out_ref, ct_ref, boldc_ref, bnewc_ref, qwt_ref, slot_ref, mom_ref, spread_ref,
     *, tables, basis, fields, zones, slots_pad
 ):
     step = pl.program_id(0)
@@ -32,8 +32,9 @@
             lax.broadcasted_iota(jnp.int32, (basis, basis), 0) == lax.broadcasted_iota(jnp.int32, (basis, basis), 1)
         ).astype(BF16)
         for t in range(tables):
+            boldc_ref[:, t * basis : (t + 1) * basis] = bold_ref[t * basis : (t + 1) * basis, :]
             piece = bnew_ref[t * basis : (t + 1) * basis, :]
-            bnewt_ref[t * basis : (t + 1) * basis, :] = lax.dot_general(
+            bnewc_ref[:, t * basis : (t + 1) * basis] = lax.dot_general(
                 eye, piece, nt, preferred_element_type=F32
             ).astype(BF16)
         weights = qw_ref[...]
@@ -57,19 +58,18 @@
     for t in range(1, tables):
         scale = jnp.where(masks[t], qwt[:, t : t + 1], scale)
     scale = scale * vol_ref[...]
-    bold = bold_ref[...]
-    bnewt = bnewt_ref[...]
+    boldc = boldc_ref[...]
+    bnewc = bnewc_ref[...]
+    empty = jnp.zeros((basis, block), BF16)
     for f in range(fields):
-        every = jnp.dot(bold, picked[f * basis : (f + 1) * basis, :], preferred_element_type=F32)
-        values = every[0:basis]
-        for t in range(1, tables):
-            values = jnp.where(masks[t], every[t * basis : (t + 1) * basis], values)
+        piece = picked[f * basis : (f + 1) * basis, :]
+        for t in range(tables):
+            spread_ref[t * basis : (t + 1) * basis, :] = jnp.where(masks[t], piece, empty)
+        values = jnp.dot(boldc, spread_ref[...], preferred_element_type=F32)
         weighted = (scale * values).astype(BF16)
-        every = jnp.dot(bnewt, weighted, preferred_element_type=F32)
-        moment = every[0:basis]
-        for t in range(1, tables):
-            moment = jnp.where(masks[t], every[t * basis : (t + 1) * basis], moment)
-        mom_ref[f * basis : (f + 1) * basis, :] = moment
+        for t in range(tables):
+            spread_ref[t * basis : (t + 1) * basis, :] = jnp.where(masks[t], weighted, empty)
+        mom_ref[f * basis : (f + 1) * basis, :] = jnp.dot(bnewc, spread_ref[...], preferred_element_type=F32)
     moments = mom_ref[...]
     high = moments.astype(BF16)
     low = (moments - high.astype(F32)).astype(BF16)
@@ -119,10 +119,12 @@
         ],
         scratch_shapes=[
             pltpu.VMEM((width, zones), BF16),
-            pltpu.VMEM(bnew.shape, BF16),
+            pltpu.VMEM((basis, tables * basis), BF16),
+            pltpu.VMEM((basis, tables * basis), BF16),
             pltpu.VMEM((basis, tables), F32),
             pltpu.VMEM((slots_pad, width), F32),
             pltpu.VMEM((width, block), F32),
+            pltpu.VMEM((tables * basis, block), BF16),
         ],
         compiler_params=pltpu.CompilerParams(dimension_semantics=("arbitrary",)),
     )(

time: 60.9 us -> 57.8 us (0.949)
  Pallas kernels: 29.6 us -> 26.4 us
    pallas_call x1, Pallas kernels: 19 us -> 15.8 us  [tet_partials(): pl.pallas_call(kernel, grid=(tet_count // block,), in_specs=[row_spec, ro...]
where the time goes in v4:
time: 57.8 us; the launch traced here: 57.4 us
  Pallas kernels  26.4 us (46%)
  starting transfers between devices  21.7 us (38%)
  waiting for transfers between devices  6.86 us (12%)
  local copies, waits for them, and re-layouts  2.3 us (4%)
    ppermute x6, starting transfers between devices, shifted(): return lax.ppermute(block, axis, route)  21.7 us
    pallas_call x1, Pallas kernels, tet_partials(): pl.pallas_call(kernel, grid=(tet_count // block,), in_specs=[row_spec, ro...  15.8 us
    pallas_call x1, Pallas kernels, finish(): pl.pallas_call(kernel, out_shape=jax.ShapeDtypeStruct((zones, width), F32...  10.6 us
    ppermute x6, waiting for transfers between devices, shifted(): return lax.ppermute(block, axis, route)  6.86 us
  transfers between devices with their start and end apart: 6, of which 3 were waited for; matrix products, arithmetic and copies ran while one was open for 1% of the time, Pallas kernels for 0%

profile of v4, /device:TPU:56, one launch (start us, length us, event | category | flops | bytes accessed | tf_op | source)
XLA Modules:
  0.0 57.4 jit_solution(425055069757293399)
XLA Ops:
  0.0 15.8 %shard_map.100 = (f32[512,256]{1,0:T(8,128)}, bf16[256,512]{1,0:T(8,128)(2,1)}) custom-call(s32[1,2048]{1,0:T(1,128)} %bitcast.8, s32[1,2048]{1,0:T(1,128)} %bitcast.9, f32[1,2048]{1,0:T(1,128)} %bitcast.10, s32[1,2048]{1,0:T(1,128)} %bitcast.11, bf16[256,512]{1,0:T(8,128)(2,1)} %coeff_ref.1, bf16[512,64]{1,0:T(8,128)(2,1)} %bitcast.6, ...), custom_call_target="tpu_custom_call" | custom-call | tf_op jit(solution)/shard_map/pallas_call | solution.py:102
  15.8 0.8 %fusion = (bf16[16,512]{1,0:T(8,128)(2,1)S(1)}, bf16[16,512]{1,0:T(8,128)(2,1)S(1)}, bf16[16,512]{1,0:T(8,128)(2,1)S(1)}, bf16[16,512]{1,0:T(8,128)(2,1)S(1)}, b...) fusion(bf16[256,512]{1,0:T(8,128)(2,1)} %get-tuple-element.8), kind=kLoop, calls=%fused_computation.14 | loop fusion | bytes 262144 | tf_op jit(solution)/shard_map/slice | solution.py:228
  16.7 2.2 %collective-permute-start.5 = (bf16[16,512]{1,0:T(8,128)(2,1)S(1)}, bf16[16,512]{1,0:T(8,128)(2,1)S(1)}, u32[]{:S(2)}, u32[]{:S(2)}) collective-permute-start(bf16[16,512]{1,0:T(8,128)(2,1)S(1)} %get-tuple-element.9), channel_id=1, source_target_pairs={{0,448},{64,0},{128,64},{192,128},{256,192},{320,256},{384,320},{4... | collective-permute-start | bytes 49160 | tf_op jit(solution)/shard_map/ppermute | solution.py:190
  18.9 0.0 collective-permute-start.4
  18.9 4.3 %collective-permute-start = (bf16[48,512]{1,0:T(8,128)(2,1)S(1)}, bf16[48,512]{1,0:T(8,128)(2,1)S(1)}, u32[]{:S(2)}, u32[]{:S(2)}) collective-permute-start(bf16[48,512]{1,0:T(8,128)(2,1)S(1)} %pad_maximum_fusion), channel_id=1, source_target_pairs={{0,1},{1,2},{2,3},{3,4},{4,5},{5,6},{6,7},{7,8},{8,9},{9,10},{10,1... | collective-permute-start | bytes 147464 | tf_op jit(solution)/shard_map/ppermute | solution.py:190
  23.2 0.8 %slice.103 = bf16[32,512]{1,0:T(8,128)(2,1)S(1)} slice(bf16[256,512]{1,0:T(8,128)(2,1)} %get-tuple-element.8), slice={[80:112], [0:512]} | slice | bytes 65536 | tf_op jit(solution)/shard_map/slice | solution.py:224
  23.9 9.4 %collective-permute-start.1 = (bf16[48,512]{1,0:T(8,128)(2,1)S(1)}, bf16[48,512]{1,0:T(8,128)(2,1)S(1)}, u32[]{:S(2)}, u32[]{:S(2)}) collective-permute-start(bf16[48,512]{1,0:T(8,128)(2,1)S(1)} %pad_maximum_fusion.1), channel_id=1, source_target_pairs={{0,63},{1,0},{2,1},{3,2},{4,3},{5,4},{6,5},{7,6},{8,7},{9,8},{10,9... | collective-permute-start | bytes 147464 | tf_op jit(solution)/shard_map/ppermute | solution.py:190
  33.3 0.0 collective-permute-done
  33.3 1.7 %collective-permute-done.1 = bf16[48,512]{1,0:T(8,128)(2,1)S(1)} collective-permute-done((bf16[48,512]{1,0:T(8,128)(2,1)S(1)}, bf16[48,512]{1,0:T(8,128)(2,1)S(1)}, u32[]{:S(2)}, u32[]{:S(2)}) %collective-permute-start.1) | collective-permute-done | bytes 49184 | tf_op jit(solution)/shard_map/ppermute | solution.py:190
  35.0 3.8 %collective-permute-start.2 = (bf16[48,512]{1,0:T(8,128)(2,1)S(1)}, bf16[48,512]{1,0:T(8,128)(2,1)S(1)}, u32[]{:S(2)}, u32[]{:S(2)}) collective-permute-start(bf16[48,512]{1,0:T(8,128)(2,1)S(1)} %pad_maximum_fusion.2), channel_id=1, source_target_pairs={{0,8},{1,9},{2,10},{3,11},{4,12},{5,13},{6,14},{7,15},{8,16},{9,17... | collective-permute-start | bytes 147464 | tf_op jit(solution)/shard_map/ppermute | solution.py:190
  38.9 2.0 %collective-permute-start.3 = (bf16[48,512]{1,0:T(8,128)(2,1)S(1)}, bf16[48,512]{1,0:T(8,128)(2,1)S(1)}, u32[]{:S(2)}, u32[]{:S(2)}) collective-permute-start(bf16[48,512]{1,0:T(8,128)(2,1)S(1)} %pad_maximum_fusion.3), channel_id=1, source_target_pairs={{0,56},{1,57},{2,58},{3,59},{4,60},{5,61},{6,62},{7,63},{8,0},{9,1... | collective-permute-start | bytes 147464 | tf_op jit(solution)/shard_map/ppermute | solution.py:190
  40.9 0.1 collective-permute-done.2
  41.0 5.0 %collective-permute-done.3 = bf16[48,512]{1,0:T(8,128)(2,1)S(1)} collective-permute-done((bf16[48,512]{1,0:T(8,128)(2,1)S(1)}, bf16[48,512]{1,0:T(8,128)(2,1)S(1)}, u32[]{:S(2)}, u32[]{:S(2)}) %collective-permute-start.3) | collective-permute-done | bytes 49184 | tf_op jit(solution)/shard_map/ppermute | solution.py:190
  46.1 0.0 collective-permute-done.4
  46.1 0.0 collective-permute-done.5
  46.1 0.0 copy-start
  46.2 0.6 %copy-done = bf16[160,512]{1,0:T(8,128)(2,1)} copy-done((bf16[160,512]{1,0:T(8,128)(2,1)}, bf16[160,512]{1,0:T(8,128)(2,1)S(1)}, u32[]{:S(2)}) %copy-start) | copy-done | bytes 163864
  46.8 10.6 %shard_map.101 = f32[256,512]{1,0:T(8,128)} custom-call(f32[512,256]{1,0:T(8,128)} %get-tuple-element.7.own_ref, bf16[160,512]{1,0:T(8,128)(2,1)} %copy-done, s32[1,160]{1,0:T(1,128)} %list_ref.1, bf16[256,4096]{1,0:T(8,128)(2,1)} %inv_ref.1), custom_call_target="tpu_custom_call" | custom-call | tf_op jit(solution)/shard_map/pallas_call | solution.py:175
  (14 shorter events, 0.1 us)
Async XLA Ops:
  16.7 29.5 %collective-permute-start.5 = (bf16[16,512]{1,0:T(8,128)(2,1)S(1)}, bf16[16,512]{1,0:T(8,128)(2,1)S(1)}, u32[]{:S(2)}, u32[]{:S(2)}) collective-permute-start(bf16[16,512]{1,0:T(8,128)(2,1)S(1)} %get-tuple-element.9), channel_id=1, source_target_pairs={{0,448},{64,0},{128,64},{192,128},{256,192},{320,256},{384,320},{4... | collective-permute-start | bytes 49160 | tf_op jit(solution)/shard_map/ppermute | solution.py:190
  18.9 27.2 %collective-permute-start.4 = (bf16[16,512]{1,0:T(8,128)(2,1)S(1)}, bf16[16,512]{1,0:T(8,128)(2,1)S(1)}, u32[]{:S(2)}, u32[]{:S(2)}) collective-permute-start(bf16[16,512]{1,0:T(8,128)(2,1)S(1)} %get-tuple-element.10), channel_id=1, source_target_pairs={{0,64},{64,128},{128,192},{192,256},{256,320},{320,384},{384,448},... | collective-permute-start | bytes 49160 | tf_op jit(solution)/shard_map/ppermute | solution.py:190
  18.9 14.4 %collective-permute-start = (bf16[48,512]{1,0:T(8,128)(2,1)S(1)}, bf16[48,512]{1,0:T(8,128)(2,1)S(1)}, u32[]{:S(2)}, u32[]{:S(2)}) collective-permute-start(bf16[48,512]{1,0:T(8,128)(2,1)S(1)} %pad_maximum_fusion), channel_id=1, source_target_pairs={{0,1},{1,2},{2,3},{3,4},{4,5},{5,6},{6,7},{7,8},{8,9},{9,10},{10,1... | collective-permute-start | bytes 147464 | tf_op jit(solution)/shard_map/ppermute | solution.py:190
  23.9 11.1 %collective-permute-start.1 = (bf16[48,512]{1,0:T(8,128)(2,1)S(1)}, bf16[48,512]{1,0:T(8,128)(2,1)S(1)}, u32[]{:S(2)}, u32[]{:S(2)}) collective-permute-start(bf16[48,512]{1,0:T(8,128)(2,1)S(1)} %pad_maximum_fusion.1), channel_id=1, source_target_pairs={{0,63},{1,0},{2,1},{3,2},{4,3},{5,4},{6,5},{7,6},{8,7},{9,8},{10,9... | collective-permute-start | bytes 147464 | tf_op jit(solution)/shard_map/ppermute | solution.py:190
  35.0 6.0 %collective-permute-start.2 = (bf16[48,512]{1,0:T(8,128)(2,1)S(1)}, bf16[48,512]{1,0:T(8,128)(2,1)S(1)}, u32[]{:S(2)}, u32[]{:S(2)}) collective-permute-start(bf16[48,512]{1,0:T(8,128)(2,1)S(1)} %pad_maximum_fusion.2), channel_id=1, source_target_pairs={{0,8},{1,9},{2,10},{3,11},{4,12},{5,13},{6,14},{7,15},{8,16},{9,17... | collective-permute-start | bytes 147464 | tf_op jit(solution)/shard_map/ppermute | solution.py:190
  38.9 7.2 %collective-permute-start.3 = (bf16[48,512]{1,0:T(8,128)(2,1)S(1)}, bf16[48,512]{1,0:T(8,128)(2,1)S(1)}, u32[]{:S(2)}, u32[]{:S(2)}) collective-permute-start(bf16[48,512]{1,0:T(8,128)(2,1)S(1)} %pad_maximum_fusion.3), channel_id=1, source_target_pairs={{0,56},{1,57},{2,58},{3,59},{4,60},{5,61},{6,62},{7,63},{8,0},{9,1... | collective-permute-start | bytes 147464 | tf_op jit(solution)/shard_map/ppermute | solution.py:190
  46.1 0.7 %copy-start = (bf16[160,512]{1,0:T(8,128)(2,1)}, bf16[160,512]{1,0:T(8,128)(2,1)S(1)}, u32[]{:S(2)}) copy-start(bf16[160,512]{1,0:T(8,128)(2,1)S(1)} %constant_dynamic-update-slice_fusion.recv_ref) | copy-start | bytes 491524

commit v5 on v4

--- a/solution.py
+++ b/solution.py
@@ -158,11 +158,17 @@
     for c in range(basis * basis // chunk):
         invt_ref[c * chunk : (c + 1) * chunk, :] = inv_ref[:, c * chunk : (c + 1) * chunk].astype(F32).T
 
+    chains = 8
+
     def body(j, carry):
-        acc = jnp.zeros((fields, zones), F32)
+        sums = [jnp.zeros((fields, zones), F32) for _ in range(chains)]
         for k in range(basis):
-            acc = acc + invt_ref[pl.ds(j * basis + k, 1), :] * h_ref[k * fields : (k + 1) * fields, :]
-        acc_ref[pl.ds(pl.multiple_of(j * fields, fields), fields), :] = acc
+            sums[k % chains] = (
+                sums[k % chains] + invt_ref[pl.ds(j * basis + k, 1), :] * h_ref[k * fields : (k + 1) * fields, :]
+            )
+        while len(sums) > 1:
+            sums = [sums[i] + sums[i + 1] for i in range(0, len(sums), 2)]
+        acc_ref[pl.ds(pl.multiple_of(j * fields, fields), fields), :] = sums[0]
         return carry
 
     lax.fori_loop(0, basis, body, 0)

time: 57.8 us -> 58.3 us (level)
  Pallas kernels: 26.4 us -> 27 us
where the time goes in v5:
time: 58.3 us; the launch traced here: 58 us
  Pallas kernels  27 us (46%)
  starting transfers between devices  21.7 us (37%)
  waiting for transfers between devices  6.86 us (12%)
  local copies, waits for them, and re-layouts  2.3 us (4%)
    ppermute x6, starting transfers between devices, shifted(): return lax.ppermute(block, axis, route)  21.7 us
    pallas_call x1, Pallas kernels, tet_partials(): pl.pallas_call(kernel, grid=(tet_count // block,), in_specs=[row_spec, ro...  15.8 us
    pallas_call x1, Pallas kernels, finish(): pl.pallas_call(kernel, out_shape=jax.ShapeDtypeStruct((zones, width), F32...  11.2 us
    ppermute x6, waiting for transfers between devices, shifted(): return lax.ppermute(block, axis, route)  6.86 us
  transfers between devices with their start and end apart: 6, of which 3 were waited for; matrix products, arithmetic and copies ran while one was open for 1% of the time, Pallas kernels for 0%

profile of v5, /device:TPU:56, one launch (start us, length us, event | category | flops | bytes accessed | tf_op | source)
XLA Modules:
  0.0 58.0 jit_solution(1206516426381347525)
XLA Ops:
  0.0 15.8 %shard_map.100 = (f32[512,256]{1,0:T(8,128)}, bf16[256,512]{1,0:T(8,128)(2,1)}) custom-call(s32[1,2048]{1,0:T(1,128)} %bitcast.8, s32[1,2048]{1,0:T(1,128)} %bitcast.9, f32[1,2048]{1,0:T(1,128)} %bitcast.10, s32[1,2048]{1,0:T(1,128)} %bitcast.11, bf16[256,512]{1,0:T(8,128)(2,1)} %coeff_ref.1, bf16[512,64]{1,0:T(8,128)(2,1)} %bitcast.6, ...), custom_call_target="tpu_custom_call" | custom-call | tf_op jit(solution)/shard_map/pallas_call | solution.py:102
  15.8 0.8 %fusion = (bf16[16,512]{1,0:T(8,128)(2,1)S(1)}, bf16[16,512]{1,0:T(8,128)(2,1)S(1)}, bf16[16,512]{1,0:T(8,128)(2,1)S(1)}, bf16[16,512]{1,0:T(8,128)(2,1)S(1)}, b...) fusion(bf16[256,512]{1,0:T(8,128)(2,1)} %get-tuple-element.8), kind=kLoop, calls=%fused_computation.14 | loop fusion | bytes 262144 | tf_op jit(solution)/shard_map/slice | solution.py:234
  16.7 2.2 %collective-permute-start.5 = (bf16[16,512]{1,0:T(8,128)(2,1)S(1)}, bf16[16,512]{1,0:T(8,128)(2,1)S(1)}, u32[]{:S(2)}, u32[]{:S(2)}) collective-permute-start(bf16[16,512]{1,0:T(8,128)(2,1)S(1)} %get-tuple-element.9), channel_id=1, source_target_pairs={{0,448},{64,0},{128,64},{192,128},{256,192},{320,256},{384,320},{4... | collective-permute-start | bytes 49160 | tf_op jit(solution)/shard_map/ppermute | solution.py:196
  18.9 0.0 collective-permute-start.4
  18.9 4.3 %collective-permute-start = (bf16[48,512]{1,0:T(8,128)(2,1)S(1)}, bf16[48,512]{1,0:T(8,128)(2,1)S(1)}, u32[]{:S(2)}, u32[]{:S(2)}) collective-permute-start(bf16[48,512]{1,0:T(8,128)(2,1)S(1)} %pad_maximum_fusion), channel_id=1, source_target_pairs={{0,1},{1,2},{2,3},{3,4},{4,5},{5,6},{6,7},{7,8},{8,9},{9,10},{10,1... | collective-permute-start | bytes 147464 | tf_op jit(solution)/shard_map/ppermute | solution.py:196
  23.2 0.8 %slice.103 = bf16[32,512]{1,0:T(8,128)(2,1)S(1)} slice(bf16[256,512]{1,0:T(8,128)(2,1)} %get-tuple-element.8), slice={[80:112], [0:512]} | slice | bytes 65536 | tf_op jit(solution)/shard_map/slice | solution.py:230
  23.9 9.4 %collective-permute-start.1 = (bf16[48,512]{1,0:T(8,128)(2,1)S(1)}, bf16[48,512]{1,0:T(8,128)(2,1)S(1)}, u32[]{:S(2)}, u32[]{:S(2)}) collective-permute-start(bf16[48,512]{1,0:T(8,128)(2,1)S(1)} %pad_maximum_fusion.1), channel_id=1, source_target_pairs={{0,63},{1,0},{2,1},{3,2},{4,3},{5,4},{6,5},{7,6},{8,7},{9,8},{10,9... | collective-permute-start | bytes 147464 | tf_op jit(solution)/shard_map/ppermute | solution.py:196
  33.3 0.0 collective-permute-done
  33.3 1.7 %collective-permute-done.1 = bf16[48,512]{1,0:T(8,128)(2,1)S(1)} collective-permute-done((bf16[48,512]{1,0:T(8,128)(2,1)S(1)}, bf16[48,512]{1,0:T(8,128)(2,1)S(1)}, u32[]{:S(2)}, u32[]{:S(2)}) %collective-permute-start.1) | collective-permute-done | bytes 49184 | tf_op jit(solution)/shard_map/ppermute | solution.py:196
  35.0 3.8 %collective-permute-start.2 = (bf16[48,512]{1,0:T(8,128)(2,1)S(1)}, bf16[48,512]{1,0:T(8,128)(2,1)S(1)}, u32[]{:S(2)}, u32[]{:S(2)}) collective-permute-start(bf16[48,512]{1,0:T(8,128)(2,1)S(1)} %pad_maximum_fusion.2), channel_id=1, source_target_pairs={{0,8},{1,9},{2,10},{3,11},{4,12},{5,13},{6,14},{7,15},{8,16},{9,17... | collective-permute-start | bytes 147464 | tf_op jit(solution)/shard_map/ppermute | solution.py:196
  38.9 2.0 %collective-permute-start.3 = (bf16[48,512]{1,0:T(8,128)(2,1)S(1)}, bf16[48,512]{1,0:T(8,128)(2,1)S(1)}, u32[]{:S(2)}, u32[]{:S(2)}) collective-permute-start(bf16[48,512]{1,0:T(8,128)(2,1)S(1)} %pad_maximum_fusion.3), channel_id=1, source_target_pairs={{0,56},{1,57},{2,58},{3,59},{4,60},{5,61},{6,62},{7,63},{8,0},{9,1... | collective-permute-start | bytes 147464 | tf_op jit(solution)/shard_map/ppermute | solution.py:196
  40.9 0.1 collective-permute-done.2
  41.0 5.0 %collective-permute-done.3 = bf16[48,512]{1,0:T(8,128)(2,1)S(1)} collective-permute-done((bf16[48,512]{1,0:T(8,128)(2,1)S(1)}, bf16[48,512]{1,0:T(8,128)(2,1)S(1)}, u32[]{:S(2)}, u32[]{:S(2)}) %collective-permute-start.3) | collective-permute-done | bytes 49184 | tf_op jit(solution)/shard_map/ppermute | solution.py:196
  46.1 0.0 collective-permute-done.4
  46.1 0.0 collective-permute-done.5
  46.1 0.0 copy-start
  46.2 0.6 %copy-done = bf16[160,512]{1,0:T(8,128)(2,1)} copy-done((bf16[160,512]{1,0:T(8,128)(2,1)}, bf16[160,512]{1,0:T(8,128)(2,1)S(1)}, u32[]{:S(2)}) %copy-start) | copy-done | bytes 163864
  46.8 11.2 %shard_map.101 = f32[256,512]{1,0:T(8,128)} custom-call(f32[512,256]{1,0:T(8,128)} %get-tuple-element.7.own_ref, bf16[160,512]{1,0:T(8,128)(2,1)} %copy-done, s32[1,160]{1,0:T(1,128)} %list_ref.1, bf16[256,4096]{1,0:T(8,128)(2,1)} %inv_ref.1), custom_call_target="tpu_custom_call" | custom-call | tf_op jit(solution)/shard_map/pallas_call | solution.py:181
  (14 shorter events, 0.1 us)
Async XLA Ops:
  16.7 29.5 %collective-permute-start.5 = (bf16[16,512]{1,0:T(8,128)(2,1)S(1)}, bf16[16,512]{1,0:T(8,128)(2,1)S(1)}, u32[]{:S(2)}, u32[]{:S(2)}) collective-permute-start(bf16[16,512]{1,0:T(8,128)(2,1)S(1)} %get-tuple-element.9), channel_id=1, source_target_pairs={{0,448},{64,0},{128,64},{192,128},{256,192},{320,256},{384,320},{4... | collective-permute-start | bytes 49160 | tf_op jit(solution)/shard_map/ppermute | solution.py:196
  18.9 27.2 %collective-permute-start.4 = (bf16[16,512]{1,0:T(8,128)(2,1)S(1)}, bf16[16,512]{1,0:T(8,128)(2,1)S(1)}, u32[]{:S(2)}, u32[]{:S(2)}) collective-permute-start(bf16[16,512]{1,0:T(8,128)(2,1)S(1)} %get-tuple-element.10), channel_id=1, source_target_pairs={{0,64},{64,128},{128,192},{192,256},{256,320},{320,384},{384,448},... | collective-permute-start | bytes 49160 | tf_op jit(solution)/shard_map/ppermute | solution.py:196
  18.9 14.4 %collective-permute-start = (bf16[48,512]{1,0:T(8,128)(2,1)S(1)}, bf16[48,512]{1,0:T(8,128)(2,1)S(1)}, u32[]{:S(2)}, u32[]{:S(2)}) collective-permute-start(bf16[48,512]{1,0:T(8,128)(2,1)S(1)} %pad_maximum_fusion), channel_id=1, source_target_pairs={{0,1},{1,2},{2,3},{3,4},{4,5},{5,6},{6,7},{7,8},{8,9},{9,10},{10,1... | collective-permute-start | bytes 147464 | tf_op jit(solution)/shard_map/ppermute | solution.py:196
  23.9 11.1 %collective-permute-start.1 = (bf16[48,512]{1,0:T(8,128)(2,1)S(1)}, bf16[48,512]{1,0:T(8,128)(2,1)S(1)}, u32[]{:S(2)}, u32[]{:S(2)}) collective-permute-start(bf16[48,512]{1,0:T(8,128)(2,1)S(1)} %pad_maximum_fusion.1), channel_id=1, source_target_pairs={{0,63},{1,0},{2,1},{3,2},{4,3},{5,4},{6,5},{7,6},{8,7},{9,8},{10,9... | collective-permute-start | bytes 147464 | tf_op jit(solution)/shard_map/ppermute | solution.py:196
  35.0 6.0 %collective-permute-start.2 = (bf16[48,512]{1,0:T(8,128)(2,1)S(1)}, bf16[48,512]{1,0:T(8,128)(2,1)S(1)}, u32[]{:S(2)}, u32[]{:S(2)}) collective-permute-start(bf16[48,512]{1,0:T(8,128)(2,1)S(1)} %pad_maximum_fusion.2), channel_id=1, source_target_pairs={{0,8},{1,9},{2,10},{3,11},{4,12},{5,13},{6,14},{7,15},{8,16},{9,17... | collective-permute-start | bytes 147464 | tf_op jit(solution)/shard_map/ppermute | solution.py:196
  38.9 7.2 %collective-permute-start.3 = (bf16[48,512]{1,0:T(8,128)(2,1)S(1)}, bf16[48,512]{1,0:T(8,128)(2,1)S(1)}, u32[]{:S(2)}, u32[]{:S(2)}) collective-permute-start(bf16[48,512]{1,0:T(8,128)(2,1)S(1)} %pad_maximum_fusion.3), channel_id=1, source_target_pairs={{0,56},{1,57},{2,58},{3,59},{4,60},{5,61},{6,62},{7,63},{8,0},{9,1... | collective-permute-start | bytes 147464 | tf_op jit(solution)/shard_map/ppermute | solution.py:196
  46.1 0.7 %copy-start = (bf16[160,512]{1,0:T(8,128)(2,1)}, bf16[160,512]{1,0:T(8,128)(2,1)S(1)}, u32[]{:S(2)}) copy-start(bf16[160,512]{1,0:T(8,128)(2,1)S(1)} %constant_dynamic-update-slice_fusion.recv_ref) | copy-start | bytes 491524

commit v6 on v5

--- a/solution.py
+++ b/solution.py
@@ -161,11 +161,10 @@
     chains = 8
 
     def body(j, carry):
+        rows = invt_ref.at[pl.ds(pl.multiple_of(j * basis, basis), basis), :]
         sums = [jnp.zeros((fields, zones), F32) for _ in range(chains)]
         for k in range(basis):
-            sums[k % chains] = (
-                sums[k % chains] + invt_ref[pl.ds(j * basis + k, 1), :] * h_ref[k * fields : (k + 1) * fields, :]
-            )
+            sums[k % chains] = sums[k % chains] + rows[k : k + 1, :] * h_ref[k * fields : (k + 1) * fields, :]
         while len(sums) > 1:
             sums = [sums[i] + sums[i + 1] for i in range(0, len(sums), 2)]
         acc_ref[pl.ds(pl.multiple_of(j * fields, fields), fields), :] = sums[0]

time: 58.3 us -> 54.8 us (0.940)
  Pallas kernels: 27 us -> 23.5 us
    pallas_call x1, Pallas kernels: 11.2 us -> 7.65 us  [finish(): pl.pallas_call(kernel, out_shape=jax.ShapeDtypeStruct((zones, width), F32...]
where the time goes in v6:
time: 54.8 us; the launch traced here: 54.5 us
  Pallas kernels  23.5 us (43%)
  starting transfers between devices  21.7 us (40%)
  waiting for transfers between devices  6.86 us (13%)
  local copies, waits for them, and re-layouts  2.3 us (4%)
    ppermute x6, starting transfers between devices, shifted(): return lax.ppermute(block, axis, route)  21.7 us
    pallas_call x1, Pallas kernels, tet_partials(): pl.pallas_call(kernel, grid=(tet_count // block,), in_specs=[row_spec, ro...  15.8 us
    pallas_call x1, Pallas kernels, finish(): pl.pallas_call(kernel, out_shape=jax.ShapeDtypeStruct((zones, width), F32...  7.65 us
    ppermute x6, waiting for transfers between devices, shifted(): return lax.ppermute(block, axis, route)  6.86 us
  transfers between devices with their start and end apart: 6, of which 3 were waited for; matrix products, arithmetic and copies ran while one was open for 1% of the time, Pallas kernels for 0%

profile of v6, /device:TPU:56, one launch (start us, length us, event | category | flops | bytes accessed | tf_op | source)
XLA Modules:
  0.0 54.5 jit_solution(18406139784999596052)
XLA Ops:
  0.0 15.8 %shard_map.100 = (f32[512,256]{1,0:T(8,128)}, bf16[256,512]{1,0:T(8,128)(2,1)}) custom-call(s32[1,2048]{1,0:T(1,128)} %bitcast.8, s32[1,2048]{1,0:T(1,128)} %bitcast.9, f32[1,2048]{1,0:T(1,128)} %bitcast.10, s32[1,2048]{1,0:T(1,128)} %bitcast.11, bf16[256,512]{1,0:T(8,128)(2,1)} %coeff_ref.1, bf16[512,64]{1,0:T(8,128)(2,1)} %bitcast.6, ...), custom_call_target="tpu_custom_call" | custom-call | tf_op jit(solution)/shard_map/pallas_call | solution.py:102
  15.8 0.8 %fusion = (bf16[16,512]{1,0:T(8,128)(2,1)S(1)}, bf16[16,512]{1,0:T(8,128)(2,1)S(1)}, bf16[16,512]{1,0:T(8,128)(2,1)S(1)}, bf16[16,512]{1,0:T(8,128)(2,1)S(1)}, b...) fusion(bf16[256,512]{1,0:T(8,128)(2,1)} %get-tuple-element.8), kind=kLoop, calls=%fused_computation.14 | loop fusion | bytes 262144 | tf_op jit(solution)/shard_map/slice | solution.py:233
  16.7 2.2 %collective-permute-start.5 = (bf16[16,512]{1,0:T(8,128)(2,1)S(1)}, bf16[16,512]{1,0:T(8,128)(2,1)S(1)}, u32[]{:S(2)}, u32[]{:S(2)}) collective-permute-start(bf16[16,512]{1,0:T(8,128)(2,1)S(1)} %get-tuple-element.9), channel_id=1, source_target_pairs={{0,448},{64,0},{128,64},{192,128},{256,192},{320,256},{384,320},{4... | collective-permute-start | bytes 49160 | tf_op jit(solution)/shard_map/ppermute | solution.py:195
  18.9 0.0 collective-permute-start.4
  18.9 4.3 %collective-permute-start = (bf16[48,512]{1,0:T(8,128)(2,1)S(1)}, bf16[48,512]{1,0:T(8,128)(2,1)S(1)}, u32[]{:S(2)}, u32[]{:S(2)}) collective-permute-start(bf16[48,512]{1,0:T(8,128)(2,1)S(1)} %pad_maximum_fusion), channel_id=1, source_target_pairs={{0,1},{1,2},{2,3},{3,4},{4,5},{5,6},{6,7},{7,8},{8,9},{9,10},{10,1... | collective-permute-start | bytes 147464 | tf_op jit(solution)/shard_map/ppermute | solution.py:195
  23.2 0.8 %slice.103 = bf16[32,512]{1,0:T(8,128)(2,1)S(1)} slice(bf16[256,512]{1,0:T(8,128)(2,1)} %get-tuple-element.8), slice={[80:112], [0:512]} | slice | bytes 65536 | tf_op jit(solution)/shard_map/slice | solution.py:229
  23.9 9.4 %collective-permute-start.1 = (bf16[48,512]{1,0:T(8,128)(2,1)S(1)}, bf16[48,512]{1,0:T(8,128)(2,1)S(1)}, u32[]{:S(2)}, u32[]{:S(2)}) collective-permute-start(bf16[48,512]{1,0:T(8,128)(2,1)S(1)} %pad_maximum_fusion.1), channel_id=1, source_target_pairs={{0,63},{1,0},{2,1},{3,2},{4,3},{5,4},{6,5},{7,6},{8,7},{9,8},{10,9... | collective-permute-start | bytes 147464 | tf_op jit(solution)/shard_map/ppermute | solution.py:195
  33.3 0.0 collective-permute-done
  33.3 1.7 %collective-permute-done.1 = bf16[48,512]{1,0:T(8,128)(2,1)S(1)} collective-permute-done((bf16[48,512]{1,0:T(8,128)(2,1)S(1)}, bf16[48,512]{1,0:T(8,128)(2,1)S(1)}, u32[]{:S(2)}, u32[]{:S(2)}) %collective-permute-start.1) | collective-permute-done | bytes 49184 | tf_op jit(solution)/shard_map/ppermute | solution.py:195
  35.0 3.8 %collective-permute-start.2 = (bf16[48,512]{1,0:T(8,128)(2,1)S(1)}, bf16[48,512]{1,0:T(8,128)(2,1)S(1)}, u32[]{:S(2)}, u32[]{:S(2)}) collective-permute-start(bf16[48,512]{1,0:T(8,128)(2,1)S(1)} %pad_maximum_fusion.2), channel_id=1, source_target_pairs={{0,8},{1,9},{2,10},{3,11},{4,12},{5,13},{6,14},{7,15},{8,16},{9,17... | collective-permute-start | bytes 147464 | tf_op jit(solution)/shard_map/ppermute | solution.py:195
  38.9 2.0 %collective-permute-start.3 = (bf16[48,512]{1,0:T(8,128)(2,1)S(1)}, bf16[48,512]{1,0:T(8,128)(2,1)S(1)}, u32[]{:S(2)}, u32[]{:S(2)}) collective-permute-start(bf16[48,512]{1,0:T(8,128)(2,1)S(1)} %pad_maximum_fusion.3), channel_id=1, source_target_pairs={{0,56},{1,57},{2,58},{3,59},{4,60},{5,61},{6,62},{7,63},{8,0},{9,1... | collective-permute-start | bytes 147464 | tf_op jit(solution)/shard_map/ppermute | solution.py:195
  40.9 0.1 collective-permute-done.2
  41.0 5.0 %collective-permute-done.3 = bf16[48,512]{1,0:T(8,128)(2,1)S(1)} collective-permute-done((bf16[48,512]{1,0:T(8,128)(2,1)S(1)}, bf16[48,512]{1,0:T(8,128)(2,1)S(1)}, u32[]{:S(2)}, u32[]{:S(2)}) %collective-permute-start.3) | collective-permute-done | bytes 49184 | tf_op jit(solution)/shard_map/ppermute | solution.py:195
  46.1 0.0 collective-permute-done.4
  46.1 0.0 collective-permute-done.5
  46.1 0.0 copy-start
  46.2 0.6 %copy-done = bf16[160,512]{1,0:T(8,128)(2,1)} copy-done((bf16[160,512]{1,0:T(8,128)(2,1)}, bf16[160,512]{1,0:T(8,128)(2,1)S(1)}, u32[]{:S(2)}) %copy-start) | copy-done | bytes 163864
  46.8 7.7 %shard_map.101 = f32[256,512]{1,0:T(8,128)} custom-call(f32[512,256]{1,0:T(8,128)} %get-tuple-element.7.own_ref, bf16[160,512]{1,0:T(8,128)(2,1)} %copy-done, s32[1,160]{1,0:T(1,128)} %list_ref.1, bf16[256,4096]{1,0:T(8,128)(2,1)} %inv_ref.1), custom_call_target="tpu_custom_call" | custom-call | tf_op jit(solution)/shard_map/pallas_call | solution.py:180
  (14 shorter events, 0.1 us)
Async XLA Ops:
  16.7 29.5 %collective-permute-start.5 = (bf16[16,512]{1,0:T(8,128)(2,1)S(1)}, bf16[16,512]{1,0:T(8,128)(2,1)S(1)}, u32[]{:S(2)}, u32[]{:S(2)}) collective-permute-start(bf16[16,512]{1,0:T(8,128)(2,1)S(1)} %get-tuple-element.9), channel_id=1, source_target_pairs={{0,448},{64,0},{128,64},{192,128},{256,192},{320,256},{384,320},{4... | collective-permute-start | bytes 49160 | tf_op jit(solution)/shard_map/ppermute | solution.py:195
  18.9 27.2 %collective-permute-start.4 = (bf16[16,512]{1,0:T(8,128)(2,1)S(1)}, bf16[16,512]{1,0:T(8,128)(2,1)S(1)}, u32[]{:S(2)}, u32[]{:S(2)}) collective-permute-start(bf16[16,512]{1,0:T(8,128)(2,1)S(1)} %get-tuple-element.10), channel_id=1, source_target_pairs={{0,64},{64,128},{128,192},{192,256},{256,320},{320,384},{384,448},... | collective-permute-start | bytes 49160 | tf_op jit(solution)/shard_map/ppermute | solution.py:195
  18.9 14.4 %collective-permute-start = (bf16[48,512]{1,0:T(8,128)(2,1)S(1)}, bf16[48,512]{1,0:T(8,128)(2,1)S(1)}, u32[]{:S(2)}, u32[]{:S(2)}) collective-permute-start(bf16[48,512]{1,0:T(8,128)(2,1)S(1)} %pad_maximum_fusion), channel_id=1, source_target_pairs={{0,1},{1,2},{2,3},{3,4},{4,5},{5,6},{6,7},{7,8},{8,9},{9,10},{10,1... | collective-permute-start | bytes 147464 | tf_op jit(solution)/shard_map/ppermute | solution.py:195
  23.9 11.1 %collective-permute-start.1 = (bf16[48,512]{1,0:T(8,128)(2,1)S(1)}, bf16[48,512]{1,0:T(8,128)(2,1)S(1)}, u32[]{:S(2)}, u32[]{:S(2)}) collective-permute-start(bf16[48,512]{1,0:T(8,128)(2,1)S(1)} %pad_maximum_fusion.1), channel_id=1, source_target_pairs={{0,63},{1,0},{2,1},{3,2},{4,3},{5,4},{6,5},{7,6},{8,7},{9,8},{10,9... | collective-permute-start | bytes 147464 | tf_op jit(solution)/shard_map/ppermute | solution.py:195
  35.0 6.0 %collective-permute-start.2 = (bf16[48,512]{1,0:T(8,128)(2,1)S(1)}, bf16[48,512]{1,0:T(8,128)(2,1)S(1)}, u32[]{:S(2)}, u32[]{:S(2)}) collective-permute-start(bf16[48,512]{1,0:T(8,128)(2,1)S(1)} %pad_maximum_fusion.2), channel_id=1, source_target_pairs={{0,8},{1,9},{2,10},{3,11},{4,12},{5,13},{6,14},{7,15},{8,16},{9,17... | collective-permute-start | bytes 147464 | tf_op jit(solution)/shard_map/ppermute | solution.py:195
  38.9 7.2 %collective-permute-start.3 = (bf16[48,512]{1,0:T(8,128)(2,1)S(1)}, bf16[48,512]{1,0:T(8,128)(2,1)S(1)}, u32[]{:S(2)}, u32[]{:S(2)}) collective-permute-start(bf16[48,512]{1,0:T(8,128)(2,1)S(1)} %pad_maximum_fusion.3), channel_id=1, source_target_pairs={{0,56},{1,57},{2,58},{3,59},{4,60},{5,61},{6,62},{7,63},{8,0},{9,1... | collective-permute-start | bytes 147464 | tf_op jit(solution)/shard_map/ppermute | solution.py:195
  46.1 0.7 %copy-start = (bf16[160,512]{1,0:T(8,128)(2,1)}, bf16[160,512]{1,0:T(8,128)(2,1)S(1)}, u32[]{:S(2)}) copy-start(bf16[160,512]{1,0:T(8,128)(2,1)S(1)} %constant_dynamic-update-slice_fusion.recv_ref) | copy-start | bytes 491524

commit v7 on v6

--- a/solution.py
+++ b/solution.py
@@ -13,7 +13,7 @@
 
 def tet_kernel(
     zone_ref, table_ref, vol_ref, dest_ref, coeff_ref, bold_ref, bnew_ref, qw_ref,
-    own_ref, slot_out_ref, ct_ref, boldc_ref, bnewc_ref, qwt_ref, slot_ref, mom_ref, spread_ref,
+    own_ref, up_ref, down_ref, ahead_ref, behind_ref, rise_ref, fall_ref, ct_ref, boldc_ref, bnewc_ref, qwt_ref, slot_ref, mom_ref, spread_ref,
     *, tables, basis, fields, zones, slots_pad
 ):
     step = pl.program_id(0)
@@ -85,10 +85,18 @@
 
     @pl.when(step == pl.num_programs(0) - 1)
     def _():
-        slot_out_ref[...] = slot_ref[...].astype(BF16)
-
-
-def tet_partials(old_coeff, bold, bnew, quad_weight, zone, table, vol, dest, slots_pad, block):
+        cap = ahead_ref.shape[0]
+        part = lambda k: slot_ref[k * cap : (k + 1) * cap, :].astype(BF16)
+        for ref, ks in ((up_ref, (0, 4, 7)), (down_ref, (1, 5, 6))):
+            for n, k in enumerate(ks):
+                ref[n * cap : (n + 1) * cap, :] = part(k)
+        ahead_ref[...] = part(8)
+        behind_ref[...] = part(9)
+        rise_ref[...] = part(2)
+        fall_ref[...] = part(3)
+
+
+def tet_partials(old_coeff, bold, bnew, quad_weight, zone, table, vol, dest, slots_pad, cap, block):
     tet_count = zone.shape[0]
     zones, width = old_coeff.shape
     tables = quad_weight.shape[0]
@@ -112,11 +120,10 @@
             whole(bnew.shape),
             whole(quad_weight.shape),
         ],
-        out_specs=[whole((width, zones)), whole((slots_pad, width))],
-        out_shape=[
-            jax.ShapeDtypeStruct((width, zones), F32),
-            jax.ShapeDtypeStruct((slots_pad, width), BF16),
-        ],
+        out_specs=[whole((width, zones))] + [whole((3 * cap, width))] * 2 + [whole((cap, width))] * 4,
+        out_shape=[jax.ShapeDtypeStruct((width, zones), F32)]
+        + [jax.ShapeDtypeStruct((3 * cap, width), BF16)] * 2
+        + [jax.ShapeDtypeStruct((cap, width), BF16)] * 4,
         scratch_shapes=[
             pltpu.VMEM((width, zones), BF16),
             pltpu.VMEM((basis, tables * basis), BF16),
@@ -139,11 +146,21 @@
     )
 
 
-def finish_kernel(own_ref, recv_ref, list_ref, inv_ref, out_ref, g_ref, h_ref, invt_ref, acc_ref, *, basis, fields):
+def finish_kernel(
+    own_ref, left_ref, right_ref, came_up_ref, came_down_ref, back_ref, front_ref, list_ref, inv_ref,
+    out_ref, recv_ref, g_ref, h_ref, invt_ref, acc_ref, *, basis, fields
+):
     width, zones = own_ref.shape
     slots = recv_ref.shape[0]
+    cap = back_ref.shape[0]
+    order = (
+        (left_ref, 0), (right_ref, 0), (came_up_ref, 0), (came_down_ref, 0), (came_up_ref, 1),
+        (came_down_ref, 2), (came_up_ref, 2), (came_down_ref, 1), (back_ref, 0), (front_ref, 0),
+    )
+    for k, (ref, n) in enumerate(order):
+        recv_ref[k * cap : (k + 1) * cap, :] = ref[n * cap : (n + 1) * cap, :].astype(F32)
     slot_hot = (lax.broadcasted_iota(jnp.int32, (zones, slots), 0) == list_ref[...]).astype(F32)
-    arrived = jnp.dot(slot_hot, recv_ref[...].astype(F32), preferred_element_type=F32)
+    arrived = jnp.dot(slot_hot, recv_ref[...], preferred_element_type=F32)
     rounded = (own_ref[...] + arrived.T).astype(BF16).astype(F32)
     lanes = 128
     halves = zones // lanes
@@ -181,12 +198,13 @@
         kernel,
         out_shape=jax.ShapeDtypeStruct((zones, width), F32),
         scratch_shapes=[
+            pltpu.VMEM((recv_row.shape[1], width), F32),
             pltpu.VMEM((zones // 128 * width, 128), F32),
             pltpu.VMEM((width, zones), F32),
             pltpu.VMEM((basis * basis, zones), F32),
             pltpu.VMEM((width, zones), F32),
         ],
-    )(own_t, received, recv_row, inv_mass)
+    )(own_t, *received, recv_row, inv_mass)
 
 
 def shifted(block, axis, distance):
@@ -218,38 +236,21 @@
 
     bold = basis_old.reshape(tables * quad, basis)
     bnew = basis_new.reshape(tables * quad, basis)
-    own_t, slot_rows = tet_partials(
-        old_coeff, bold, bnew, quad_weight, tet_zone, tet_table, tet_volume, tet_dest, slots_pad, block
-    )
-    outgoing = slot_rows[:slot_total].reshape(partner_count, slot_cap, row_width)
-
+    own_t, going_up, going_down, ahead, behind, rise, fall = tet_partials(
+        old_coeff, bold, bnew, quad_weight, tet_zone, tet_table, tet_volume, tet_dest, slots_pad, slot_cap, block
+    )
     lane_count = lax.axis_size("yz")
     face_side = 1 << (lane_count.bit_length() - 1) // 2
-    going_up = jnp.concatenate([outgoing[0], outgoing[4], outgoing[7]], axis=0)
-    going_down = jnp.concatenate([outgoing[1], outgoing[5], outgoing[6]], axis=0)
-    from_left = shifted(going_up, "yz", 1).reshape(3, slot_cap, row_width)
-    from_right = shifted(going_down, "yz", -1).reshape(3, slot_cap, row_width)
-    from_back = shifted(outgoing[8], "gx", 1)
-    from_front = shifted(outgoing[9], "gx", -1)
-    upward = jnp.concatenate([outgoing[2], from_left[1], from_right[2]], axis=0)
-    downward = jnp.concatenate([outgoing[3], from_left[2], from_right[1]], axis=0)
-    came_up = shifted(upward, "yz", face_side).reshape(3, slot_cap, row_width)
-    came_down = shifted(downward, "yz", -face_side).reshape(3, slot_cap, row_width)
-    received = jnp.concatenate(
-        [
-            from_left[0],
-            from_right[0],
-            came_up[0],
-            came_down[0],
-            came_up[1],
-            came_down[2],
-            came_up[2],
-            came_down[1],
-            from_back,
-            from_front,
-        ],
-        axis=0,
-    )
+    from_left = shifted(going_up, "yz", 1)
+    from_right = shifted(going_down, "yz", -1)
+    from_back = shifted(ahead, "gx", 1)
+    from_front = shifted(behind, "gx", -1)
+    block_of = lambda x, n: x[n * slot_cap : (n + 1) * slot_cap]
+    upward = jnp.concatenate([rise, block_of(from_left, 1), block_of(from_right, 2)], axis=0)
+    downward = jnp.concatenate([fall, block_of(from_left, 2), block_of(from_right, 1)], axis=0)
+    came_up = shifted(upward, "yz", face_side)
+    came_down = shifted(downward, "yz", -face_side)
+    received = (from_left, from_right, came_up, came_down, from_back, from_front)
     return finish(own_t, received, recv_list, inv_mass, basis, fields)
 
 

time: 54.8 us -> 56.9 us (1.038)
  the two profiles are of different devices: /device:TPU:56 before, /device:TPU:1 now
where the time goes in v7:
time: 56.9 us; the launch traced here: 56.4 us
  starting transfers between devices  26 us (46%)
  Pallas kernels  23.5 us (41%)
  waiting for transfers between devices  4.82 us (8%)
  other arithmetic  1.46 us (3%)
  local copies, waits for them, and re-layouts  0.62 us (1%)
    ppermute x6, starting transfers between devices, shifted(): return lax.ppermute(block, axis, route)  26 us
    pallas_call x1, Pallas kernels, tet_partials(): pl.pallas_call(kernel, grid=(tet_count // block,), in_specs=[row_spec, ro...  15.8 us
    pallas_call x1, Pallas kernels, finish(): pl.pallas_call(kernel, out_shape=jax.ShapeDtypeStruct((zones, width), F32...  7.68 us
    ppermute x6, waiting for transfers between devices, shifted(): return lax.ppermute(block, axis, route)  4.82 us
  transfers between devices with their start and end apart: 6, of which 3 were waited for; matrix products, arithmetic and copies ran while one was open for 1% of the time, Pallas kernels for 0%

profile of v7, /device:TPU:1, one launch (start us, length us, event | category | flops | bytes accessed | tf_op | source)
XLA Modules:
  0.0 56.4 jit_solution(1443264592856084473)
XLA Ops:
  0.0 15.8 %shard_map.100 = (f32[512,256]{1,0:T(8,128)}, bf16[48,512]{1,0:T(8,128)(2,1)}, bf16[48,512]{1,0:T(8,128)(2,1)}, bf16[16,512]{1,0:T(8,128)(2,1)}, bf16[16,512]{1,...) custom-call(s32[1,2048]{1,0:T(1,128)} %bitcast.8, s32[1,2048]{1,0:T(1,128)} %bitcast.9, ...), custom_call_target="tpu_custom_call" | custom-call | tf_op jit(solution)/shard_map/pallas_call | solution.py:110
  15.8 4.8 %collective-permute-start = (bf16[48,512]{1,0:T(8,128)(2,1)}, bf16[48,512]{1,0:T(8,128)(2,1)S(1)}, u32[]{:S(2)}, u32[]{:S(2)}) collective-permute-start(bf16[48,512]{1,0:T(8,128)(2,1)} %get-tuple-element.13), channel_id=1, source_target_pairs={{0,1},{1,2},{2,3},{3,4},{4,5},{5,6},{6,7},{7,8},{8,9},{9,10},{10,1... | collective-permute-start | bytes 147464 | tf_op jit(solution)/shard_map/ppermute | solution.py:213
  20.6 11.5 %collective-permute-start.1 = (bf16[48,512]{1,0:T(8,128)(2,1)}, bf16[48,512]{1,0:T(8,128)(2,1)S(1)}, u32[]{:S(2)}, u32[]{:S(2)}) collective-permute-start(bf16[48,512]{1,0:T(8,128)(2,1)} %get-tuple-element.14), channel_id=1, source_target_pairs={{0,63},{1,0},{2,1},{3,2},{4,3},{5,4},{6,5},{7,6},{8,7},{9,8},{10,9... | collective-permute-start | bytes 147464 | tf_op jit(solution)/shard_map/ppermute | solution.py:213
  32.1 0.0 collective-permute-done.left_ref
  32.1 0.0 copy-start
  32.2 1.4 %collective-permute-done.1.right_ref = bf16[48,512]{1,0:T(8,128)(2,1)S(1)} collective-permute-done((bf16[48,512]{1,0:T(8,128)(2,1)}, bf16[48,512]{1,0:T(8,128)(2,1)S(1)}, u32[]{:S(2)}, u32[]{:S(2)}) %collective-permute-start.1) | collective-permute-done | bytes 49184 | tf_op jit(solution)/shard_map/ppermute | solution.py:213
  33.6 0.0 copy-start.1
  33.6 0.7 %pad_maximum_fusion = bf16[48,512]{1,0:T(8,128)(2,1)S(1)} fusion(bf16[16,512]{1,0:T(8,128)(2,1)S(1)} %get-tuple-element.22, bf16[16,512]{1,0:T(8,128)(2,1)S(1)} %get-tuple-element.20, bf16[16,512]{1,0:T(8,128)(2,1)} %get-tuple-element.15), kind=kLoop, calls=%fused_computation | loop fusion | flops 147456 | bytes 98304 | tf_op jit(solution)/shard_map/concatenate | solution.py:249
  34.3 1.9 %collective-permute-start.2 = (bf16[48,512]{1,0:T(8,128)(2,1)S(1)}, bf16[48,512]{1,0:T(8,128)(2,1)S(1)}, u32[]{:S(2)}, u32[]{:S(2)}) collective-permute-start(bf16[48,512]{1,0:T(8,128)(2,1)S(1)} %pad_maximum_fusion), channel_id=1, source_target_pairs={{0,8},{1,9},{2,10},{3,11},{4,12},{5,13},{6,14},{7,15},{8,16},{9,17... | collective-permute-start | bytes 147464 | tf_op jit(solution)/shard_map/ppermute | solution.py:213
  36.3 0.7 %pad_maximum_fusion.1 = bf16[48,512]{1,0:T(8,128)(2,1)S(1)} fusion(bf16[16,512]{1,0:T(8,128)(2,1)S(1)} %get-tuple-element.21, bf16[16,512]{1,0:T(8,128)(2,1)S(1)} %get-tuple-element.19, bf16[16,512]{1,0:T(8,128)(2,1)} %get-tuple-element.16), kind=kLoop, calls=%fused_computation.1 | loop fusion | flops 147456 | bytes 98304 | tf_op jit(solution)/shard_map/concatenate | solution.py:250
  37.0 4.6 %collective-permute-start.3 = (bf16[48,512]{1,0:T(8,128)(2,1)S(1)}, bf16[48,512]{1,0:T(8,128)(2,1)S(1)}, u32[]{:S(2)}, u32[]{:S(2)}) collective-permute-start(bf16[48,512]{1,0:T(8,128)(2,1)S(1)} %pad_maximum_fusion.1), channel_id=1, source_target_pairs={{0,56},{1,57},{2,58},{3,59},{4,60},{5,61},{6,62},{7,63},{8,0},{9,1... | collective-permute-start | bytes 147464 | tf_op jit(solution)/shard_map/ppermute | solution.py:213
  41.5 3.2 %collective-permute-start.4 = (bf16[16,512]{1,0:T(8,128)(2,1)}, bf16[16,512]{1,0:T(8,128)(2,1)S(1)}, u32[]{:S(2)}, u32[]{:S(2)}) collective-permute-start(bf16[16,512]{1,0:T(8,128)(2,1)} %get-tuple-element.17), channel_id=1, source_target_pairs={{0,64},{64,128},{128,192},{192,256},{256,320},{320,384},{384,448},... | collective-permute-start | bytes 49160 | tf_op jit(solution)/shard_map/ppermute | solution.py:213
  44.7 0.0 collective-permute-start.5
  44.7 1.1 %collective-permute-done.4.back_ref = bf16[16,512]{1,0:T(8,128)(2,1)S(1)} collective-permute-done((bf16[16,512]{1,0:T(8,128)(2,1)}, bf16[16,512]{1,0:T(8,128)(2,1)S(1)}, u32[]{:S(2)}, u32[]{:S(2)}) %collective-permute-start.4) | collective-permute-done | bytes 16416 | tf_op jit(solution)/shard_map/ppermute | solution.py:213
  45.8 0.0 copy-start.4
  45.8 2.3 %collective-permute-done.5.front_ref = bf16[16,512]{1,0:T(8,128)(2,1)S(1)} collective-permute-done((bf16[16,512]{1,0:T(8,128)(2,1)}, bf16[16,512]{1,0:T(8,128)(2,1)S(1)}, u32[]{:S(2)}, u32[]{:S(2)}) %collective-permute-start.5) | collective-permute-done | bytes 16416 | tf_op jit(solution)/shard_map/ppermute | solution.py:213
  48.1 0.0 copy-start.5
  48.1 0.0 collective-permute-done.2.came_up_ref
  48.1 0.0 copy-start.2
  48.1 0.0 collective-permute-done.3.came_down_ref
  48.1 0.0 copy-start.3
  48.1 0.0 copy-done
  48.1 0.0 copy-done.1
  48.2 0.0 copy-done.4
  48.2 0.5 copy-done.5
  48.7 0.0 copy-done.2
  48.7 0.0 copy-done.3
  48.8 7.7 %shard_map.101 = f32[256,512]{1,0:T(8,128)} custom-call(f32[512,256]{1,0:T(8,128)} %get-tuple-element.12.own_ref, bf16[48,512]{1,0:T(8,128)(2,1)} %copy-done, bf16[48,512]{1,0:T(8,128)(2,1)} %copy-done.1, bf16[48,512]{1,0:T(8,128)(2,1)} %copy-done.2, bf16[48,512]{1,0:T(8,128)(2,1)} %copy-done.3, bf16[16,512]{1,0:T(8,128)(2,1)} %copy-done.4, ...), custom_call_target="tpu_custom_call" | custom-call | tf_op jit(solution)/shard_map/pallas_call | solution.py:197
  (2 shorter events, 0.0 us)
Async XLA Ops:
  15.8 16.3 %collective-permute-start = (bf16[48,512]{1,0:T(8,128)(2,1)}, bf16[48,512]{1,0:T(8,128)(2,1)S(1)}, u32[]{:S(2)}, u32[]{:S(2)}) collective-permute-start(bf16[48,512]{1,0:T(8,128)(2,1)} %get-tuple-element.13), channel_id=1, source_target_pairs={{0,1},{1,2},{2,3},{3,4},{4,5},{5,6},{6,7},{7,8},{8,9},{9,10},{10,1... | collective-permute-start | bytes 147464 | tf_op jit(solution)/shard_map/ppermute | solution.py:213
  20.6 13.0 %collective-permute-start.1 = (bf16[48,512]{1,0:T(8,128)(2,1)}, bf16[48,512]{1,0:T(8,128)(2,1)S(1)}, u32[]{:S(2)}, u32[]{:S(2)}) collective-permute-start(bf16[48,512]{1,0:T(8,128)(2,1)} %get-tuple-element.14), channel_id=1, source_target_pairs={{0,63},{1,0},{2,1},{3,2},{4,3},{5,4},{6,5},{7,6},{8,7},{9,8},{10,9... | collective-permute-start | bytes 147464 | tf_op jit(solution)/shard_map/ppermute | solution.py:213
  32.1 16.0 %copy-start = (bf16[48,512]{1,0:T(8,128)(2,1)}, bf16[48,512]{1,0:T(8,128)(2,1)S(1)}, u32[]{:S(2)}) copy-start(bf16[48,512]{1,0:T(8,128)(2,1)S(1)} %collective-permute-done.left_ref) | copy-start | bytes 147460
  33.6 14.6 %copy-start.1 = (bf16[48,512]{1,0:T(8,128)(2,1)}, bf16[48,512]{1,0:T(8,128)(2,1)S(1)}, u32[]{:S(2)}) copy-start(bf16[48,512]{1,0:T(8,128)(2,1)S(1)} %collective-permute-done.1.right_ref) | copy-start | bytes 147460
  34.3 13.8 %collective-permute-start.2 = (bf16[48,512]{1,0:T(8,128)(2,1)S(1)}, bf16[48,512]{1,0:T(8,128)(2,1)S(1)}, u32[]{:S(2)}, u32[]{:S(2)}) collective-permute-start(bf16[48,512]{1,0:T(8,128)(2,1)S(1)} %pad_maximum_fusion), channel_id=1, source_target_pairs={{0,8},{1,9},{2,10},{3,11},{4,12},{5,13},{6,14},{7,15},{8,16},{9,17... | collective-permute-start | bytes 147464 | tf_op jit(solution)/shard_map/ppermute | solution.py:213
  37.0 11.1 %collective-permute-start.3 = (bf16[48,512]{1,0:T(8,128)(2,1)S(1)}, bf16[48,512]{1,0:T(8,128)(2,1)S(1)}, u32[]{:S(2)}, u32[]{:S(2)}) collective-permute-start(bf16[48,512]{1,0:T(8,128)(2,1)S(1)} %pad_maximum_fusion.1), channel_id=1, source_target_pairs={{0,56},{1,57},{2,58},{3,59},{4,60},{5,61},{6,62},{7,63},{8,0},{9,1... | collective-permute-start | bytes 147464 | tf_op jit(solution)/shard_map/ppermute | solution.py:213
  41.5 4.3 %collective-permute-start.4 = (bf16[16,512]{1,0:T(8,128)(2,1)}, bf16[16,512]{1,0:T(8,128)(2,1)S(1)}, u32[]{:S(2)}, u32[]{:S(2)}) collective-permute-start(bf16[16,512]{1,0:T(8,128)(2,1)} %get-tuple-element.17), channel_id=1, source_target_pairs={{0,64},{64,128},{128,192},{192,256},{256,320},{320,384},{384,448},... | collective-permute-start | bytes 49160 | tf_op jit(solution)/shard_map/ppermute | solution.py:213
  44.7 3.4 %collective-permute-start.5 = (bf16[16,512]{1,0:T(8,128)(2,1)}, bf16[16,512]{1,0:T(8,128)(2,1)S(1)}, u32[]{:S(2)}, u32[]{:S(2)}) collective-permute-start(bf16[16,512]{1,0:T(8,128)(2,1)} %get-tuple-element.18), channel_id=1, source_target_pairs={{0,448},{64,0},{128,64},{192,128},{256,192},{320,256},{384,320},{4... | collective-permute-start | bytes 49160 | tf_op jit(solution)/shard_map/ppermute | solution.py:213
  45.8 2.3 %copy-start.4 = (bf16[16,512]{1,0:T(8,128)(2,1)}, bf16[16,512]{1,0:T(8,128)(2,1)S(1)}, u32[]{:S(2)}) copy-start(bf16[16,512]{1,0:T(8,128)(2,1)S(1)} %collective-permute-done.4.back_ref) | copy-start | bytes 49156
  48.1 0.6 %copy-start.5 = (bf16[16,512]{1,0:T(8,128)(2,1)}, bf16[16,512]{1,0:T(8,128)(2,1)S(1)}, u32[]{:S(2)}) copy-start(bf16[16,512]{1,0:T(8,128)(2,1)S(1)} %collective-permute-done.5.front_ref) | copy-start | bytes 49156
  48.1 0.6 %copy-start.2 = (bf16[48,512]{1,0:T(8,128)(2,1)}, bf16[48,512]{1,0:T(8,128)(2,1)S(1)}, u32[]{:S(2)}) copy-start(bf16[48,512]{1,0:T(8,128)(2,1)S(1)} %collective-permute-done.2.came_up_ref) | copy-start | bytes 147460
  48.1 0.6 %copy-start.3 = (bf16[48,512]{1,0:T(8,128)(2,1)}, bf16[48,512]{1,0:T(8,128)(2,1)S(1)}, u32[]{:S(2)}) copy-start(bf16[48,512]{1,0:T(8,128)(2,1)S(1)} %collective-permute-done.3.came_down_ref) | copy-start | bytes 147460

commit v8 on v4

--- a/solution.py
+++ b/solution.py
@@ -155,17 +155,34 @@
                 pl.ds(half * width + k, fields, stride=basis), :
             ]
     chunk = 128
+    nt = (((1,), (1,)), ((), ()))
+    eye = (
+        lax.broadcasted_iota(jnp.int32, (chunk, chunk), 0) == lax.broadcasted_iota(jnp.int32, (chunk, chunk), 1)
+    ).astype(BF16)
     for c in range(basis * basis // chunk):
-        invt_ref[c * chunk : (c + 1) * chunk, :] = inv_ref[:, c * chunk : (c + 1) * chunk].astype(F32).T
-
-    def body(j, carry):
-        acc = jnp.zeros((fields, zones), F32)
+        invt_ref[c * chunk : (c + 1) * chunk, :] = lax.dot_general(
+            eye, inv_ref[:, c * chunk : (c + 1) * chunk], nt, preferred_element_type=F32
+        )
+
+    chains = 4
+    pair = 2
+
+    def body(jj, carry):
+        rows = invt_ref.at[pl.ds(pl.multiple_of(jj * pair * basis, pair * basis), pair * basis), :]
+        sums = [[jnp.zeros((fields, zones), F32) for _ in range(chains)] for _ in range(pair)]
         for k in range(basis):
-            acc = acc + invt_ref[pl.ds(j * basis + k, 1), :] * h_ref[k * fields : (k + 1) * fields, :]
-        acc_ref[pl.ds(pl.multiple_of(j * fields, fields), fields), :] = acc
+            mass = h_ref[k * fields : (k + 1) * fields, :]
+            for p in range(pair):
+                sums[p][k % chains] = sums[p][k % chains] + rows[p * basis + k : p * basis + k + 1, :] * mass
+        for p in range(pair):
+            part = sums[p]
+            while len(part) > 1:
+                part = [part[i] + part[i + 1] for i in range(0, len(part), 2)]
+            start = pl.multiple_of((jj * pair + p) * fields, fields)
+            acc_ref[pl.ds(start, fields), :] = part[0]
         return carry
 
-    lax.fori_loop(0, basis, body, 0)
+    lax.fori_loop(0, basis // pair, body, 0)
     out_ref[...] = acc_ref[...].T
 
 

time: 57.8 us -> 53.9 us (0.933)
  Pallas kernels: 26.4 us -> 22.5 us
    pallas_call x1, Pallas kernels: 10.6 us -> 6.67 us  [finish(): pl.pallas_call(kernel, out_shape=jax.ShapeDtypeStruct((zones, width), F32...]
  transfers between devices with their start and end apart: 6 -> 6, of which waited for: 3 -> 3; matrix products, arithmetic and copies ran while one was open for 1% -> 2% of each run, Pallas kernels for 0% -> 0%
where the time goes in v8:
time: 53.9 us; the launch traced here: 53.5 us
  Pallas kernels  22.5 us (42%)
  starting transfers between devices  21.7 us (40%)
  waiting for transfers between devices  6.86 us (13%)
  local copies, waits for them, and re-layouts  2.3 us (4%)
    ppermute x6, starting transfers between devices, shifted(): return lax.ppermute(block, axis, route)  21.7 us
    pallas_call x1, Pallas kernels, tet_partials(): pl.pallas_call(kernel, grid=(tet_count // block,), in_specs=[row_spec, ro...  15.8 us
    ppermute x6, waiting for transfers between devices, shifted(): return lax.ppermute(block, axis, route)  6.86 us
    pallas_call x1, Pallas kernels, finish(): pl.pallas_call(kernel, out_shape=jax.ShapeDtypeStruct((zones, width), F32...  6.67 us
  transfers between devices with their start and end apart: 6, of which 3 were waited for; matrix products, arithmetic and copies ran while one was open for 2% of the time, Pallas kernels for 0%

profile of v8, /device:TPU:56, one launch (start us, length us, event | category | flops | bytes accessed | tf_op | source)
XLA Modules:
  0.0 53.5 jit_solution(6983050456592368275)
XLA Ops:
  0.0 15.8 %shard_map.100 = (f32[512,256]{1,0:T(8,128)}, bf16[256,512]{1,0:T(8,128)(2,1)}) custom-call(s32[1,2048]{1,0:T(1,128)} %bitcast.8, s32[1,2048]{1,0:T(1,128)} %bitcast.9, f32[1,2048]{1,0:T(1,128)} %bitcast.10, s32[1,2048]{1,0:T(1,128)} %bitcast.11, bf16[256,512]{1,0:T(8,128)(2,1)} %coeff_ref.1, bf16[512,64]{1,0:T(8,128)(2,1)} %bitcast.6, ...), custom_call_target="tpu_custom_call" | custom-call | tf_op jit(solution)/shard_map/pallas_call | solution.py:102
  15.8 0.8 %fusion = (bf16[16,512]{1,0:T(8,128)(2,1)S(1)}, bf16[16,512]{1,0:T(8,128)(2,1)S(1)}, bf16[16,512]{1,0:T(8,128)(2,1)S(1)}, bf16[16,512]{1,0:T(8,128)(2,1)S(1)}, b...) fusion(bf16[256,512]{1,0:T(8,128)(2,1)} %get-tuple-element.8), kind=kLoop, calls=%fused_computation.14 | loop fusion | bytes 262144 | tf_op jit(solution)/shard_map/slice | solution.py:245
  16.7 2.2 %collective-permute-start.5 = (bf16[16,512]{1,0:T(8,128)(2,1)S(1)}, bf16[16,512]{1,0:T(8,128)(2,1)S(1)}, u32[]{:S(2)}, u32[]{:S(2)}) collective-permute-start(bf16[16,512]{1,0:T(8,128)(2,1)S(1)} %get-tuple-element.9), channel_id=1, source_target_pairs={{0,448},{64,0},{128,64},{192,128},{256,192},{320,256},{384,320},{4... | collective-permute-start | bytes 49160 | tf_op jit(solution)/shard_map/ppermute | solution.py:207
  18.9 0.0 collective-permute-start.4
  18.9 4.3 %collective-permute-start = (bf16[48,512]{1,0:T(8,128)(2,1)S(1)}, bf16[48,512]{1,0:T(8,128)(2,1)S(1)}, u32[]{:S(2)}, u32[]{:S(2)}) collective-permute-start(bf16[48,512]{1,0:T(8,128)(2,1)S(1)} %pad_maximum_fusion), channel_id=1, source_target_pairs={{0,1},{1,2},{2,3},{3,4},{4,5},{5,6},{6,7},{7,8},{8,9},{9,10},{10,1... | collective-permute-start | bytes 147464 | tf_op jit(solution)/shard_map/ppermute | solution.py:207
  23.2 0.8 %slice.103 = bf16[32,512]{1,0:T(8,128)(2,1)S(1)} slice(bf16[256,512]{1,0:T(8,128)(2,1)} %get-tuple-element.8), slice={[80:112], [0:512]} | slice | bytes 65536 | tf_op jit(solution)/shard_map/slice | solution.py:241
  23.9 9.4 %collective-permute-start.1 = (bf16[48,512]{1,0:T(8,128)(2,1)S(1)}, bf16[48,512]{1,0:T(8,128)(2,1)S(1)}, u32[]{:S(2)}, u32[]{:S(2)}) collective-permute-start(bf16[48,512]{1,0:T(8,128)(2,1)S(1)} %pad_maximum_fusion.1), channel_id=1, source_target_pairs={{0,63},{1,0},{2,1},{3,2},{4,3},{5,4},{6,5},{7,6},{8,7},{9,8},{10,9... | collective-permute-start | bytes 147464 | tf_op jit(solution)/shard_map/ppermute | solution.py:207
  33.3 0.0 collective-permute-done
  33.3 1.7 %collective-permute-done.1 = bf16[48,512]{1,0:T(8,128)(2,1)S(1)} collective-permute-done((bf16[48,512]{1,0:T(8,128)(2,1)S(1)}, bf16[48,512]{1,0:T(8,128)(2,1)S(1)}, u32[]{:S(2)}, u32[]{:S(2)}) %collective-permute-start.1) | collective-permute-done | bytes 49184 | tf_op jit(solution)/shard_map/ppermute | solution.py:207
  35.0 3.8 %collective-permute-start.2 = (bf16[48,512]{1,0:T(8,128)(2,1)S(1)}, bf16[48,512]{1,0:T(8,128)(2,1)S(1)}, u32[]{:S(2)}, u32[]{:S(2)}) collective-permute-start(bf16[48,512]{1,0:T(8,128)(2,1)S(1)} %pad_maximum_fusion.2), channel_id=1, source_target_pairs={{0,8},{1,9},{2,10},{3,11},{4,12},{5,13},{6,14},{7,15},{8,16},{9,17... | collective-permute-start | bytes 147464 | tf_op jit(solution)/shard_map/ppermute | solution.py:207
  38.9 2.0 %collective-permute-start.3 = (bf16[48,512]{1,0:T(8,128)(2,1)S(1)}, bf16[48,512]{1,0:T(8,128)(2,1)S(1)}, u32[]{:S(2)}, u32[]{:S(2)}) collective-permute-start(bf16[48,512]{1,0:T(8,128)(2,1)S(1)} %pad_maximum_fusion.3), channel_id=1, source_target_pairs={{0,56},{1,57},{2,58},{3,59},{4,60},{5,61},{6,62},{7,63},{8,0},{9,1... | collective-permute-start | bytes 147464 | tf_op jit(solution)/shard_map/ppermute | solution.py:207
  40.9 0.1 collective-permute-done.2
  41.0 5.0 %collective-permute-done.3 = bf16[48,512]{1,0:T(8,128)(2,1)S(1)} collective-permute-done((bf16[48,512]{1,0:T(8,128)(2,1)S(1)}, bf16[48,512]{1,0:T(8,128)(2,1)S(1)}, u32[]{:S(2)}, u32[]{:S(2)}) %collective-permute-start.3) | collective-permute-done | bytes 49184 | tf_op jit(solution)/shard_map/ppermute | solution.py:207
  46.1 0.0 collective-permute-done.4
  46.1 0.0 collective-permute-done.5
  46.1 0.0 copy-start
  46.2 0.6 %copy-done = bf16[160,512]{1,0:T(8,128)(2,1)} copy-done((bf16[160,512]{1,0:T(8,128)(2,1)}, bf16[160,512]{1,0:T(8,128)(2,1)S(1)}, u32[]{:S(2)}) %copy-start) | copy-done | bytes 163864
  46.8 6.7 %shard_map.101 = f32[256,512]{1,0:T(8,128)} custom-call(f32[512,256]{1,0:T(8,128)} %get-tuple-element.7.own_ref, bf16[160,512]{1,0:T(8,128)(2,1)} %copy-done, s32[1,160]{1,0:T(1,128)} %list_ref.1, bf16[256,4096]{1,0:T(8,128)(2,1)} %inv_ref.1), custom_call_target="tpu_custom_call" | custom-call | tf_op jit(solution)/shard_map/pallas_call | solution.py:192
  (14 shorter events, 0.1 us)
Async XLA Ops:
  16.7 29.5 %collective-permute-start.5 = (bf16[16,512]{1,0:T(8,128)(2,1)S(1)}, bf16[16,512]{1,0:T(8,128)(2,1)S(1)}, u32[]{:S(2)}, u32[]{:S(2)}) collective-permute-start(bf16[16,512]{1,0:T(8,128)(2,1)S(1)} %get-tuple-element.9), channel_id=1, source_target_pairs={{0,448},{64,0},{128,64},{192,128},{256,192},{320,256},{384,320},{4... | collective-permute-start | bytes 49160 | tf_op jit(solution)/shard_map/ppermute | solution.py:207
  18.9 27.2 %collective-permute-start.4 = (bf16[16,512]{1,0:T(8,128)(2,1)S(1)}, bf16[16,512]{1,0:T(8,128)(2,1)S(1)}, u32[]{:S(2)}, u32[]{:S(2)}) collective-permute-start(bf16[16,512]{1,0:T(8,128)(2,1)S(1)} %get-tuple-element.10), channel_id=1, source_target_pairs={{0,64},{64,128},{128,192},{192,256},{256,320},{320,384},{384,448},... | collective-permute-start | bytes 49160 | tf_op jit(solution)/shard_map/ppermute | solution.py:207
  18.9 14.4 %collective-permute-start = (bf16[48,512]{1,0:T(8,128)(2,1)S(1)}, bf16[48,512]{1,0:T(8,128)(2,1)S(1)}, u32[]{:S(2)}, u32[]{:S(2)}) collective-permute-start(bf16[48,512]{1,0:T(8,128)(2,1)S(1)} %pad_maximum_fusion), channel_id=1, source_target_pairs={{0,1},{1,2},{2,3},{3,4},{4,5},{5,6},{6,7},{7,8},{8,9},{9,10},{10,1... | collective-permute-start | bytes 147464 | tf_op jit(solution)/shard_map/ppermute | solution.py:207
  23.9 11.1 %collective-permute-start.1 = (bf16[48,512]{1,0:T(8,128)(2,1)S(1)}, bf16[48,512]{1,0:T(8,128)(2,1)S(1)}, u32[]{:S(2)}, u32[]{:S(2)}) collective-permute-start(bf16[48,512]{1,0:T(8,128)(2,1)S(1)} %pad_maximum_fusion.1), channel_id=1, source_target_pairs={{0,63},{1,0},{2,1},{3,2},{4,3},{5,4},{6,5},{7,6},{8,7},{9,8},{10,9... | collective-permute-start | bytes 147464 | tf_op jit(solution)/shard_map/ppermute | solution.py:207
  35.0 6.0 %collective-permute-start.2 = (bf16[48,512]{1,0:T(8,128)(2,1)S(1)}, bf16[48,512]{1,0:T(8,128)(2,1)S(1)}, u32[]{:S(2)}, u32[]{:S(2)}) collective-permute-start(bf16[48,512]{1,0:T(8,128)(2,1)S(1)} %pad_maximum_fusion.2), channel_id=1, source_target_pairs={{0,8},{1,9},{2,10},{3,11},{4,12},{5,13},{6,14},{7,15},{8,16},{9,17... | collective-permute-start | bytes 147464 | tf_op jit(solution)/shard_map/ppermute | solution.py:207
  38.9 7.2 %collective-permute-start.3 = (bf16[48,512]{1,0:T(8,128)(2,1)S(1)}, bf16[48,512]{1,0:T(8,128)(2,1)S(1)}, u32[]{:S(2)}, u32[]{:S(2)}) collective-permute-start(bf16[48,512]{1,0:T(8,128)(2,1)S(1)} %pad_maximum_fusion.3), channel_id=1, source_target_pairs={{0,56},{1,57},{2,58},{3,59},{4,60},{5,61},{6,62},{7,63},{8,0},{9,1... | collective-permute-start | bytes 147464 | tf_op jit(solution)/shard_map/ppermute | solution.py:207
  46.1 0.7 %copy-start = (bf16[160,512]{1,0:T(8,128)(2,1)}, bf16[160,512]{1,0:T(8,128)(2,1)S(1)}, u32[]{:S(2)}) copy-start(bf16[160,512]{1,0:T(8,128)(2,1)S(1)} %constant_dynamic-update-slice_fusion.recv_ref) | copy-start | bytes 491524

commit v9 on v8

--- a/solution.py
+++ b/solution.py
@@ -226,7 +226,7 @@
     partner_count = 10
     slot_cap = slot_total // partner_count
     slots_pad = -(-slot_total // 128) * 128
-    block = min(512, tet_zone.shape[0])
+    block = min(2048, tet_zone.shape[0])
 
     bold = basis_old.reshape(tables * quad, basis)
     bnew = basis_new.reshape(tables * quad, basis)

time: 53.9 us -> 47.7 us (0.88)
  Pallas kernels: 22.5 us -> 16.4 us
    pallas_call x1, Pallas kernels: 15.8 us -> 9.71 us  [tet_partials(): pl.pallas_call(kernel, grid=(tet_count // block,), in_specs=[row_spec, ro...]
where the time goes in v9:
time: 47.7 us; the launch traced here: 47.4 us
  starting transfers between devices  21.7 us (45%)
  Pallas kernels  16.4 us (34%)
  waiting for transfers between devices  6.85 us (14%)
  local copies, waits for them, and re-layouts  2.3 us (5%)
    ppermute x6, starting transfers between devices, shifted(): return lax.ppermute(block, axis, route)  21.7 us
    pallas_call x1, Pallas kernels, tet_partials(): pl.pallas_call(kernel, grid=(tet_count // block,), in_specs=[row_spec, ro...  9.71 us
    ppermute x6, waiting for transfers between devices, shifted(): return lax.ppermute(block, axis, route)  6.85 us
    pallas_call x1, Pallas kernels, finish(): pl.pallas_call(kernel, out_shape=jax.ShapeDtypeStruct((zones, width), F32...  6.66 us
  transfers between devices with their start and end apart: 6, of which 3 were waited for; matrix products, arithmetic and copies ran while one was open for 2% of the time, Pallas kernels for 0%

profile of v9, /device:TPU:56, one launch (start us, length us, event | category | flops | bytes accessed | tf_op | source)
XLA Modules:
  0.0 47.4 jit_solution(15809239715709238051)
XLA Ops:
  0.0 9.7 %shard_map.100 = (f32[512,256]{1,0:T(8,128)}, bf16[256,512]{1,0:T(8,128)(2,1)}) custom-call(s32[1,2048]{1,0:T(1,128)} %bitcast.8, s32[1,2048]{1,0:T(1,128)} %bitcast.9, f32[1,2048]{1,0:T(1,128)} %bitcast.10, s32[1,2048]{1,0:T(1,128)} %bitcast.11, bf16[256,512]{1,0:T(8,128)(2,1)} %coeff_ref.1, bf16[512,64]{1,0:T(8,128)(2,1)} %bitcast.6, ...), custom_call_target="tpu_custom_call" | custom-call | tf_op jit(solution)/shard_map/pallas_call | solution.py:102
  9.7 0.8 %fusion = (bf16[16,512]{1,0:T(8,128)(2,1)S(1)}, bf16[16,512]{1,0:T(8,128)(2,1)S(1)}, bf16[16,512]{1,0:T(8,128)(2,1)S(1)}, bf16[16,512]{1,0:T(8,128)(2,1)S(1)}, b...) fusion(bf16[256,512]{1,0:T(8,128)(2,1)} %get-tuple-element.8), kind=kLoop, calls=%fused_computation.14 | loop fusion | bytes 262144 | tf_op jit(solution)/shard_map/slice | solution.py:245
  10.6 2.2 %collective-permute-start.5 = (bf16[16,512]{1,0:T(8,128)(2,1)S(1)}, bf16[16,512]{1,0:T(8,128)(2,1)S(1)}, u32[]{:S(2)}, u32[]{:S(2)}) collective-permute-start(bf16[16,512]{1,0:T(8,128)(2,1)S(1)} %get-tuple-element.9), channel_id=1, source_target_pairs={{0,448},{64,0},{128,64},{192,128},{256,192},{320,256},{384,320},{4... | collective-permute-start | bytes 49160 | tf_op jit(solution)/shard_map/ppermute | solution.py:207
  12.8 0.0 collective-permute-start.4
  12.8 4.3 %collective-permute-start = (bf16[48,512]{1,0:T(8,128)(2,1)S(1)}, bf16[48,512]{1,0:T(8,128)(2,1)S(1)}, u32[]{:S(2)}, u32[]{:S(2)}) collective-permute-start(bf16[48,512]{1,0:T(8,128)(2,1)S(1)} %pad_maximum_fusion), channel_id=1, source_target_pairs={{0,1},{1,2},{2,3},{3,4},{4,5},{5,6},{6,7},{7,8},{8,9},{9,10},{10,1... | collective-permute-start | bytes 147464 | tf_op jit(solution)/shard_map/ppermute | solution.py:207
  17.1 0.8 %slice.103 = bf16[32,512]{1,0:T(8,128)(2,1)S(1)} slice(bf16[256,512]{1,0:T(8,128)(2,1)} %get-tuple-element.8), slice={[80:112], [0:512]} | slice | bytes 65536 | tf_op jit(solution)/shard_map/slice | solution.py:241
  17.8 9.4 %collective-permute-start.1 = (bf16[48,512]{1,0:T(8,128)(2,1)S(1)}, bf16[48,512]{1,0:T(8,128)(2,1)S(1)}, u32[]{:S(2)}, u32[]{:S(2)}) collective-permute-start(bf16[48,512]{1,0:T(8,128)(2,1)S(1)} %pad_maximum_fusion.1), channel_id=1, source_target_pairs={{0,63},{1,0},{2,1},{3,2},{4,3},{5,4},{6,5},{7,6},{8,7},{9,8},{10,9... | collective-permute-start | bytes 147464 | tf_op jit(solution)/shard_map/ppermute | solution.py:207
  27.2 0.0 collective-permute-done
  27.2 1.7 %collective-permute-done.1 = bf16[48,512]{1,0:T(8,128)(2,1)S(1)} collective-permute-done((bf16[48,512]{1,0:T(8,128)(2,1)S(1)}, bf16[48,512]{1,0:T(8,128)(2,1)S(1)}, u32[]{:S(2)}, u32[]{:S(2)}) %collective-permute-start.1) | collective-permute-done | bytes 49184 | tf_op jit(solution)/shard_map/ppermute | solution.py:207
  28.9 3.8 %collective-permute-start.2 = (bf16[48,512]{1,0:T(8,128)(2,1)S(1)}, bf16[48,512]{1,0:T(8,128)(2,1)S(1)}, u32[]{:S(2)}, u32[]{:S(2)}) collective-permute-start(bf16[48,512]{1,0:T(8,128)(2,1)S(1)} %pad_maximum_fusion.2), channel_id=1, source_target_pairs={{0,8},{1,9},{2,10},{3,11},{4,12},{5,13},{6,14},{7,15},{8,16},{9,17... | collective-permute-start | bytes 147464 | tf_op jit(solution)/shard_map/ppermute | solution.py:207
  32.8 2.0 %collective-permute-start.3 = (bf16[48,512]{1,0:T(8,128)(2,1)S(1)}, bf16[48,512]{1,0:T(8,128)(2,1)S(1)}, u32[]{:S(2)}, u32[]{:S(2)}) collective-permute-start(bf16[48,512]{1,0:T(8,128)(2,1)S(1)} %pad_maximum_fusion.3), channel_id=1, source_target_pairs={{0,56},{1,57},{2,58},{3,59},{4,60},{5,61},{6,62},{7,63},{8,0},{9,1... | collective-permute-start | bytes 147464 | tf_op jit(solution)/shard_map/ppermute | solution.py:207
  34.8 0.1 collective-permute-done.2
  34.9 5.0 %collective-permute-done.3 = bf16[48,512]{1,0:T(8,128)(2,1)S(1)} collective-permute-done((bf16[48,512]{1,0:T(8,128)(2,1)S(1)}, bf16[48,512]{1,0:T(8,128)(2,1)S(1)}, u32[]{:S(2)}, u32[]{:S(2)}) %collective-permute-start.3) | collective-permute-done | bytes 49184 | tf_op jit(solution)/shard_map/ppermute | solution.py:207
  40.0 0.0 collective-permute-done.4
  40.0 0.0 collective-permute-done.5
  40.0 0.0 copy-start
  40.0 0.6 %copy-done = bf16[160,512]{1,0:T(8,128)(2,1)} copy-done((bf16[160,512]{1,0:T(8,128)(2,1)}, bf16[160,512]{1,0:T(8,128)(2,1)S(1)}, u32[]{:S(2)}) %copy-start) | copy-done | bytes 163864
  40.7 6.7 %shard_map.101 = f32[256,512]{1,0:T(8,128)} custom-call(f32[512,256]{1,0:T(8,128)} %get-tuple-element.7.own_ref, bf16[160,512]{1,0:T(8,128)(2,1)} %copy-done, s32[1,160]{1,0:T(1,128)} %list_ref.1, bf16[256,4096]{1,0:T(8,128)(2,1)} %inv_ref.1), custom_call_target="tpu_custom_call" | custom-call | tf_op jit(solution)/shard_map/pallas_call | solution.py:192
  (14 shorter events, 0.1 us)
Async XLA Ops:
  10.6 29.5 %collective-permute-start.5 = (bf16[16,512]{1,0:T(8,128)(2,1)S(1)}, bf16[16,512]{1,0:T(8,128)(2,1)S(1)}, u32[]{:S(2)}, u32[]{:S(2)}) collective-permute-start(bf16[16,512]{1,0:T(8,128)(2,1)S(1)} %get-tuple-element.9), channel_id=1, source_target_pairs={{0,448},{64,0},{128,64},{192,128},{256,192},{320,256},{384,320},{4... | collective-permute-start | bytes 49160 | tf_op jit(solution)/shard_map/ppermute | solution.py:207
  12.8 27.2 %collective-permute-start.4 = (bf16[16,512]{1,0:T(8,128)(2,1)S(1)}, bf16[16,512]{1,0:T(8,128)(2,1)S(1)}, u32[]{:S(2)}, u32[]{:S(2)}) collective-permute-start(bf16[16,512]{1,0:T(8,128)(2,1)S(1)} %get-tuple-element.10), channel_id=1, source_target_pairs={{0,64},{64,128},{128,192},{192,256},{256,320},{320,384},{384,448},... | collective-permute-start | bytes 49160 | tf_op jit(solution)/shard_map/ppermute | solution.py:207
  12.8 14.4 %collective-permute-start = (bf16[48,512]{1,0:T(8,128)(2,1)S(1)}, bf16[48,512]{1,0:T(8,128)(2,1)S(1)}, u32[]{:S(2)}, u32[]{:S(2)}) collective-permute-start(bf16[48,512]{1,0:T(8,128)(2,1)S(1)} %pad_maximum_fusion), channel_id=1, source_target_pairs={{0,1},{1,2},{2,3},{3,4},{4,5},{5,6},{6,7},{7,8},{8,9},{9,10},{10,1... | collective-permute-start | bytes 147464 | tf_op jit(solution)/shard_map/ppermute | solution.py:207
  17.8 11.1 %collective-permute-start.1 = (bf16[48,512]{1,0:T(8,128)(2,1)S(1)}, bf16[48,512]{1,0:T(8,128)(2,1)S(1)}, u32[]{:S(2)}, u32[]{:S(2)}) collective-permute-start(bf16[48,512]{1,0:T(8,128)(2,1)S(1)} %pad_maximum_fusion.1), channel_id=1, source_target_pairs={{0,63},{1,0},{2,1},{3,2},{4,3},{5,4},{6,5},{7,6},{8,7},{9,8},{10,9... | collective-permute-start | bytes 147464 | tf_op jit(solution)/shard_map/ppermute | solution.py:207
  28.9 6.0 %collective-permute-start.2 = (bf16[48,512]{1,0:T(8,128)(2,1)S(1)}, bf16[48,512]{1,0:T(8,128)(2,1)S(1)}, u32[]{:S(2)}, u32[]{:S(2)}) collective-permute-start(bf16[48,512]{1,0:T(8,128)(2,1)S(1)} %pad_maximum_fusion.2), channel_id=1, source_target_pairs={{0,8},{1,9},{2,10},{3,11},{4,12},{5,13},{6,14},{7,15},{8,16},{9,17... | collective-permute-start | bytes 147464 | tf_op jit(solution)/shard_map/ppermute | solution.py:207
  32.8 7.2 %collective-permute-start.3 = (bf16[48,512]{1,0:T(8,128)(2,1)S(1)}, bf16[48,512]{1,0:T(8,128)(2,1)S(1)}, u32[]{:S(2)}, u32[]{:S(2)}) collective-permute-start(bf16[48,512]{1,0:T(8,128)(2,1)S(1)} %pad_maximum_fusion.3), channel_id=1, source_target_pairs={{0,56},{1,57},{2,58},{3,59},{4,60},{5,61},{6,62},{7,63},{8,0},{9,1... | collective-permute-start | bytes 147464 | tf_op jit(solution)/shard_map/ppermute | solution.py:207
  40.0 0.7 %copy-start = (bf16[160,512]{1,0:T(8,128)(2,1)}, bf16[160,512]{1,0:T(8,128)(2,1)S(1)}, u32[]{:S(2)}) copy-start(bf16[160,512]{1,0:T(8,128)(2,1)S(1)} %constant_dynamic-update-slice_fusion.recv_ref) | copy-start | bytes 491524

commit v10 on v9

--- a/solution.py
+++ b/solution.py
@@ -13,7 +13,7 @@
 
 def tet_kernel(
     zone_ref, table_ref, vol_ref, dest_ref, coeff_ref, bold_ref, bnew_ref, qw_ref,
-    own_ref, slot_out_ref, ct_ref, boldc_ref, bnewc_ref, qwt_ref, slot_ref, mom_ref, spread_ref,
+    own_ref, slot_out_ref, ct_ref, boldc_ref, bnewc_ref, qwt_ref, slot_ref, mom_ref, spread_ref, mask_ref,
     *, tables, basis, fields, zones, slots_pad
 ):
     step = pl.program_id(0)
@@ -60,15 +60,16 @@
     scale = scale * vol_ref[...]
     boldc = boldc_ref[...]
     bnewc = bnewc_ref[...]
-    empty = jnp.zeros((basis, block), BF16)
+    for t in range(tables):
+        mask_ref[t * basis : (t + 1) * basis, :] = jnp.broadcast_to(masks[t].astype(BF16), (basis, block))
     for f in range(fields):
         piece = picked[f * basis : (f + 1) * basis, :]
         for t in range(tables):
-            spread_ref[t * basis : (t + 1) * basis, :] = jnp.where(masks[t], piece, empty)
+            spread_ref[t * basis : (t + 1) * basis, :] = piece * mask_ref[t * basis : (t + 1) * basis, :]
         values = jnp.dot(boldc, spread_ref[...], preferred_element_type=F32)
         weighted = (scale * values).astype(BF16)
         for t in range(tables):
-            spread_ref[t * basis : (t + 1) * basis, :] = jnp.where(masks[t], weighted, empty)
+            spread_ref[t * basis : (t + 1) * basis, :] = weighted * mask_ref[t * basis : (t + 1) * basis, :]
         mom_ref[f * basis : (f + 1) * basis, :] = jnp.dot(bnewc, spread_ref[...], preferred_element_type=F32)
     moments = mom_ref[...]
     high = moments.astype(BF16)
@@ -124,6 +125,7 @@
             pltpu.VMEM((basis, tables), F32),
             pltpu.VMEM((slots_pad, width), F32),
             pltpu.VMEM((width, block), F32),
+            pltpu.VMEM((tables * basis, block), BF16),
             pltpu.VMEM((tables * basis, block), BF16),
         ],
         compiler_params=pltpu.CompilerParams(dimension_semantics=("arbitrary",)),
@@ -164,8 +166,8 @@
             eye, inv_ref[:, c * chunk : (c + 1) * chunk], nt, preferred_element_type=F32
         )
 
-    chains = 4
-    pair = 2
+    chains = 2
+    pair = 4
 
     def body(jj, carry):
         rows = invt_ref.at[pl.ds(pl.multiple_of(jj * pair * basis, pair * basis), pair * basis), :]

time: 47.7 us -> 47.4 us (level)
  no operation moved by 1% of the time
where the time goes in v10:
time: 47.4 us; the launch traced here: 47 us
  starting transfers between devices  21.7 us (46%)
  Pallas kernels  16 us (34%)
  waiting for transfers between devices  6.85 us (14%)
  local copies, waits for them, and re-layouts  2.3 us (5%)
    ppermute x6, starting transfers between devices, shifted(): return lax.ppermute(block, axis, route)  21.7 us
    pallas_call x1, Pallas kernels, tet_partials(): pl.pallas_call(kernel, grid=(tet_count // block,), in_specs=[row_spec, ro...  9.68 us
    ppermute x6, waiting for transfers between devices, shifted(): return lax.ppermute(block, axis, route)  6.85 us
    pallas_call x1, Pallas kernels, finish(): pl.pallas_call(kernel, out_shape=jax.ShapeDtypeStruct((zones, width), F32...  6.35 us
  transfers between devices with their start and end apart: 6, of which 3 were waited for; matrix products, arithmetic and copies ran while one was open for 2% of the time, Pallas kernels for 0%

profile of v10, /device:TPU:56, one launch (start us, length us, event | category | flops | bytes accessed | tf_op | source)
XLA Modules:
  0.0 47.0 jit_solution(11604686114530834233)
XLA Ops:
  0.0 9.7 %shard_map.100 = (f32[512,256]{1,0:T(8,128)}, bf16[256,512]{1,0:T(8,128)(2,1)}) custom-call(s32[1,2048]{1,0:T(1,128)} %bitcast.8, s32[1,2048]{1,0:T(1,128)} %bitcast.9, f32[1,2048]{1,0:T(1,128)} %bitcast.10, s32[1,2048]{1,0:T(1,128)} %bitcast.11, bf16[256,512]{1,0:T(8,128)(2,1)} %coeff_ref.1, bf16[512,64]{1,0:T(8,128)(2,1)} %bitcast.6, ...), custom_call_target="tpu_custom_call" | custom-call | tf_op jit(solution)/shard_map/pallas_call | solution.py:103
  9.7 0.8 %fusion = (bf16[16,512]{1,0:T(8,128)(2,1)S(1)}, bf16[16,512]{1,0:T(8,128)(2,1)S(1)}, bf16[16,512]{1,0:T(8,128)(2,1)S(1)}, bf16[16,512]{1,0:T(8,128)(2,1)S(1)}, b...) fusion(bf16[256,512]{1,0:T(8,128)(2,1)} %get-tuple-element.8), kind=kLoop, calls=%fused_computation.14 | loop fusion | bytes 262144 | tf_op jit(solution)/shard_map/slice | solution.py:247
  10.5 2.2 %collective-permute-start.5 = (bf16[16,512]{1,0:T(8,128)(2,1)S(1)}, bf16[16,512]{1,0:T(8,128)(2,1)S(1)}, u32[]{:S(2)}, u32[]{:S(2)}) collective-permute-start(bf16[16,512]{1,0:T(8,128)(2,1)S(1)} %get-tuple-element.9), channel_id=1, source_target_pairs={{0,448},{64,0},{128,64},{192,128},{256,192},{320,256},{384,320},{4... | collective-permute-start | bytes 49160 | tf_op jit(solution)/shard_map/ppermute | solution.py:209
  12.7 0.0 collective-permute-start.4
  12.8 4.3 %collective-permute-start = (bf16[48,512]{1,0:T(8,128)(2,1)S(1)}, bf16[48,512]{1,0:T(8,128)(2,1)S(1)}, u32[]{:S(2)}, u32[]{:S(2)}) collective-permute-start(bf16[48,512]{1,0:T(8,128)(2,1)S(1)} %pad_maximum_fusion), channel_id=1, source_target_pairs={{0,1},{1,2},{2,3},{3,4},{4,5},{5,6},{6,7},{7,8},{8,9},{9,10},{10,1... | collective-permute-start | bytes 147464 | tf_op jit(solution)/shard_map/ppermute | solution.py:209
  17.0 0.8 %slice.103 = bf16[32,512]{1,0:T(8,128)(2,1)S(1)} slice(bf16[256,512]{1,0:T(8,128)(2,1)} %get-tuple-element.8), slice={[80:112], [0:512]} | slice | bytes 65536 | tf_op jit(solution)/shard_map/slice | solution.py:243
  17.8 9.4 %collective-permute-start.1 = (bf16[48,512]{1,0:T(8,128)(2,1)S(1)}, bf16[48,512]{1,0:T(8,128)(2,1)S(1)}, u32[]{:S(2)}, u32[]{:S(2)}) collective-permute-start(bf16[48,512]{1,0:T(8,128)(2,1)S(1)} %pad_maximum_fusion.1), channel_id=1, source_target_pairs={{0,63},{1,0},{2,1},{3,2},{4,3},{5,4},{6,5},{7,6},{8,7},{9,8},{10,9... | collective-permute-start | bytes 147464 | tf_op jit(solution)/shard_map/ppermute | solution.py:209
  27.2 0.0 collective-permute-done
  27.2 1.7 %collective-permute-done.1 = bf16[48,512]{1,0:T(8,128)(2,1)S(1)} collective-permute-done((bf16[48,512]{1,0:T(8,128)(2,1)S(1)}, bf16[48,512]{1,0:T(8,128)(2,1)S(1)}, u32[]{:S(2)}, u32[]{:S(2)}) %collective-permute-start.1) | collective-permute-done | bytes 49184 | tf_op jit(solution)/shard_map/ppermute | solution.py:209
  28.9 3.8 %collective-permute-start.2 = (bf16[48,512]{1,0:T(8,128)(2,1)S(1)}, bf16[48,512]{1,0:T(8,128)(2,1)S(1)}, u32[]{:S(2)}, u32[]{:S(2)}) collective-permute-start(bf16[48,512]{1,0:T(8,128)(2,1)S(1)} %pad_maximum_fusion.2), channel_id=1, source_target_pairs={{0,8},{1,9},{2,10},{3,11},{4,12},{5,13},{6,14},{7,15},{8,16},{9,17... | collective-permute-start | bytes 147464 | tf_op jit(solution)/shard_map/ppermute | solution.py:209
  32.7 2.0 %collective-permute-start.3 = (bf16[48,512]{1,0:T(8,128)(2,1)S(1)}, bf16[48,512]{1,0:T(8,128)(2,1)S(1)}, u32[]{:S(2)}, u32[]{:S(2)}) collective-permute-start(bf16[48,512]{1,0:T(8,128)(2,1)S(1)} %pad_maximum_fusion.3), channel_id=1, source_target_pairs={{0,56},{1,57},{2,58},{3,59},{4,60},{5,61},{6,62},{7,63},{8,0},{9,1... | collective-permute-start | bytes 147464 | tf_op jit(solution)/shard_map/ppermute | solution.py:209
  34.8 0.1 collective-permute-done.2
  34.9 5.0 %collective-permute-done.3 = bf16[48,512]{1,0:T(8,128)(2,1)S(1)} collective-permute-done((bf16[48,512]{1,0:T(8,128)(2,1)S(1)}, bf16[48,512]{1,0:T(8,128)(2,1)S(1)}, u32[]{:S(2)}, u32[]{:S(2)}) %collective-permute-start.3) | collective-permute-done | bytes 49184 | tf_op jit(solution)/shard_map/ppermute | solution.py:209
  40.0 0.0 collective-permute-done.4
  40.0 0.0 collective-permute-done.5
  40.0 0.0 copy-start
  40.0 0.6 %copy-done = bf16[160,512]{1,0:T(8,128)(2,1)} copy-done((bf16[160,512]{1,0:T(8,128)(2,1)}, bf16[160,512]{1,0:T(8,128)(2,1)S(1)}, u32[]{:S(2)}) %copy-start) | copy-done | bytes 163864
  40.7 6.3 %shard_map.101 = f32[256,512]{1,0:T(8,128)} custom-call(f32[512,256]{1,0:T(8,128)} %get-tuple-element.7.own_ref, bf16[160,512]{1,0:T(8,128)(2,1)} %copy-done, s32[1,160]{1,0:T(1,128)} %list_ref.1, bf16[256,4096]{1,0:T(8,128)(2,1)} %inv_ref.1), custom_call_target="tpu_custom_call" | custom-call | tf_op jit(solution)/shard_map/pallas_call | solution.py:194
  (14 shorter events, 0.1 us)
Async XLA Ops:
  10.5 29.5 %collective-permute-start.5 = (bf16[16,512]{1,0:T(8,128)(2,1)S(1)}, bf16[16,512]{1,0:T(8,128)(2,1)S(1)}, u32[]{:S(2)}, u32[]{:S(2)}) collective-permute-start(bf16[16,512]{1,0:T(8,128)(2,1)S(1)} %get-tuple-element.9), channel_id=1, source_target_pairs={{0,448},{64,0},{128,64},{192,128},{256,192},{320,256},{384,320},{4... | collective-permute-start | bytes 49160 | tf_op jit(solution)/shard_map/ppermute | solution.py:209
  12.7 27.2 %collective-permute-start.4 = (bf16[16,512]{1,0:T(8,128)(2,1)S(1)}, bf16[16,512]{1,0:T(8,128)(2,1)S(1)}, u32[]{:S(2)}, u32[]{:S(2)}) collective-permute-start(bf16[16,512]{1,0:T(8,128)(2,1)S(1)} %get-tuple-element.10), channel_id=1, source_target_pairs={{0,64},{64,128},{128,192},{192,256},{256,320},{320,384},{384,448},... | collective-permute-start | bytes 49160 | tf_op jit(solution)/shard_map/ppermute | solution.py:209
  12.8 14.4 %collective-permute-start = (bf16[48,512]{1,0:T(8,128)(2,1)S(1)}, bf16[48,512]{1,0:T(8,128)(2,1)S(1)}, u32[]{:S(2)}, u32[]{:S(2)}) collective-permute-start(bf16[48,512]{1,0:T(8,128)(2,1)S(1)} %pad_maximum_fusion), channel_id=1, source_target_pairs={{0,1},{1,2},{2,3},{3,4},{4,5},{5,6},{6,7},{7,8},{8,9},{9,10},{10,1... | collective-permute-start | bytes 147464 | tf_op jit(solution)/shard_map/ppermute | solution.py:209
  17.8 11.1 %collective-permute-start.1 = (bf16[48,512]{1,0:T(8,128)(2,1)S(1)}, bf16[48,512]{1,0:T(8,128)(2,1)S(1)}, u32[]{:S(2)}, u32[]{:S(2)}) collective-permute-start(bf16[48,512]{1,0:T(8,128)(2,1)S(1)} %pad_maximum_fusion.1), channel_id=1, source_target_pairs={{0,63},{1,0},{2,1},{3,2},{4,3},{5,4},{6,5},{7,6},{8,7},{9,8},{10,9... | collective-permute-start | bytes 147464 | tf_op jit(solution)/shard_map/ppermute | solution.py:209
  28.9 6.0 %collective-permute-start.2 = (bf16[48,512]{1,0:T(8,128)(2,1)S(1)}, bf16[48,512]{1,0:T(8,128)(2,1)S(1)}, u32[]{:S(2)}, u32[]{:S(2)}) collective-permute-start(bf16[48,512]{1,0:T(8,128)(2,1)S(1)} %pad_maximum_fusion.2), channel_id=1, source_target_pairs={{0,8},{1,9},{2,10},{3,11},{4,12},{5,13},{6,14},{7,15},{8,16},{9,17... | collective-permute-start | bytes 147464 | tf_op jit(solution)/shard_map/ppermute | solution.py:209
  32.7 7.2 %collective-permute-start.3 = (bf16[48,512]{1,0:T(8,128)(2,1)S(1)}, bf16[48,512]{1,0:T(8,128)(2,1)S(1)}, u32[]{:S(2)}, u32[]{:S(2)}) collective-permute-start(bf16[48,512]{1,0:T(8,128)(2,1)S(1)} %pad_maximum_fusion.3), channel_id=1, source_target_pairs={{0,56},{1,57},{2,58},{3,59},{4,60},{5,61},{6,62},{7,63},{8,0},{9,1... | collective-permute-start | bytes 147464 | tf_op jit(solution)/shard_map/ppermute | solution.py:209
  40.0 0.7 %copy-start = (bf16[160,512]{1,0:T(8,128)(2,1)}, bf16[160,512]{1,0:T(8,128)(2,1)S(1)}, u32[]{:S(2)}) copy-start(bf16[160,512]{1,0:T(8,128)(2,1)S(1)} %constant_dynamic-update-slice_fusion.recv_ref) | copy-start | bytes 491524

commit v11 on v9

--- a/solution.py
+++ b/solution.py
@@ -164,8 +164,8 @@
             eye, inv_ref[:, c * chunk : (c + 1) * chunk], nt, preferred_element_type=F32
         )
 
-    chains = 4
-    pair = 2
+    chains = 2
+    pair = 4
 
     def body(jj, carry):
         rows = invt_ref.at[pl.ds(pl.multiple_of(jj * pair * basis, pair * basis), pair * basis), :]

time: 47.7 us -> 47.4 us (level)
  no operation moved by 1% of the time
where the time goes in v11:
time: 47.4 us; the launch traced here: 47 us
  starting transfers between devices  21.7 us (46%)
  Pallas kernels  16 us (34%)
  waiting for transfers between devices  6.85 us (14%)
  local copies, waits for them, and re-layouts  2.3 us (5%)
    ppermute x6, starting transfers between devices, shifted(): return lax.ppermute(block, axis, route)  21.7 us
    pallas_call x1, Pallas kernels, tet_partials(): pl.pallas_call(kernel, grid=(tet_count // block,), in_specs=[row_spec, ro...  9.71 us
    ppermute x6, waiting for transfers between devices, shifted(): return lax.ppermute(block, axis, route)  6.85 us
    pallas_call x1, Pallas kernels, finish(): pl.pallas_call(kernel, out_shape=jax.ShapeDtypeStruct((zones, width), F32...  6.34 us
  transfers between devices with their start and end apart: 6, of which 3 were waited for; matrix products, arithmetic and copies ran while one was open for 2% of the time, Pallas kernels for 0%

profile of v11, /device:TPU:56, one launch (start us, length us, event | category | flops | bytes accessed | tf_op | source)
XLA Modules:
  0.0 47.0 jit_solution(17866205657012105802)
XLA Ops:
  0.0 9.7 %shard_map.100 = (f32[512,256]{1,0:T(8,128)}, bf16[256,512]{1,0:T(8,128)(2,1)}) custom-call(s32[1,2048]{1,0:T(1,128)} %bitcast.8, s32[1,2048]{1,0:T(1,128)} %bitcast.9, f32[1,2048]{1,0:T(1,128)} %bitcast.10, s32[1,2048]{1,0:T(1,128)} %bitcast.11, bf16[256,512]{1,0:T(8,128)(2,1)} %coeff_ref.1, bf16[512,64]{1,0:T(8,128)(2,1)} %bitcast.6, ...), custom_call_target="tpu_custom_call" | custom-call | tf_op jit(solution)/shard_map/pallas_call | solution.py:102
  9.7 0.8 %fusion = (bf16[16,512]{1,0:T(8,128)(2,1)S(1)}, bf16[16,512]{1,0:T(8,128)(2,1)S(1)}, bf16[16,512]{1,0:T(8,128)(2,1)S(1)}, bf16[16,512]{1,0:T(8,128)(2,1)S(1)}, b...) fusion(bf16[256,512]{1,0:T(8,128)(2,1)} %get-tuple-element.8), kind=kLoop, calls=%fused_computation.14 | loop fusion | bytes 262144 | tf_op jit(solution)/shard_map/slice | solution.py:245
  10.6 2.2 %collective-permute-start.5 = (bf16[16,512]{1,0:T(8,128)(2,1)S(1)}, bf16[16,512]{1,0:T(8,128)(2,1)S(1)}, u32[]{:S(2)}, u32[]{:S(2)}) collective-permute-start(bf16[16,512]{1,0:T(8,128)(2,1)S(1)} %get-tuple-element.9), channel_id=1, source_target_pairs={{0,448},{64,0},{128,64},{192,128},{256,192},{320,256},{384,320},{4... | collective-permute-start | bytes 49160 | tf_op jit(solution)/shard_map/ppermute | solution.py:207
  12.8 0.0 collective-permute-start.4
  12.8 4.3 %collective-permute-start = (bf16[48,512]{1,0:T(8,128)(2,1)S(1)}, bf16[48,512]{1,0:T(8,128)(2,1)S(1)}, u32[]{:S(2)}, u32[]{:S(2)}) collective-permute-start(bf16[48,512]{1,0:T(8,128)(2,1)S(1)} %pad_maximum_fusion), channel_id=1, source_target_pairs={{0,1},{1,2},{2,3},{3,4},{4,5},{5,6},{6,7},{7,8},{8,9},{9,10},{10,1... | collective-permute-start | bytes 147464 | tf_op jit(solution)/shard_map/ppermute | solution.py:207
  17.1 0.8 %slice.103 = bf16[32,512]{1,0:T(8,128)(2,1)S(1)} slice(bf16[256,512]{1,0:T(8,128)(2,1)} %get-tuple-element.8), slice={[80:112], [0:512]} | slice | bytes 65536 | tf_op jit(solution)/shard_map/slice | solution.py:241
  17.8 9.4 %collective-permute-start.1 = (bf16[48,512]{1,0:T(8,128)(2,1)S(1)}, bf16[48,512]{1,0:T(8,128)(2,1)S(1)}, u32[]{:S(2)}, u32[]{:S(2)}) collective-permute-start(bf16[48,512]{1,0:T(8,128)(2,1)S(1)} %pad_maximum_fusion.1), channel_id=1, source_target_pairs={{0,63},{1,0},{2,1},{3,2},{4,3},{5,4},{6,5},{7,6},{8,7},{9,8},{10,9... | collective-permute-start | bytes 147464 | tf_op jit(solution)/shard_map/ppermute | solution.py:207
  27.2 0.0 collective-permute-done
  27.2 1.7 %collective-permute-done.1 = bf16[48,512]{1,0:T(8,128)(2,1)S(1)} collective-permute-done((bf16[48,512]{1,0:T(8,128)(2,1)S(1)}, bf16[48,512]{1,0:T(8,128)(2,1)S(1)}, u32[]{:S(2)}, u32[]{:S(2)}) %collective-permute-start.1) | collective-permute-done | bytes 49184 | tf_op jit(solution)/shard_map/ppermute | solution.py:207
  28.9 3.8 %collective-permute-start.2 = (bf16[48,512]{1,0:T(8,128)(2,1)S(1)}, bf16[48,512]{1,0:T(8,128)(2,1)S(1)}, u32[]{:S(2)}, u32[]{:S(2)}) collective-permute-start(bf16[48,512]{1,0:T(8,128)(2,1)S(1)} %pad_maximum_fusion.2), channel_id=1, source_target_pairs={{0,8},{1,9},{2,10},{3,11},{4,12},{5,13},{6,14},{7,15},{8,16},{9,17... | collective-permute-start | bytes 147464 | tf_op jit(solution)/shard_map/ppermute | solution.py:207
  32.8 2.0 %collective-permute-start.3 = (bf16[48,512]{1,0:T(8,128)(2,1)S(1)}, bf16[48,512]{1,0:T(8,128)(2,1)S(1)}, u32[]{:S(2)}, u32[]{:S(2)}) collective-permute-start(bf16[48,512]{1,0:T(8,128)(2,1)S(1)} %pad_maximum_fusion.3), channel_id=1, source_target_pairs={{0,56},{1,57},{2,58},{3,59},{4,60},{5,61},{6,62},{7,63},{8,0},{9,1... | collective-permute-start | bytes 147464 | tf_op jit(solution)/shard_map/ppermute | solution.py:207
  34.8 0.1 collective-permute-done.2
  34.9 5.0 %collective-permute-done.3 = bf16[48,512]{1,0:T(8,128)(2,1)S(1)} collective-permute-done((bf16[48,512]{1,0:T(8,128)(2,1)S(1)}, bf16[48,512]{1,0:T(8,128)(2,1)S(1)}, u32[]{:S(2)}, u32[]{:S(2)}) %collective-permute-start.3) | collective-permute-done | bytes 49184 | tf_op jit(solution)/shard_map/ppermute | solution.py:207
  40.0 0.0 collective-permute-done.4
  40.0 0.0 collective-permute-done.5
  40.0 0.0 copy-start
  40.0 0.6 %copy-done = bf16[160,512]{1,0:T(8,128)(2,1)} copy-done((bf16[160,512]{1,0:T(8,128)(2,1)}, bf16[160,512]{1,0:T(8,128)(2,1)S(1)}, u32[]{:S(2)}) %copy-start) | copy-done | bytes 163864
  40.7 6.3 %shard_map.101 = f32[256,512]{1,0:T(8,128)} custom-call(f32[512,256]{1,0:T(8,128)} %get-tuple-element.7.own_ref, bf16[160,512]{1,0:T(8,128)(2,1)} %copy-done, s32[1,160]{1,0:T(1,128)} %list_ref.1, bf16[256,4096]{1,0:T(8,128)(2,1)} %inv_ref.1), custom_call_target="tpu_custom_call" | custom-call | tf_op jit(solution)/shard_map/pallas_call | solution.py:192
  (14 shorter events, 0.1 us)
Async XLA Ops:
  10.6 29.5 %collective-permute-start.5 = (bf16[16,512]{1,0:T(8,128)(2,1)S(1)}, bf16[16,512]{1,0:T(8,128)(2,1)S(1)}, u32[]{:S(2)}, u32[]{:S(2)}) collective-permute-start(bf16[16,512]{1,0:T(8,128)(2,1)S(1)} %get-tuple-element.9), channel_id=1, source_target_pairs={{0,448},{64,0},{128,64},{192,128},{256,192},{320,256},{384,320},{4... | collective-permute-start | bytes 49160 | tf_op jit(solution)/shard_map/ppermute | solution.py:207
  12.8 27.2 %collective-permute-start.4 = (bf16[16,512]{1,0:T(8,128)(2,1)S(1)}, bf16[16,512]{1,0:T(8,128)(2,1)S(1)}, u32[]{:S(2)}, u32[]{:S(2)}) collective-permute-start(bf16[16,512]{1,0:T(8,128)(2,1)S(1)} %get-tuple-element.10), channel_id=1, source_target_pairs={{0,64},{64,128},{128,192},{192,256},{256,320},{320,384},{384,448},... | collective-permute-start | bytes 49160 | tf_op jit(solution)/shard_map/ppermute | solution.py:207
  12.8 14.4 %collective-permute-start = (bf16[48,512]{1,0:T(8,128)(2,1)S(1)}, bf16[48,512]{1,0:T(8,128)(2,1)S(1)}, u32[]{:S(2)}, u32[]{:S(2)}) collective-permute-start(bf16[48,512]{1,0:T(8,128)(2,1)S(1)} %pad_maximum_fusion), channel_id=1, source_target_pairs={{0,1},{1,2},{2,3},{3,4},{4,5},{5,6},{6,7},{7,8},{8,9},{9,10},{10,1... | collective-permute-start | bytes 147464 | tf_op jit(solution)/shard_map/ppermute | solution.py:207
  17.8 11.1 %collective-permute-start.1 = (bf16[48,512]{1,0:T(8,128)(2,1)S(1)}, bf16[48,512]{1,0:T(8,128)(2,1)S(1)}, u32[]{:S(2)}, u32[]{:S(2)}) collective-permute-start(bf16[48,512]{1,0:T(8,128)(2,1)S(1)} %pad_maximum_fusion.1), channel_id=1, source_target_pairs={{0,63},{1,0},{2,1},{3,2},{4,3},{5,4},{6,5},{7,6},{8,7},{9,8},{10,9... | collective-permute-start | bytes 147464 | tf_op jit(solution)/shard_map/ppermute | solution.py:207
  28.9 6.0 %collective-permute-start.2 = (bf16[48,512]{1,0:T(8,128)(2,1)S(1)}, bf16[48,512]{1,0:T(8,128)(2,1)S(1)}, u32[]{:S(2)}, u32[]{:S(2)}) collective-permute-start(bf16[48,512]{1,0:T(8,128)(2,1)S(1)} %pad_maximum_fusion.2), channel_id=1, source_target_pairs={{0,8},{1,9},{2,10},{3,11},{4,12},{5,13},{6,14},{7,15},{8,16},{9,17... | collective-permute-start | bytes 147464 | tf_op jit(solution)/shard_map/ppermute | solution.py:207
  32.8 7.2 %collective-permute-start.3 = (bf16[48,512]{1,0:T(8,128)(2,1)S(1)}, bf16[48,512]{1,0:T(8,128)(2,1)S(1)}, u32[]{:S(2)}, u32[]{:S(2)}) collective-permute-start(bf16[48,512]{1,0:T(8,128)(2,1)S(1)} %pad_maximum_fusion.3), channel_id=1, source_target_pairs={{0,56},{1,57},{2,58},{3,59},{4,60},{5,61},{6,62},{7,63},{8,0},{9,1... | collective-permute-start | bytes 147464 | tf_op jit(solution)/shard_map/ppermute | solution.py:207
  40.0 0.7 %copy-start = (bf16[160,512]{1,0:T(8,128)(2,1)}, bf16[160,512]{1,0:T(8,128)(2,1)S(1)}, u32[]{:S(2)}) copy-start(bf16[160,512]{1,0:T(8,128)(2,1)S(1)} %constant_dynamic-update-slice_fusion.recv_ref) | copy-start | bytes 491524

commit v12 on v10

--- a/solution.py
+++ b/solution.py
@@ -203,6 +203,21 @@
     )(own_t, received, recv_row, inv_mass)
 
 
+def split_shift(up_block, down_block, axis, distance, far_up, far_down):
+    count = lax.axis_size(axis)
+    up_near = [(i, (i + distance) % count) for i in range(count) if not far_up(i)]
+    down_near = [(i, (i - distance) % count) for i in range(count) if not far_down(i)]
+    far = [(i, (i + distance) % count) for i in range(count) if far_up(i)]
+    far += [(i, (i - distance) % count) for i in range(count) if far_down(i)]
+    here = lax.axis_index(axis)
+    near_left = lax.ppermute(up_block, axis, up_near)
+    near_right = lax.ppermute(down_block, axis, down_near)
+    wrapped = lax.ppermute(jnp.where(far_up(here), up_block, down_block), axis, far)
+    from_left = jnp.where(far_up((here - distance) % count), wrapped, near_left)
+    from_right = jnp.where(far_down((here + distance) % count), wrapped, near_right)
+    return from_left, from_right
+
+
 def shifted(block, axis, distance):
     count = lax.axis_size(axis)
     route = [(i, (i + distance) % count) for i in range(count)]
@@ -241,14 +256,20 @@
     face_side = 1 << (lane_count.bit_length() - 1) // 2
     going_up = jnp.concatenate([outgoing[0], outgoing[4], outgoing[7]], axis=0)
     going_down = jnp.concatenate([outgoing[1], outgoing[5], outgoing[6]], axis=0)
-    from_left = shifted(going_up, "yz", 1).reshape(3, slot_cap, row_width)
-    from_right = shifted(going_down, "yz", -1).reshape(3, slot_cap, row_width)
+    from_left, from_right = split_shift(
+        going_up, going_down, "yz", 1, lambda i: i % face_side == face_side - 1, lambda i: i % face_side == 0
+    )
+    from_left = from_left.reshape(3, slot_cap, row_width)
+    from_right = from_right.reshape(3, slot_cap, row_width)
     from_back = shifted(outgoing[8], "gx", 1)
     from_front = shifted(outgoing[9], "gx", -1)
     upward = jnp.concatenate([outgoing[2], from_left[1], from_right[2]], axis=0)
     downward = jnp.concatenate([outgoing[3], from_left[2], from_right[1]], axis=0)
-    came_up = shifted(upward, "yz", face_side).reshape(3, slot_cap, row_width)
-    came_down = shifted(downward, "yz", -face_side).reshape(3, slot_cap, row_width)
+    came_up, came_down = split_shift(
+        upward, downward, "yz", face_side, lambda i: i >= lane_count - face_side, lambda i: i < face_side
+    )
+    came_up = came_up.reshape(3, slot_cap, row_width)
+    came_down = came_down.reshape(3, slot_cap, row_width)
     received = jnp.concatenate(
         [
             from_left[0],

time: 47.4 us -> 50.6 us (1.068)
  the two profiles are of different devices: /device:TPU:56 before, /device:TPU:64 now
where the time goes in v12:
time: 50.6 us; the launch traced here: 50.2 us
  starting transfers between devices  17.8 us (35%)
  Pallas kernels  16 us (32%)
  waiting for transfers between devices  13.7 us (27%)
  local copies, waits for them, and re-layouts  2.3 us (5%)
    ppermute x2, waiting for transfers between devices, split_shift(): near_left = lax.ppermute(up_block, axis, up_near)  10.7 us
    pallas_call x1, Pallas kernels, tet_partials(): pl.pallas_call(kernel, grid=(tet_count // block,), in_specs=[row_spec, ro...  9.68 us
    ppermute x2, starting transfers between devices, split_shift(): near_right = lax.ppermute(down_block, axis, down_near)  8.2 us
    pallas_call x1, Pallas kernels, finish(): pl.pallas_call(kernel, out_shape=jax.ShapeDtypeStruct((zones, width), F32...  6.34 us
    ppermute x2, starting transfers between devices, split_shift(): lax.ppermute(jnp.where(far_up(here), up_block, down_block), axis, far)  5.88 us
    ppermute x2, starting transfers between devices, split_shift(): near_left = lax.ppermute(up_block, axis, up_near)  3.21 us
    ppermute x2, waiting for transfers between devices, shifted(): return lax.ppermute(block, axis, route)  2.78 us
  transfers between devices with their start and end apart: 8, of which 4 were waited for; matrix products, arithmetic and copies ran while one was open for 0% of the time, Pallas kernels for 0%

profile of v12, /device:TPU:64, one launch (start us, length us, event | category | flops | bytes accessed | tf_op | source)
XLA Modules:
  0.0 50.2 jit_solution(14576133999511755465)
XLA Ops:
  0.0 9.7 %shard_map.100 = (f32[512,256]{1,0:T(8,128)}, bf16[256,512]{1,0:T(8,128)(2,1)}) custom-call(s32[1,2048]{1,0:T(1,128)} %bitcast.8, s32[1,2048]{1,0:T(1,128)} %bitcast.9, f32[1,2048]{1,0:T(1,128)} %bitcast.10, s32[1,2048]{1,0:T(1,128)} %bitcast.11, bf16[256,512]{1,0:T(8,128)(2,1)} %coeff_ref.1, bf16[512,64]{1,0:T(8,128)(2,1)} %bitcast.6, ...), custom_call_target="tpu_custom_call" | custom-call | tf_op jit(solution)/shard_map/pallas_call | solution.py:103
  9.7 0.8 %slice.102 = bf16[32,512]{1,0:T(8,128)(2,1)S(1)} slice(bf16[256,512]{1,0:T(8,128)(2,1)} %get-tuple-element.8), slice={[80:112], [0:512]} | slice | bytes 65536 | tf_op jit(solution)/shard_map/slice | solution.py:258
  10.4 0.8 %fusion = (bf16[16,512]{1,0:T(8,128)(2,1)S(1)}, bf16[16,512]{1,0:T(8,128)(2,1)S(1)}, bf16[16,512]{1,0:T(8,128)(2,1)S(1)}, bf16[16,512]{1,0:T(8,128)(2,1)S(1)}, b...) fusion(bf16[256,512]{1,0:T(8,128)(2,1)} %get-tuple-element.8), kind=kLoop, calls=%fused_computation.20 | loop fusion | bytes 262144 | tf_op jit(solution)/shard_map/slice | solution.py:265
  11.3 6.9 %collective-permute-start.2 = (bf16[48,512]{1,0:T(8,128)(2,1)S(1)}, bf16[48,512]{1,0:T(8,128)(2,1)S(1)}, u32[]{:S(2)}, u32[]{:S(2)}) collective-permute-start(bf16[48,512]{1,0:T(8,128)(2,1)S(1)} %get-tuple-element.30), channel_id=1, source_target_pairs={{1,0},{2,1},{3,2},{4,3},{5,4},{6,5},{7,6},{9,8},{10,9},{11,10},{12... | collective-permute-start | bytes 147464 | tf_op jit(solution)/shard_map/ppermute | solution.py:214
  18.2 0.7 %collective-permute-start = (bf16[48,512]{1,0:T(8,128)(2,1)S(1)}, bf16[48,512]{1,0:T(8,128)(2,1)S(1)}, u32[]{:S(2)}, u32[]{:S(2)}) collective-permute-start(bf16[48,512]{1,0:T(8,128)(2,1)S(1)} %get-tuple-element.31), channel_id=1, source_target_pairs={{7,8},{15,16},{23,24},{31,32},{39,40},{47,48},{55,56},{63,0},{0,63... | collective-permute-start | bytes 147464 | tf_op jit(solution)/shard_map/ppermute | solution.py:215
  18.9 1.9 %collective-permute-start.1 = (bf16[48,512]{1,0:T(8,128)(2,1)S(1)}, bf16[48,512]{1,0:T(8,128)(2,1)S(1)}, u32[]{:S(2)}, u32[]{:S(2)}) collective-permute-start(bf16[48,512]{1,0:T(8,128)(2,1)S(1)} %get-tuple-element.32), channel_id=1, source_target_pairs={{0,1},{1,2},{2,3},{3,4},{4,5},{5,6},{6,7},{8,9},{9,10},{10,11},{11... | collective-permute-start | bytes 147464 | tf_op jit(solution)/shard_map/ppermute | solution.py:213
  20.9 0.0 collective-permute-done.2
  20.9 0.0 collective-permute-done
  20.9 9.7 %collective-permute-done.1 = bf16[48,512]{1,0:T(8,128)(2,1)S(1)} collective-permute-done((bf16[48,512]{1,0:T(8,128)(2,1)S(1)}, bf16[48,512]{1,0:T(8,128)(2,1)S(1)}, u32[]{:S(2)}, u32[]{:S(2)}) %collective-permute-start.1) | collective-permute-done | bytes 49184 | tf_op jit(solution)/shard_map/ppermute | solution.py:213
  30.7 1.3 %collective-permute-start.5 = (bf16[48,512]{1,0:T(8,128)(2,1)S(1)}, bf16[48,512]{1,0:T(8,128)(2,1)S(1)}, u32[]{:S(2)}, u32[]{:S(2)}) collective-permute-start(bf16[48,512]{1,0:T(8,128)(2,1)S(1)} %get-tuple-element.19), channel_id=1, source_target_pairs={{8,0},{9,1},{10,2},{11,3},{12,4},{13,5},{14,6},{15,7},{16,8},{17,9... | collective-permute-start | bytes 147464 | tf_op jit(solution)/shard_map/ppermute | solution.py:214
  32.0 5.2 %collective-permute-start.3 = (bf16[48,512]{1,0:T(8,128)(2,1)S(1)}, bf16[48,512]{1,0:T(8,128)(2,1)S(1)}, u32[]{:S(2)}, u32[]{:S(2)}) collective-permute-start(bf16[48,512]{1,0:T(8,128)(2,1)S(1)} %get-tuple-element.20), channel_id=1, source_target_pairs={{56,0},{57,1},{58,2},{59,3},{60,4},{61,5},{62,6},{63,7},{0,56},{1,... | collective-permute-start | bytes 147464 | tf_op jit(solution)/shard_map/ppermute | solution.py:215
  37.3 1.3 %collective-permute-start.4 = (bf16[48,512]{1,0:T(8,128)(2,1)S(1)}, bf16[48,512]{1,0:T(8,128)(2,1)S(1)}, u32[]{:S(2)}, u32[]{:S(2)}) collective-permute-start(bf16[48,512]{1,0:T(8,128)(2,1)S(1)} %get-tuple-element.21), channel_id=1, source_target_pairs={{0,8},{1,9},{2,10},{3,11},{4,12},{5,13},{6,14},{7,15},{8,16},{9,17... | collective-permute-start | bytes 147464 | tf_op jit(solution)/shard_map/ppermute | solution.py:213
  38.6 0.2 collective-permute-start.7
  38.8 0.3 collective-permute-start.6
  39.1 0.0 collective-permute-done.5
  39.1 0.2 collective-permute-done.3
  39.3 1.0 %collective-permute-done.4 = bf16[48,512]{1,0:T(8,128)(2,1)S(1)} collective-permute-done((bf16[48,512]{1,0:T(8,128)(2,1)S(1)}, bf16[48,512]{1,0:T(8,128)(2,1)S(1)}, u32[]{:S(2)}, u32[]{:S(2)}) %collective-permute-start.4) | collective-permute-done | bytes 49184 | tf_op jit(solution)/shard_map/ppermute | solution.py:213
  40.4 2.8 %collective-permute-done.6 = bf16[16,512]{1,0:T(8,128)(2,1)S(1)} collective-permute-done((bf16[16,512]{1,0:T(8,128)(2,1)S(1)}, bf16[16,512]{1,0:T(8,128)(2,1)S(1)}, u32[]{:S(2)}, u32[]{:S(2)}) %collective-permute-start.6) | collective-permute-done | bytes 16416 | tf_op jit(solution)/shard_map/ppermute | solution.py:224
  43.2 0.0 collective-permute-done.7
  43.2 0.0 copy-start
  43.2 0.7 %copy-done = bf16[160,512]{1,0:T(8,128)(2,1)} copy-done((bf16[160,512]{1,0:T(8,128)(2,1)}, bf16[160,512]{1,0:T(8,128)(2,1)S(1)}, u32[]{:S(2)}) %copy-start) | copy-done | bytes 163864
  43.8 6.3 %shard_map.101 = f32[256,512]{1,0:T(8,128)} custom-call(f32[512,256]{1,0:T(8,128)} %get-tuple-element.7.own_ref, bf16[160,512]{1,0:T(8,128)(2,1)} %copy-done, s32[1,160]{1,0:T(1,128)} %list_ref.1, bf16[256,4096]{1,0:T(8,128)(2,1)} %inv_ref.1), custom_call_target="tpu_custom_call" | custom-call | tf_op jit(solution)/shard_map/pallas_call | solution.py:194
  (14 shorter events, 0.1 us)
Async XLA Ops:
  11.3 9.6 %collective-permute-start.2 = (bf16[48,512]{1,0:T(8,128)(2,1)S(1)}, bf16[48,512]{1,0:T(8,128)(2,1)S(1)}, u32[]{:S(2)}, u32[]{:S(2)}) collective-permute-start(bf16[48,512]{1,0:T(8,128)(2,1)S(1)} %get-tuple-element.30), channel_id=1, source_target_pairs={{1,0},{2,1},{3,2},{4,3},{5,4},{6,5},{7,6},{9,8},{10,9},{11,10},{12... | collective-permute-start | bytes 147464 | tf_op jit(solution)/shard_map/ppermute | solution.py:214
  18.2 2.7 %collective-permute-start = (bf16[48,512]{1,0:T(8,128)(2,1)S(1)}, bf16[48,512]{1,0:T(8,128)(2,1)S(1)}, u32[]{:S(2)}, u32[]{:S(2)}) collective-permute-start(bf16[48,512]{1,0:T(8,128)(2,1)S(1)} %get-tuple-element.31), channel_id=1, source_target_pairs={{7,8},{15,16},{23,24},{31,32},{39,40},{47,48},{55,56},{63,0},{0,63... | collective-permute-start | bytes 147464 | tf_op jit(solution)/shard_map/ppermute | solution.py:215
  18.9 11.7 %collective-permute-start.1 = (bf16[48,512]{1,0:T(8,128)(2,1)S(1)}, bf16[48,512]{1,0:T(8,128)(2,1)S(1)}, u32[]{:S(2)}, u32[]{:S(2)}) collective-permute-start(bf16[48,512]{1,0:T(8,128)(2,1)S(1)} %get-tuple-element.32), channel_id=1, source_target_pairs={{0,1},{1,2},{2,3},{3,4},{4,5},{5,6},{6,7},{8,9},{9,10},{10,11},{11... | collective-permute-start | bytes 147464 | tf_op jit(solution)/shard_map/ppermute | solution.py:213
  30.7 8.4 %collective-permute-start.5 = (bf16[48,512]{1,0:T(8,128)(2,1)S(1)}, bf16[48,512]{1,0:T(8,128)(2,1)S(1)}, u32[]{:S(2)}, u32[]{:S(2)}) collective-permute-start(bf16[48,512]{1,0:T(8,128)(2,1)S(1)} %get-tuple-element.19), channel_id=1, source_target_pairs={{8,0},{9,1},{10,2},{11,3},{12,4},{13,5},{14,6},{15,7},{16,8},{17,9... | collective-permute-start | bytes 147464 | tf_op jit(solution)/shard_map/ppermute | solution.py:214
  32.0 7.3 %collective-permute-start.3 = (bf16[48,512]{1,0:T(8,128)(2,1)S(1)}, bf16[48,512]{1,0:T(8,128)(2,1)S(1)}, u32[]{:S(2)}, u32[]{:S(2)}) collective-permute-start(bf16[48,512]{1,0:T(8,128)(2,1)S(1)} %get-tuple-element.20), channel_id=1, source_target_pairs={{56,0},{57,1},{58,2},{59,3},{60,4},{61,5},{62,6},{63,7},{0,56},{1,... | collective-permute-start | bytes 147464 | tf_op jit(solution)/shard_map/ppermute | solution.py:215
  37.3 3.0 %collective-permute-start.4 = (bf16[48,512]{1,0:T(8,128)(2,1)S(1)}, bf16[48,512]{1,0:T(8,128)(2,1)S(1)}, u32[]{:S(2)}, u32[]{:S(2)}) collective-permute-start(bf16[48,512]{1,0:T(8,128)(2,1)S(1)} %get-tuple-element.21), channel_id=1, source_target_pairs={{0,8},{1,9},{2,10},{3,11},{4,12},{5,13},{6,14},{7,15},{8,16},{9,17... | collective-permute-start | bytes 147464 | tf_op jit(solution)/shard_map/ppermute | solution.py:213
  38.6 4.6 %collective-permute-start.7 = (bf16[16,512]{1,0:T(8,128)(2,1)S(1)}, bf16[16,512]{1,0:T(8,128)(2,1)S(1)}, u32[]{:S(2)}, u32[]{:S(2)}) collective-permute-start(bf16[16,512]{1,0:T(8,128)(2,1)S(1)} %get-tuple-element.9), channel_id=1, source_target_pairs={{0,448},{64,0},{128,64},{192,128},{256,192},{320,256},{384,320},{4... | collective-permute-start | bytes 49160 | tf_op jit(solution)/shard_map/ppermute | solution.py:224
  38.8 4.4 %collective-permute-start.6 = (bf16[16,512]{1,0:T(8,128)(2,1)S(1)}, bf16[16,512]{1,0:T(8,128)(2,1)S(1)}, u32[]{:S(2)}, u32[]{:S(2)}) collective-permute-start(bf16[16,512]{1,0:T(8,128)(2,1)S(1)} %get-tuple-element.10), channel_id=1, source_target_pairs={{0,64},{64,128},{128,192},{192,256},{256,320},{320,384},{384,448},... | collective-permute-start | bytes 49160 | tf_op jit(solution)/shard_map/ppermute | solution.py:224
  43.2 0.7 %copy-start = (bf16[160,512]{1,0:T(8,128)(2,1)}, bf16[160,512]{1,0:T(8,128)(2,1)S(1)}, u32[]{:S(2)}) copy-start(bf16[160,512]{1,0:T(8,128)(2,1)S(1)} %constant_dynamic-update-slice_fusion.recv_ref) | copy-start | bytes 491524

commit v13 on v10

--- a/solution.py
+++ b/solution.py
@@ -14,7 +14,7 @@
 def tet_kernel(
     zone_ref, table_ref, vol_ref, dest_ref, coeff_ref, bold_ref, bnew_ref, qw_ref,
     own_ref, slot_out_ref, ct_ref, boldc_ref, bnewc_ref, qwt_ref, slot_ref, mom_ref, spread_ref, mask_ref,
-    *, tables, basis, fields, zones, slots_pad
+    *, tables, basis, fields, zones, slots_pad, single
 ):
     step = pl.program_id(0)
     nt = (((1,), (1,)), ((), ()))
@@ -22,8 +22,9 @@
 
     @pl.when(step == 0)
     def _():
-        own_ref[...] = jnp.zeros_like(own_ref)
-        slot_ref[...] = jnp.zeros_like(slot_ref)
+        if not single:
+            own_ref[...] = jnp.zeros_like(own_ref)
+            slot_ref[...] = jnp.zeros_like(slot_ref)
         row = lax.broadcasted_iota(jnp.int32, (width, width), 0)
         col = lax.broadcasted_iota(jnp.int32, (width, width), 1)
         shuffle = (col == (row % basis) * fields + row // basis).astype(BF16)
@@ -76,17 +77,23 @@
     low = (moments - high.astype(F32)).astype(BF16)
     dest = dest_ref[...]
     own_hot = (lax.broadcasted_iota(jnp.int32, (zones, block), 0) == dest).astype(BF16)
-    own_ref[...] += lax.dot_general(high, own_hot, nt, preferred_element_type=F32) + lax.dot_general(
+    own_part = lax.dot_general(high, own_hot, nt, preferred_element_type=F32) + lax.dot_general(
         low, own_hot, nt, preferred_element_type=F32
     )
     slot_hot = (lax.broadcasted_iota(jnp.int32, (slots_pad, block), 0) + zones == dest).astype(BF16)
-    slot_ref[...] += lax.dot_general(slot_hot, high, nt, preferred_element_type=F32) + lax.dot_general(
+    slot_part = lax.dot_general(slot_hot, high, nt, preferred_element_type=F32) + lax.dot_general(
         slot_hot, low, nt, preferred_element_type=F32
     )
-
-    @pl.when(step == pl.num_programs(0) - 1)
-    def _():
-        slot_out_ref[...] = slot_ref[...].astype(BF16)
+    if single:
+        own_ref[...] = own_part
+        slot_out_ref[...] = slot_part.astype(BF16)
+    else:
+        own_ref[...] += own_part
+        slot_ref[...] += slot_part
+
+        @pl.when(step == pl.num_programs(0) - 1)
+        def _():
+            slot_out_ref[...] = slot_ref[...].astype(BF16)
 
 
 def tet_partials(old_coeff, bold, bnew, quad_weight, zone, table, vol, dest, slots_pad, block):
@@ -96,7 +103,8 @@
     basis = bold.shape[1]
     fields = width // basis
     kernel = functools.partial(
-        tet_kernel, tables=tables, basis=basis, fields=fields, zones=zones, slots_pad=slots_pad
+        tet_kernel, tables=tables, basis=basis, fields=fields, zones=zones, slots_pad=slots_pad,
+        single=tet_count == block,
     )
     row_spec = pl.BlockSpec((1, block), lambda i: (0, i))
     whole = lambda shape: pl.BlockSpec(shape, lambda i: (0, 0))

time: 47.4 us -> 47.4 us (level)
  no operation moved by 1% of the time
where the time goes in v13:
time: 47.4 us; the launch traced here: 47 us
  starting transfers between devices  21.7 us (46%)
  Pallas kernels  16.1 us (34%)
  waiting for transfers between devices  6.85 us (14%)
  local copies, waits for them, and re-layouts  2.3 us (5%)
    ppermute x6, starting transfers between devices, shifted(): return lax.ppermute(block, axis, route)  21.7 us
    pallas_call x1, Pallas kernels, tet_partials(): pl.pallas_call(kernel, grid=(tet_count // block,), in_specs=[row_spec, ro...  9.7 us
    ppermute x6, waiting for transfers between devices, shifted(): return lax.ppermute(block, axis, route)  6.85 us
    pallas_call x1, Pallas kernels, finish(): pl.pallas_call(kernel, out_shape=jax.ShapeDtypeStruct((zones, width), F32...  6.35 us
  transfers between devices with their start and end apart: 6, of which 3 were waited for; matrix products, arithmetic and copies ran while one was open for 2% of the time, Pallas kernels for 0%

profile of v13, /device:TPU:56, one launch (start us, length us, event | category | flops | bytes accessed | tf_op | source)
XLA Modules:
  0.0 47.0 jit_solution(16674688897347700699)
XLA Ops:
  0.0 9.7 %shard_map.100 = (f32[512,256]{1,0:T(8,128)}, bf16[256,512]{1,0:T(8,128)(2,1)}) custom-call(s32[1,2048]{1,0:T(1,128)} %bitcast.8, s32[1,2048]{1,0:T(1,128)} %bitcast.9, f32[1,2048]{1,0:T(1,128)} %bitcast.10, s32[1,2048]{1,0:T(1,128)} %bitcast.11, bf16[256,512]{1,0:T(8,128)(2,1)} %coeff_ref.1, bf16[512,64]{1,0:T(8,128)(2,1)} %bitcast.6, ...), custom_call_target="tpu_custom_call" | custom-call | tf_op jit(solution)/shard_map/pallas_call | solution.py:111
  9.7 0.8 %fusion = (bf16[16,512]{1,0:T(8,128)(2,1)S(1)}, bf16[16,512]{1,0:T(8,128)(2,1)S(1)}, bf16[16,512]{1,0:T(8,128)(2,1)S(1)}, bf16[16,512]{1,0:T(8,128)(2,1)S(1)}, b...) fusion(bf16[256,512]{1,0:T(8,128)(2,1)} %get-tuple-element.8), kind=kLoop, calls=%fused_computation.14 | loop fusion | bytes 262144 | tf_op jit(solution)/shard_map/slice | solution.py:255
  10.6 2.2 %collective-permute-start.5 = (bf16[16,512]{1,0:T(8,128)(2,1)S(1)}, bf16[16,512]{1,0:T(8,128)(2,1)S(1)}, u32[]{:S(2)}, u32[]{:S(2)}) collective-permute-start(bf16[16,512]{1,0:T(8,128)(2,1)S(1)} %get-tuple-element.9), channel_id=1, source_target_pairs={{0,448},{64,0},{128,64},{192,128},{256,192},{320,256},{384,320},{4... | collective-permute-start | bytes 49160 | tf_op jit(solution)/shard_map/ppermute | solution.py:217
  12.8 0.0 collective-permute-start.4
  12.8 4.3 %collective-permute-start = (bf16[48,512]{1,0:T(8,128)(2,1)S(1)}, bf16[48,512]{1,0:T(8,128)(2,1)S(1)}, u32[]{:S(2)}, u32[]{:S(2)}) collective-permute-start(bf16[48,512]{1,0:T(8,128)(2,1)S(1)} %pad_maximum_fusion), channel_id=1, source_target_pairs={{0,1},{1,2},{2,3},{3,4},{4,5},{5,6},{6,7},{7,8},{8,9},{9,10},{10,1... | collective-permute-start | bytes 147464 | tf_op jit(solution)/shard_map/ppermute | solution.py:217
  17.1 0.8 %slice.103 = bf16[32,512]{1,0:T(8,128)(2,1)S(1)} slice(bf16[256,512]{1,0:T(8,128)(2,1)} %get-tuple-element.8), slice={[80:112], [0:512]} | slice | bytes 65536 | tf_op jit(solution)/shard_map/slice | solution.py:251
  17.8 9.4 %collective-permute-start.1 = (bf16[48,512]{1,0:T(8,128)(2,1)S(1)}, bf16[48,512]{1,0:T(8,128)(2,1)S(1)}, u32[]{:S(2)}, u32[]{:S(2)}) collective-permute-start(bf16[48,512]{1,0:T(8,128)(2,1)S(1)} %pad_maximum_fusion.1), channel_id=1, source_target_pairs={{0,63},{1,0},{2,1},{3,2},{4,3},{5,4},{6,5},{7,6},{8,7},{9,8},{10,9... | collective-permute-start | bytes 147464 | tf_op jit(solution)/shard_map/ppermute | solution.py:217
  27.2 0.0 collective-permute-done
  27.2 1.7 %collective-permute-done.1 = bf16[48,512]{1,0:T(8,128)(2,1)S(1)} collective-permute-done((bf16[48,512]{1,0:T(8,128)(2,1)S(1)}, bf16[48,512]{1,0:T(8,128)(2,1)S(1)}, u32[]{:S(2)}, u32[]{:S(2)}) %collective-permute-start.1) | collective-permute-done | bytes 49184 | tf_op jit(solution)/shard_map/ppermute | solution.py:217
  28.9 3.8 %collective-permute-start.2 = (bf16[48,512]{1,0:T(8,128)(2,1)S(1)}, bf16[48,512]{1,0:T(8,128)(2,1)S(1)}, u32[]{:S(2)}, u32[]{:S(2)}) collective-permute-start(bf16[48,512]{1,0:T(8,128)(2,1)S(1)} %pad_maximum_fusion.2), channel_id=1, source_target_pairs={{0,8},{1,9},{2,10},{3,11},{4,12},{5,13},{6,14},{7,15},{8,16},{9,17... | collective-permute-start | bytes 147464 | tf_op jit(solution)/shard_map/ppermute | solution.py:217
  32.8 2.1 %collective-permute-start.3 = (bf16[48,512]{1,0:T(8,128)(2,1)S(1)}, bf16[48,512]{1,0:T(8,128)(2,1)S(1)}, u32[]{:S(2)}, u32[]{:S(2)}) collective-permute-start(bf16[48,512]{1,0:T(8,128)(2,1)S(1)} %pad_maximum_fusion.3), channel_id=1, source_target_pairs={{0,56},{1,57},{2,58},{3,59},{4,60},{5,61},{6,62},{7,63},{8,0},{9,1... | collective-permute-start | bytes 147464 | tf_op jit(solution)/shard_map/ppermute | solution.py:217
  34.8 0.1 collective-permute-done.2
  34.9 5.0 %collective-permute-done.3 = bf16[48,512]{1,0:T(8,128)(2,1)S(1)} collective-permute-done((bf16[48,512]{1,0:T(8,128)(2,1)S(1)}, bf16[48,512]{1,0:T(8,128)(2,1)S(1)}, u32[]{:S(2)}, u32[]{:S(2)}) %collective-permute-start.3) | collective-permute-done | bytes 49184 | tf_op jit(solution)/shard_map/ppermute | solution.py:217
  40.0 0.0 collective-permute-done.4
  40.0 0.0 collective-permute-done.5
  40.0 0.0 copy-start
  40.0 0.6 %copy-done = bf16[160,512]{1,0:T(8,128)(2,1)} copy-done((bf16[160,512]{1,0:T(8,128)(2,1)}, bf16[160,512]{1,0:T(8,128)(2,1)S(1)}, u32[]{:S(2)}) %copy-start) | copy-done | bytes 163864
  40.7 6.3 %shard_map.101 = f32[256,512]{1,0:T(8,128)} custom-call(f32[512,256]{1,0:T(8,128)} %get-tuple-element.7.own_ref, bf16[160,512]{1,0:T(8,128)(2,1)} %copy-done, s32[1,160]{1,0:T(1,128)} %list_ref.1, bf16[256,4096]{1,0:T(8,128)(2,1)} %inv_ref.1), custom_call_target="tpu_custom_call" | custom-call | tf_op jit(solution)/shard_map/pallas_call | solution.py:202
  (14 shorter events, 0.1 us)
Async XLA Ops:
  10.6 29.5 %collective-permute-start.5 = (bf16[16,512]{1,0:T(8,128)(2,1)S(1)}, bf16[16,512]{1,0:T(8,128)(2,1)S(1)}, u32[]{:S(2)}, u32[]{:S(2)}) collective-permute-start(bf16[16,512]{1,0:T(8,128)(2,1)S(1)} %get-tuple-element.9), channel_id=1, source_target_pairs={{0,448},{64,0},{128,64},{192,128},{256,192},{320,256},{384,320},{4... | collective-permute-start | bytes 49160 | tf_op jit(solution)/shard_map/ppermute | solution.py:217
  12.8 27.2 %collective-permute-start.4 = (bf16[16,512]{1,0:T(8,128)(2,1)S(1)}, bf16[16,512]{1,0:T(8,128)(2,1)S(1)}, u32[]{:S(2)}, u32[]{:S(2)}) collective-permute-start(bf16[16,512]{1,0:T(8,128)(2,1)S(1)} %get-tuple-element.10), channel_id=1, source_target_pairs={{0,64},{64,128},{128,192},{192,256},{256,320},{320,384},{384,448},... | collective-permute-start | bytes 49160 | tf_op jit(solution)/shard_map/ppermute | solution.py:217
  12.8 14.4 %collective-permute-start = (bf16[48,512]{1,0:T(8,128)(2,1)S(1)}, bf16[48,512]{1,0:T(8,128)(2,1)S(1)}, u32[]{:S(2)}, u32[]{:S(2)}) collective-permute-start(bf16[48,512]{1,0:T(8,128)(2,1)S(1)} %pad_maximum_fusion), channel_id=1, source_target_pairs={{0,1},{1,2},{2,3},{3,4},{4,5},{5,6},{6,7},{7,8},{8,9},{9,10},{10,1... | collective-permute-start | bytes 147464 | tf_op jit(solution)/shard_map/ppermute | solution.py:217
  17.8 11.1 %collective-permute-start.1 = (bf16[48,512]{1,0:T(8,128)(2,1)S(1)}, bf16[48,512]{1,0:T(8,128)(2,1)S(1)}, u32[]{:S(2)}, u32[]{:S(2)}) collective-permute-start(bf16[48,512]{1,0:T(8,128)(2,1)S(1)} %pad_maximum_fusion.1), channel_id=1, source_target_pairs={{0,63},{1,0},{2,1},{3,2},{4,3},{5,4},{6,5},{7,6},{8,7},{9,8},{10,9... | collective-permute-start | bytes 147464 | tf_op jit(solution)/shard_map/ppermute | solution.py:217
  28.9 6.0 %collective-permute-start.2 = (bf16[48,512]{1,0:T(8,128)(2,1)S(1)}, bf16[48,512]{1,0:T(8,128)(2,1)S(1)}, u32[]{:S(2)}, u32[]{:S(2)}) collective-permute-start(bf16[48,512]{1,0:T(8,128)(2,1)S(1)} %pad_maximum_fusion.2), channel_id=1, source_target_pairs={{0,8},{1,9},{2,10},{3,11},{4,12},{5,13},{6,14},{7,15},{8,16},{9,17... | collective-permute-start | bytes 147464 | tf_op jit(solution)/shard_map/ppermute | solution.py:217
  32.8 7.2 %collective-permute-start.3 = (bf16[48,512]{1,0:T(8,128)(2,1)S(1)}, bf16[48,512]{1,0:T(8,128)(2,1)S(1)}, u32[]{:S(2)}, u32[]{:S(2)}) collective-permute-start(bf16[48,512]{1,0:T(8,128)(2,1)S(1)} %pad_maximum_fusion.3), channel_id=1, source_target_pairs={{0,56},{1,57},{2,58},{3,59},{4,60},{5,61},{6,62},{7,63},{8,0},{9,1... | collective-permute-start | bytes 147464 | tf_op jit(solution)/shard_map/ppermute | solution.py:217
  40.0 0.7 %copy-start = (bf16[160,512]{1,0:T(8,128)(2,1)}, bf16[160,512]{1,0:T(8,128)(2,1)S(1)}, u32[]{:S(2)}) copy-start(bf16[160,512]{1,0:T(8,128)(2,1)S(1)} %constant_dynamic-update-slice_fusion.recv_ref) | copy-start | bytes 491524
